TPU v7x, 256 devices: a whole 4x4x8 slice. The times are simulated.
256 devices in a mesh: dp: 32 (over z, x), et: 8 (over y, core).
Axes of the slice: x: 4, y: 4, z: 8, core: 2. Of those that a mesh axis runs over, the one named last changes fastest.
Arguments:
- tokens: bfloat16 [4096, 2048], P('dp', 'et'), may hold values from -6 to 6
- cotangent: bfloat16 [4096, 2048], P('dp', 'et'), may hold values from -1.5 to 1.5
- expert_ids: int32 [4096, 8], P('dp'), may hold values from 0 to 63, all different within a row; in each aligned block of 128 rows (0 to 127, 128 to 255, ...) at most 24 rows name the same one
- route_gates: bfloat16 [4096, 8], P('dp'), may hold values from 0.049804688 to 0.3984375
- gate_proj: bfloat16 [64, 2048, 1024], P('dp', None, 'et'), may hold values from -0.125 to 0.125
- up_proj: bfloat16 [64, 2048, 1024], P('dp', None, 'et'), may hold values from -0.125 to 0.125
- down_proj: bfloat16 [64, 1024, 2048], P('dp', 'et'), may hold values from -0.1875 to 0.1875
Outputs:
- mixed: bfloat16 [4096, 2048], P('dp', 'et')
- grad_tokens: bfloat16 [4096, 2048], P('dp', 'et')
- grad_gates: float32 [4096, 8], P('dp')
- grad_gate_proj: float32 [64, 2048, 1024], P('dp', None, 'et')
- grad_up_proj: float32 [64, 2048, 1024], P('dp', None, 'et')
- grad_down_proj: float32 [64, 1024, 2048], P('dp', 'et')
Inputs may be any that keep to these rules, and one draw needn't show every extreme that they name: `expert_ids`: each row names 8 different experts. Among the rows of one device (128 aligned rows), no expert is named more than 24 times, a bound that some block reaches.
All inputs are finite; a program needn't handle non-finite values.
Results may differ from a plain program's by a relative error of at most 0.015.
Values may be sent and summed in bfloat16 or wider, within the bound.
No kernel may reach another device: no remote copies, remote signals or barrier semaphores. Data moves between devices by JAX's collectives and lax.ppermute only.
A program may use at most 128 MiB of HBM per device.

v0:
```python
import jax
import jax.numpy as jnp
from jax import lax
from jax.sharding import PartitionSpec as P


def places_in_block(chosen, experts):
    flattened = chosen.reshape(-1)
    onehot = (flattened[:, None] == jnp.arange(experts, dtype=jnp.int32)[None, :]).astype(jnp.int32)
    before = jnp.cumsum(onehot, axis=0) - onehot
    return jnp.sum(before * onehot, axis=1)


def pick_rows(lookup, inputs, cotangent, gate_values, per_token):
    holder = lookup // per_token
    inputs_ext = jnp.concatenate([inputs, jnp.zeros((1, inputs.shape[1]), jnp.bfloat16)], axis=0)
    cotangent_ext = jnp.concatenate(
        [cotangent, jnp.zeros((1, cotangent.shape[1]), jnp.bfloat16)], axis=0
    )
    gates_ext = jnp.concatenate([gate_values, jnp.zeros((1,), jnp.float32)], axis=0)
    picked = inputs_ext[holder]
    scaled = (gates_ext[lookup][:, None] * cotangent_ext[holder].astype(jnp.float32)).astype(
        jnp.bfloat16
    )
    return (picked, scaled)


def local(tokens, cotangent, expert_ids, route_gates, gate_proj, up_proj, down_proj):
    groups = lax.axis_size("dp")
    local_experts = gate_proj.shape[0]
    experts = local_experts * groups
    tok_rows, per_token = expert_ids.shape
    features = gate_proj.shape[1]
    capacity = 3 * tok_rows * per_token // (2 * experts)
    assignments = tok_rows * per_token
    places = places_in_block(expert_ids, experts)
    slot_index = expert_ids.reshape(-1) * capacity + places
    gates_flat = route_gates.reshape(-1).astype(jnp.float32)
    lookup = (
        jnp.full((experts * capacity,), assignments, jnp.int32)
        .at[slot_index]
        .set(jnp.arange(assignments, dtype=jnp.int32))
    )
    full_tokens, full_cot = (
        lax.all_gather(tokens, "et", axis=1, tiled=True),
        lax.all_gather(cotangent, "et", axis=1, tiled=True),
    )
    picked, scaled = pick_rows(lookup, full_tokens, full_cot, gates_flat, per_token)
    expert_in, expert_cot = (
        lax.all_to_all(
            picked.reshape(experts, capacity, features),
            "dp",
            split_axis=0,
            concat_axis=1,
            tiled=True,
        ),
        lax.all_to_all(
            scaled.reshape(experts, capacity, features),
            "dp",
            split_axis=0,
            concat_axis=1,
            tiled=True,
        ),
    )
    pre_gate = jnp.einsum("esd,edf->esf", expert_in, gate_proj, preferred_element_type=jnp.float32)
    pre_up = jnp.einsum("esd,edf->esf", expert_in, up_proj, preferred_element_type=jnp.float32)
    sigmoid_gate = jax.nn.sigmoid(pre_gate)
    silu_gate = pre_gate * sigmoid_gate
    hidden = (silu_gate * pre_up).astype(jnp.bfloat16)
    out_part = jnp.einsum("esf,efd->esd", hidden, down_proj, preferred_element_type=jnp.float32)
    grad_hidden = jnp.einsum(
        "esd,efd->esf", expert_cot, down_proj, preferred_element_type=jnp.float32
    )
    grad_pre_gate = (
        grad_hidden * pre_up * sigmoid_gate * (1.0 + pre_gate * (1.0 - sigmoid_gate))
    ).astype(jnp.bfloat16)
    grad_pre_up = (grad_hidden * silu_gate).astype(jnp.bfloat16)
    grad_down = jnp.einsum("esf,esd->efd", hidden, expert_cot, preferred_element_type=jnp.float32)
    grad_gate_w = jnp.einsum(
        "esd,esf->edf", expert_in, grad_pre_gate, preferred_element_type=jnp.float32
    )
    grad_up_w = jnp.einsum(
        "esd,esf->edf", expert_in, grad_pre_up, preferred_element_type=jnp.float32
    )
    in_part = jnp.einsum(
        "esf,edf->esd", grad_pre_gate, gate_proj, preferred_element_type=jnp.float32
    )
    in_part = in_part + jnp.einsum(
        "esf,edf->esd", grad_pre_up, up_proj, preferred_element_type=jnp.float32
    )
    out_sum, in_sum = (
        lax.psum_scatter(
            out_part.astype(jnp.bfloat16), "et", scatter_dimension=2, tiled=True
        ).astype(jnp.float32),
        lax.psum_scatter(
            in_part.astype(jnp.bfloat16), "et", scatter_dimension=2, tiled=True
        ).astype(jnp.float32),
    )
    back_out, back_grad = (
        lax.all_to_all(out_sum.astype(jnp.bfloat16), "dp", split_axis=1, concat_axis=0, tiled=True),
        lax.all_to_all(in_sum.astype(jnp.bfloat16), "dp", split_axis=1, concat_axis=0, tiled=True),
    )
    slice_width = tokens.shape[1]
    out_rows = (
        back_out.reshape(experts * capacity, slice_width)[slot_index]
        .reshape(tok_rows, per_token, slice_width)
        .astype(jnp.float32)
    )
    grad_rows = (
        back_grad.reshape(experts * capacity, slice_width)[slot_index]
        .reshape(tok_rows, per_token, slice_width)
        .astype(jnp.float32)
    )
    mixed = jnp.sum(route_gates.astype(jnp.float32)[:, :, None] * out_rows, axis=1).astype(
        jnp.bfloat16
    )
    gate_part = jnp.sum(cotangent.astype(jnp.float32)[:, None, :] * out_rows, axis=2)
    grad_gates = lax.psum(gate_part, "et")
    grad_tokens = jnp.sum(grad_rows, axis=1).astype(jnp.bfloat16)
    return (mixed, grad_tokens, grad_gates, grad_gate_w, grad_up_w, grad_down)


def solution(mesh):
    in_specs = (
        P("dp", "et"),
        P("dp", "et"),
        P("dp", None),
        P("dp", None),
        P("dp", None, "et"),
        P("dp", None, "et"),
        P("dp", "et", None),
    )
    out_specs = (
        P("dp", "et"),
        P("dp", "et"),
        P("dp", None),
        P("dp", None, "et"),
        P("dp", None, "et"),
        P("dp", "et", None),
    )
    return jax.shard_map(local, mesh=mesh, in_specs=in_specs, out_specs=out_specs, check_vma=False)
```

profile of v0, /device:TPU:2, one launch (start us, length us, event | category | flops | bytes accessed | tf_op | source)
XLA Modules:
  0.0 559.8 jit_solution(13934327767836784123)
XLA Ops:
  7.2 0.0 copy-start
  7.2 0.0 copy-start.8
  7.2 0.8 broadcast_multiply_fusion
  8.0 0.8 copy.35
  8.8 0.1 eq.29
  8.9 0.1 eq.25
  9.0 0.8 copy.42
  9.8 0.1 convert_element_type.70
  9.9 0.1 copy.34
  10.0 0.1 mul.74
  10.1 18.0 %reduce-window.6 = s32[64,8,128]{2,1,0:T(8,128)S(1)} reduce-window(s32[64,8,128]{2,1,0:T(8,128)S(1)} %fusion.7, s32[]{:T(128)} %constant.32.clone.1), window={size=1x1x128 pad=0_0x0_0x127_0}, to_apply=%region_0.0 | reduce-window | flops 8323072 | bytes 524292 | tf_op jit(solution)/shard_map/reduce-window
  28.1 0.1 slice.18
  28.2 0.1 copy.37
  28.4 0.1 copy.38
  28.5 0.1 broadcast_add_fusion
  28.7 0.1 fusion.6
  28.8 4.3 scatter_custom_fusion
  33.1 8.4 %gather_fusion.2 = f32[1536]{0:T(1024)S(1)} fusion(f32[1025]{0:T(1024)S(1)} %maximum_convert_fusion, s32[2048]{0:T(1024)S(1)} %pad_clamp_fusion), kind=kCustom, calls=%fused_computation.2 | custom fusion | bytes 18432 | tf_op jit(solution)/shard_map/gather | solution.py:22
  41.5 0.1 mul.79
  41.6 13.6 %all_gather.7 = bf16[128,2048]{1,0:T(8,128)(2,1)S(1)} all-gather(bf16[128,256]{1,0:T(8,128)(2,1)S(1)} %copy-done.8), channel_id=1, replica_groups=mesh['dp'=32,'et'=8] {'et'}, dimensions={1}, use_global_device_ids=true | all-gather | bytes 589824 | tf_op jit(solution)/shard_map/all_gather | solution.py:46
  55.3 7.1 %gather_fusion.3 = bf16[1536,2048]{1,0:T(8,128)(2,1)} fusion(bf16[129,2048]{1,0:T(8,128)(2,1)S(1)} %concatenate.15, s32[2048]{0:T(1024)S(1)} %pad_clamp_fusion.1), kind=kCustom, calls=%fused_computation.3 | custom fusion | bytes 12589056 | tf_op jit(solution)/shard_map/gather | solution.py:22
  62.4 6.5 %fusion = bf16[64,24,2048]{2,1,0:T(8,128)(2,1)} fusion(bf16[64,24,2048]{2,1,0:T(8,128)(2,1)} %bitcast.77, f32[64,24]{1,0:T(8,128)S(1)} %mul.79), kind=kLoop, calls=%fused_computation.7 | loop fusion | flops 9437184 | bytes 12589056 | tf_op jit(solution)/shard_map/convert_element_type | solution.py:22
  69.0 11.8 %all-to-all-start.2 = ((bf16[64,24,2048]{2,1,0:T(8,128)(2,1)}), bf16[64,24,2048]{2,1,0:T(8,128)(2,1)}, u32[]{:S(2)}, u32[]{:S(2)}) async-start(bf16[64,24,2048]{2,1,0:T(8,128)(2,1)} %fusion), calls=%async_computation.3 | async-start | bytes 12582912 | tf_op jit(solution)/shard_map/all_to_all | solution.py:57
  80.8 13.1 %all_gather.6 = bf16[128,2048]{1,0:T(8,128)(2,1)S(1)} all-gather(bf16[128,256]{1,0:T(8,128)(2,1)S(1)} %copy-done.11), channel_id=1, replica_groups=mesh['dp'=32,'et'=8] {'et'}, dimensions={1}, use_global_device_ids=true | all-gather | bytes 589824 | tf_op jit(solution)/shard_map/all_gather | solution.py:45
  93.9 7.1 %gather_fusion = bf16[1536,2048]{1,0:T(8,128)(2,1)} fusion(bf16[129,2048]{1,0:T(8,128)(2,1)S(1)} %concatenate.12, s32[2048]{0:T(1024)S(1)} %pad_clamp_fusion.1), kind=kCustom, calls=%fused_computation | custom fusion | bytes 12589056 | tf_op jit(solution)/shard_map/gather | solution.py:21
  101.0 124.2 %all-to-all-done.2 = bf16[64,24,2048]{2,1,0:T(8,128)(2,1)} async-done(((bf16[64,24,2048]{2,1,0:T(8,128)(2,1)}), bf16[64,24,2048]{2,1,0:T(8,128)(2,1)}, u32[]{:S(2)}, u32[]{:S(2)}) %all-to-all-start.2) | async-done | bytes 6291488 | tf_op jit(solution)/shard_map/all_to_all | solution.py:57
  225.3 10.9 %all-to-all-start = ((bf16[64,24,2048]{2,1,0:T(8,128)(2,1)}), bf16[64,24,2048]{2,1,0:T(8,128)(2,1)}, u32[]{:S(2)}, u32[]{:S(2)}) async-start(bf16[64,24,2048]{2,1,0:T(8,128)(2,1)} %bitcast.76), calls=%async_computation | async-start | bytes 12582912 | tf_op jit(solution)/shard_map/all_to_all | solution.py:50
  236.2 0.2 reduce-scatter.3.cloned.1.call-start
  236.4 6.6 %copy.43 = bf16[2,32,24,2048]{3,2,1,0:T(8,128)(2,1)} copy(bf16[2,32,24,2048]{3,2,0,1:T(8,128)(2,1)} %bitcast.14) | data formatting | bytes 12582912 | tf_op jit(solution)/shard_map/all_to_all | solution.py:57
  243.0 136.4 %all-to-all-done = bf16[64,24,2048]{2,1,0:T(8,128)(2,1)} async-done(((bf16[64,24,2048]{2,1,0:T(8,128)(2,1)}), bf16[64,24,2048]{2,1,0:T(8,128)(2,1)}, u32[]{:S(2)}, u32[]{:S(2)}) %all-to-all-start) | async-done | bytes 6291488 | tf_op jit(solution)/shard_map/all_to_all | solution.py:50
  379.4 3.5 copy.39
  382.9 0.0 copy-start.3
  382.9 1.8 fusion.13
  384.7 0.2 copy-done.3
  384.9 1.8 fusion.12
  386.7 1.0 slice-done.2
  387.6 0.7 slice-done.3
  388.3 3.0 multiply_convert_fusion
  391.3 4.4 convolution_convert_fusion
  395.6 0.0 reduce-scatter.3.cloned.1.call-update
  395.7 0.3 reduce-scatter.5.cloned.1.call-start
  395.9 0.0 copy-start.5
  395.9 2.8 fusion.14
  398.8 4.4 add_convert_fusion
  403.2 0.0 reduce-scatter.5.cloned.1.call-update
  403.2 37.6 %reduce-scatter.3.cloned.1.call-done = bf16[2,768,256]{2,1,0:T(8,128)(2,1)} async-done(((bf16[2,768,2048]{2,1,0:T(8,128)(2,1)}), bf16[2,768,256]{2,1,0:T(8,128)(2,1)}) %reduce-scatter.3.cloned.1.call-update) | async-done | bytes 786448 | tf_op jit(solution)/shard_map/reduce_scatter | solution.py:92
  440.8 2.8 copy.40
  443.6 10.2 %all-to-all-start.1 = ((bf16[2,768,256]{2,0,1:T(2,128)(2,1)}), bf16[2,768,256]{2,0,1:T(2,128)(2,1)}, u32[]{:S(2)}, u32[]{:S(2)}) async-start(bf16[2,768,256]{2,0,1:T(2,128)(2,1)} %copy.40), calls=%async_computation.2 | async-start | bytes 1572864 | tf_op jit(solution)/shard_map/all_to_all | solution.py:100
  453.8 0.7 copy.33
  454.6 0.7 convert_element_type.77
  455.2 33.4 %reduce-scatter.5.cloned.1.call-done = bf16[2,768,256]{2,1,0:T(8,128)(2,1)} async-done(((bf16[2,768,2048]{2,1,0:T(8,128)(2,1)}), bf16[2,768,256]{2,1,0:T(8,128)(2,1)}) %reduce-scatter.5.cloned.1.call-update) | async-done | bytes 786448 | tf_op jit(solution)/shard_map/reduce_scatter | solution.py:95
  488.7 2.8 copy.44
  491.5 10.4 %all-to-all-start.3 = ((bf16[2,768,256]{2,0,1:T(2,128)(2,1)}), bf16[2,768,256]{2,0,1:T(2,128)(2,1)}, u32[]{:S(2)}, u32[]{:S(2)}) async-start(bf16[2,768,256]{2,0,1:T(2,128)(2,1)} %copy.44), calls=%async_computation.5 | async-start | bytes 1572864 | tf_op jit(solution)/shard_map/all_to_all | solution.py:101
  501.9 5.3 fusion.17
  507.2 3.9 fusion.16
  511.1 3.9 fusion.15
  515.0 1.2 copy.41
  516.2 3.9 gather_fusion.1
  520.2 1.1 fusion.2
  521.3 24.8 %psum.7 = f32[128,8]{1,0:T(8,128)S(1)} all-reduce(f32[128,8]{1,0:T(8,128)S(1)} %get-tuple-element.12), channel_id=1, replica_groups=mesh['dp'=32,'et'=8] {'et'}, use_global_device_ids=true, to_apply=%region_9.10 | all-reduce | flops 1024 | bytes 8192 | tf_op jit(solution)/shard_map/psum | solution.py:118
  546.2 0.7 copy.49
  546.8 1.2 copy.45
  548.1 3.9 gather_fusion.4
  552.0 1.0 bitcast_reduce_fusion
  (43 shorter events, 0.2 us)
Async XLA Ops:
  7.2 379.5 %copy-start = (bf16[2,128,2048]{2,1,0:T(8,128)(2,1)S(1)}, bf16[2,128,2048]{2,1,0:T(8,128)(2,1)}, u32[]{:S(2)}) copy-start(bf16[2,128,2048]{2,1,0:T(8,128)(2,1)} %param.13) | copy-start | bytes 3145732
  7.2 34.4 %copy-start.8 = (bf16[128,256]{1,0:T(8,128)(2,1)S(1)}, bf16[128,256]{1,0:T(8,128)(2,1)}, u32[]{:S(2)}) copy-start(bf16[128,256]{1,0:T(8,128)(2,1)} %param.8) | copy-start | bytes 196612
  69.0 11.8 %copy-start.11 = (bf16[128,256]{1,0:T(8,128)(2,1)S(1)}, bf16[128,256]{1,0:T(8,128)(2,1)}, u32[]{:S(2)}) copy-start(bf16[128,256]{1,0:T(8,128)(2,1)} %param.7) | copy-start | bytes 196612
  69.0 156.3 %all-to-all-start.2 = ((bf16[64,24,2048]{2,1,0:T(8,128)(2,1)}), bf16[64,24,2048]{2,1,0:T(8,128)(2,1)}, u32[]{:S(2)}, u32[]{:S(2)}) async-start(bf16[64,24,2048]{2,1,0:T(8,128)(2,1)} %fusion), calls=%async_computation.3 | async-start | bytes 12582912 | tf_op jit(solution)/shard_map/all_to_all | solution.py:57
  225.3 154.1 %all-to-all-start = ((bf16[64,24,2048]{2,1,0:T(8,128)(2,1)}), bf16[64,24,2048]{2,1,0:T(8,128)(2,1)}, u32[]{:S(2)}, u32[]{:S(2)}) async-start(bf16[64,24,2048]{2,1,0:T(8,128)(2,1)} %bitcast.76), calls=%async_computation | async-start | bytes 12582912 | tf_op jit(solution)/shard_map/all_to_all | solution.py:50
  236.2 204.6 %reduce-scatter.3.cloned.1.call-start = ((), (), s32[]{:S(2)}) async-start(), calls=%async_computation.6 | async-start | bytes 7077888 | tf_op jit(solution)/shard_map/reduce_scatter | solution.py:92
  379.4 3.5 copy-start.2
  382.8 3.8 copy-start.1
  382.9 2.0 copy-start.3
  382.9 4.8 slice-start.2
  384.9 3.4 slice-start.3
  395.7 93.0 %reduce-scatter.5.cloned.1.call-start = ((), (), s32[]{:S(2)}) async-start(), calls=%async_computation.7 | async-start | bytes 7077888 | tf_op jit(solution)/shard_map/reduce_scatter | solution.py:95
  395.9 2.9 copy-start.5
  403.2 50.6 %copy-start.12 = (bf16[128,8]{0,1:T(8,128)(2,1)S(1)}, bf16[128,8]{0,1:T(8,128)(2,1)}, u32[]{:S(2)}) copy-start(bf16[128,8]{0,1:T(8,128)(2,1)} %param.10) | copy-start | bytes 6148
  403.2 51.4 %copy-start.9 = (bf16[128,256]{1,0:T(8,128)(2,1)S(1)}, bf16[128,256]{1,0:T(8,128)(2,1)}, u32[]{:S(2)}) copy-start(bf16[128,256]{1,0:T(8,128)(2,1)} %param.8) | copy-start | bytes 196612
  443.6 47.9 %all-to-all-start.1 = ((bf16[2,768,256]{2,0,1:T(2,128)(2,1)}), bf16[2,768,256]{2,0,1:T(2,128)(2,1)}, u32[]{:S(2)}, u32[]{:S(2)}) async-start(bf16[2,768,256]{2,0,1:T(2,128)(2,1)} %copy.40), calls=%async_computation.2 | async-start | bytes 1572864 | tf_op jit(solution)/shard_map/all_to_all | solution.py:100
  491.5 15.7 %slice-start = ((s8[6291456]{0:T(1024)(128)(4,1)}), s8[2097152]{0:T(1024)(128)(4,1)S(1)}, s32[]{:S(2)}) async-start(s8[6291456]{0:T(1024)(128)(4,1)} %bitcast.66), calls=%async_computation.8 | async-start | bytes 4194304
  491.5 55.3 %all-to-all-start.3 = ((bf16[2,768,256]{2,0,1:T(2,128)(2,1)}), bf16[2,768,256]{2,0,1:T(2,128)(2,1)}, u32[]{:S(2)}, u32[]{:S(2)}) async-start(bf16[2,768,256]{2,0,1:T(2,128)(2,1)} %copy.44), calls=%async_computation.5 | async-start | bytes 1572864 | tf_op jit(solution)/shard_map/all_to_all | solution.py:101
  501.9 5.3 slice-start.1
  501.9 5.3 copy-start.6
  507.2 3.9 copy-start.4
  511.1 9.1 %copy-start.7 = (f32[128,256]{1,0:T(8,128)S(1)}, f32[128,256]{1,0:T(8,128)}, u32[]{:S(2)}) copy-start(f32[128,256]{1,0:T(8,128)} %convert_element_type.77) | copy-start | bytes 393220
  511.1 9.1 %copy-start.10 = (f32[128,8]{1,0:T(8,128)S(1)}, f32[128,8]{1,0:T(8,128)}, u32[]{:S(2)}) copy-start(f32[128,8]{1,0:T(8,128)} %copy.33) | copy-start | bytes 12292
Sparse Core Ops, SparseCore 0:
  395.8 44.9 reduce-scatter.2
  443.4 45.2 reduce-scatter.4
where the time goes:
time: 561 us; the launch traced here: 560 us
  waiting for transfers between devices  332 us (59%)
  local copies, waits for them, and re-layouts  58.8 us (10%)
  blocking collectives  51.6 us (9%)
  starting transfers between devices  43.7 us (8%)
  matrix products  31.2 us (6%)
  other arithmetic  28.4 us (5%)
  between operations  14.4 us (3%)
    all_to_all x1, waiting for transfers between devices, local(): lax.all_to_all(picked.reshape(experts, capacity, features), 'dp', split_a...  136 us
    all_to_all x1, waiting for transfers between devices, local(): lax.all_to_all(scaled.reshape(experts, capacity, features), 'dp', split_a...  124 us
    reduce_scatter x1, waiting for transfers between devices, local(): lax.psum_scatter(out_part.astype(jnp.bfloat16), 'et', scatter_dimension=2...  37.6 us
    reduce_scatter x1, waiting for transfers between devices, local(): lax.psum_scatter(in_part.astype(jnp.bfloat16), 'et', scatter_dimension=2,...  33.4 us
    psum x1, blocking collectives, local(): grad_gates = lax.psum(gate_part, 'et')  24.8 us
    another operation x3, other arithmetic  18.2 us
    all_gather x1, blocking collectives, local(): lax.all_gather(cotangent, 'et', axis=1, tiled=True)  13.6 us
    all_gather x1, blocking collectives, local(): lax.all_gather(tokens, 'et', axis=1, tiled=True)  13.1 us
  transfers between devices with their start and end apart: 6, of which 4 were waited for; matrix products, arithmetic and copies ran while one was open for 9% of the time, Pallas kernels for 0%

commit v1 on v0

v1 whole, which is shorter than its diff:
```python
import jax
import jax.numpy as jnp
from jax import lax
from jax.sharding import PartitionSpec as P


def places_in_block(chosen, experts):
    flattened = chosen.reshape(-1)
    pairs = flattened.shape[0]
    onehot = (flattened[:, None] == jnp.arange(experts, dtype=jnp.int32)[None, :]).astype(jnp.bfloat16)
    rows = lax.broadcasted_iota(jnp.int32, (pairs, pairs), 0)
    cols = lax.broadcasted_iota(jnp.int32, (pairs, pairs), 1)
    earlier = (cols < rows).astype(jnp.bfloat16)
    before = jnp.dot(earlier, onehot, preferred_element_type=jnp.float32)
    return jnp.sum(before * onehot.astype(jnp.float32), axis=1).astype(jnp.int32)


def local(tokens, cotangent, expert_ids, route_gates, gate_proj, up_proj, down_proj):
    groups = lax.axis_size("dp")
    shards = lax.axis_size("et")
    local_experts, features, units = gate_proj.shape
    experts = local_experts * groups
    tok_rows, per_token = expert_ids.shape
    width = tokens.shape[1]
    capacity = 3 * tok_rows * per_token // (2 * experts)
    slots = experts * capacity
    places = places_in_block(expert_ids, experts)
    slot_index = (expert_ids.reshape(-1) * capacity + places).reshape(tok_rows, per_token)
    match = slot_index[None, :, :] == jnp.arange(slots, dtype=jnp.int32)[:, None, None]
    select = jnp.any(match, axis=2).astype(jnp.bfloat16)
    gate_select = jnp.sum(
        jnp.where(match, route_gates[None, :, :].astype(jnp.float32), 0.0), axis=2
    ).astype(jnp.bfloat16)
    picked = jnp.dot(select, tokens, preferred_element_type=jnp.float32).astype(jnp.bfloat16)
    scaled = jnp.dot(gate_select, cotangent, preferred_element_type=jnp.float32).astype(
        jnp.bfloat16
    )
    expert_in_part, expert_cot_part = (
        lax.all_to_all(
            picked.reshape(experts, capacity, width), "dp", split_axis=0, concat_axis=1, tiled=True
        ),
        lax.all_to_all(
            scaled.reshape(experts, capacity, width), "dp", split_axis=0, concat_axis=1, tiled=True
        ),
    )
    expert_in = lax.all_gather(expert_in_part, "et", axis=0)
    expert_cot = lax.all_gather(expert_cot_part, "et", axis=0)
    gate_w = gate_proj.reshape(local_experts, shards, width, units)
    up_w = up_proj.reshape(local_experts, shards, width, units)
    down_w = down_proj.reshape(local_experts, units, shards, width)
    pre_gate = jnp.einsum("jesd,ejdf->esf", expert_in, gate_w, preferred_element_type=jnp.float32)
    pre_up = jnp.einsum("jesd,ejdf->esf", expert_in, up_w, preferred_element_type=jnp.float32)
    sigmoid_gate = jax.nn.sigmoid(pre_gate)
    silu_gate = pre_gate * sigmoid_gate
    hidden = (silu_gate * pre_up).astype(jnp.bfloat16)
    out_part = jnp.einsum("esf,efd->esd", hidden, down_proj, preferred_element_type=jnp.float32)
    grad_hidden = jnp.einsum(
        "jesd,efjd->esf", expert_cot, down_w, preferred_element_type=jnp.float32
    )
    grad_pre_gate = (
        grad_hidden * pre_up * sigmoid_gate * (1.0 + pre_gate * (1.0 - sigmoid_gate))
    ).astype(jnp.bfloat16)
    grad_pre_up = (grad_hidden * silu_gate).astype(jnp.bfloat16)
    grad_down = jnp.einsum(
        "esf,jesd->efjd", hidden, expert_cot, preferred_element_type=jnp.float32
    ).reshape(local_experts, units, features)
    grad_gate_w = jnp.einsum(
        "jesd,esf->ejdf", expert_in, grad_pre_gate, preferred_element_type=jnp.float32
    ).reshape(local_experts, features, units)
    grad_up_w = jnp.einsum(
        "jesd,esf->ejdf", expert_in, grad_pre_up, preferred_element_type=jnp.float32
    ).reshape(local_experts, features, units)
    in_part = jnp.einsum(
        "esf,edf->esd", grad_pre_gate, gate_proj, preferred_element_type=jnp.float32
    )
    in_part = in_part + jnp.einsum(
        "esf,edf->esd", grad_pre_up, up_proj, preferred_element_type=jnp.float32
    )
    out_sum, in_sum = (
        lax.psum_scatter(out_part.astype(jnp.bfloat16), "et", scatter_dimension=2, tiled=True),
        lax.psum_scatter(in_part.astype(jnp.bfloat16), "et", scatter_dimension=2, tiled=True),
    )
    back_out, back_grad = (
        lax.all_to_all(out_sum, "dp", split_axis=1, concat_axis=0, tiled=True),
        lax.all_to_all(in_sum, "dp", split_axis=1, concat_axis=0, tiled=True),
    )
    back_out = back_out.reshape(slots, width)
    back_grad = back_grad.reshape(slots, width)
    mixed = jnp.einsum(
        "st,sd->td", gate_select, back_out, preferred_element_type=jnp.float32
    ).astype(jnp.bfloat16)
    grad_tokens = jnp.einsum(
        "st,sd->td", select, back_grad, preferred_element_type=jnp.float32
    ).astype(jnp.bfloat16)
    out_rows = back_out[slot_index.reshape(-1)].reshape(tok_rows, per_token, width).astype(
        jnp.float32
    )
    gate_part = jnp.sum(cotangent.astype(jnp.float32)[:, None, :] * out_rows, axis=2)
    grad_gates = lax.psum(gate_part, "et")
    return (mixed, grad_tokens, grad_gates, grad_gate_w, grad_up_w, grad_down)


def solution(mesh):
    in_specs = (
        P("dp", "et"),
        P("dp", "et"),
        P("dp", None),
        P("dp", None),
        P("dp", None, "et"),
        P("dp", None, "et"),
        P("dp", "et", None),
    )
    out_specs = (
        P("dp", "et"),
        P("dp", "et"),
        P("dp", None),
        P("dp", None, "et"),
        P("dp", None, "et"),
        P("dp", "et", None),
    )
    return jax.shard_map(local, mesh=mesh, in_specs=in_specs, out_specs=out_specs, check_vma=False)
```

time: 561 us -> 314 us (0.56)
  waiting for transfers between devices: 332 us -> 114 us
  local copies, waits for them, and re-layouts: 58.8 us -> 18.6 us
  blocking collectives: 51.6 us -> 85.2 us
  starting transfers between devices: 43.7 us -> 20.5 us
  matrix products: 31.2 us -> 46 us
  other arithmetic: 28.4 us -> 14.6 us
    all_to_all x4 -> x2, waiting for transfers between devices: 261 us -> 0.01 us  [the longest x1 0.01 us: local(): lax.all_to_all(in_sum, 'dp', split_axis=1, concat_axis=0, tiled=True)]
    all_to_all x0 -> x2, blocking collectives: none -> 60.5 us  [the longest x1 33.9 us: local(): lax.all_to_all(picked.reshape(experts, capacity, width), 'dp', split_axis...]
    all_gather x0 -> x2, waiting for transfers between devices: none -> 41.7 us  [the longest x1 37.7 us: local(): expert_cot = lax.all_gather(expert_cot_part, 'et', axis=0)]
    all_gather x2 -> x0, blocking collectives: 26.7 us -> none  [the longest x1 13.6 us: local(): lax.all_gather(cotangent, 'et', axis=1, tiled=True)]
    gather x5 -> x1, local copies, waits for them, and re-layouts: 30.5 us -> 3.94 us  [local(): back_out[slot_index.reshape(-1)].reshape(tok_rows, per_token, width)]
    all_to_all x4 -> x2, starting transfers between devices: 43.2 us -> 20.2 us  [the longest x1 10.1 us: local(): lax.all_to_all(out_sum, 'dp', split_axis=1, concat_axis=0, tiled=True)]
    another operation x3 -> x0, other arithmetic: 18.2 us -> none
    dot_general x6 -> x11, matrix products: 19.6 us -> 35.4 us  [the longest x1 6.83 us: local(): jnp.einsum('jesd,esf->ejdf', expert_in, grad_pre_up, preferred_element_ty...]
  transfers between devices with their start and end apart: 6 -> 6, of which waited for: 4 -> 4; matrix products, arithmetic and copies ran while one was open for 9% -> 18% of each run, Pallas kernels for 0% -> 0%
where the time goes in v1:
time: 314 us
  waiting for transfers between devices  114 us (36%)
  blocking collectives  85.2 us (27%)
  matrix products  46 us (15%)
  starting transfers between devices  20.5 us (7%)
  local copies, waits for them, and re-layouts  18.6 us (6%)
  other arithmetic  14.6 us (5%)
  between operations  14.1 us (4%)
    reduce_scatter x1, waiting for transfers between devices, local(): lax.psum_scatter(out_part.astype(jnp.bfloat16), 'et', scatter_dimension=2...  39 us
    all_gather x1, waiting for transfers between devices, local(): expert_cot = lax.all_gather(expert_cot_part, 'et', axis=0)  37.7 us
    all_to_all x1, blocking collectives, local(): lax.all_to_all(picked.reshape(experts, capacity, width), 'dp', split_axis...  33.9 us
    reduce_scatter x1, waiting for transfers between devices, local(): lax.psum_scatter(in_part.astype(jnp.bfloat16), 'et', scatter_dimension=2,...  33.7 us
    all_to_all x1, blocking collectives, local(): lax.all_to_all(scaled.reshape(experts, capacity, width), 'dp', split_axis...  26.7 us
    psum x1, blocking collectives, local(): grad_gates = lax.psum(gate_part, 'et')  24.7 us
    all_to_all x1, starting transfers between devices, local(): lax.all_to_all(out_sum, 'dp', split_axis=1, concat_axis=0, tiled=True)  10.1 us
    all_to_all x1, starting transfers between devices, local(): lax.all_to_all(in_sum, 'dp', split_axis=1, concat_axis=0, tiled=True)  10.1 us
  transfers between devices with their start and end apart: 6, of which 4 were waited for; matrix products, arithmetic and copies ran while one was open for 18% of the time, Pallas kernels for 0%

profile of v1, /device:TPU:2, one launch (start us, length us, event | category | flops | bytes accessed | tf_op | source)
XLA Modules:
  0.0 313.6 jit_solution(2388499186354638069)
XLA Ops:
  7.2 0.0 copy-start
  7.2 0.0 copy-start.15
  7.2 0.0 copy-start.14
  7.2 0.0 all-gather.3.cloned.1.call-start
  7.2 0.9 copy.67
  8.1 0.1 eq.28
  8.2 0.0 copy-start.2
  8.2 0.6 fusion.3
  8.8 0.1 convert_element_type.76
  9.0 5.6 %fusion = pred[1536,128]{1,0:T(8,128)(4,1)S(1)} fusion(s32[128,8]{0,1:T(8,128)S(1)} %copy.69), kind=kLoop, calls=%fused_computation.4 | loop fusion | flops 2949120 | bytes 200704 | tf_op jit(solution)/shard_map/reduce_or | solution.py:30
  14.6 0.0 copy-start.11
  14.6 1.3 convolution_convert_fusion.2
  15.9 33.9 %all_to_all.60 = bf16[64,24,256]{2,1,0:T(8,128)(2,1)S(1)} all-to-all(bf16[64,24,256]{2,1,0:T(8,128)(2,1)S(1)} %bitcast.93), channel_id=1, replica_groups=mesh['dp'=32,'et'=8] {'dp'}, dimensions={0} | all-to-all | bytes 1572864 | tf_op jit(solution)/shard_map/all_to_all | solution.py:39
  49.7 0.9 copy.70
  50.7 0.0 copy-done.11
  50.7 0.0 all-gather.3.cloned.1.call-update
  50.7 0.0 all-gather.5.cloned.1.call-start
  50.7 0.0 copy-done.15
  50.8 8.1 %select_reduce_fusion = bf16[1536,128]{1,0:T(8,128)(2,1)S(1)} fusion(f32[128,8]{0,1:T(8,128)S(1)} %convert_element_type.77, s32[128,8]{0,1:T(8,128)S(1)} %copy.69), kind=kLoop, calls=%fused_computation.2 | loop fusion | flops 4521984 | bytes 401408 | tf_op jit(solution)/shard_map/reduce_sum | solution.py:31
  58.9 0.3 convolution_convert_fusion.1
  59.3 26.7 %all_to_all.61 = bf16[64,24,256]{2,1,0:T(8,128)(2,1)S(1)} all-to-all(bf16[64,24,256]{2,1,0:T(8,128)(2,1)S(1)} %bitcast.94), channel_id=1, replica_groups=mesh['dp'=32,'et'=8] {'dp'}, dimensions={0} | all-to-all | bytes 1572864 | tf_op jit(solution)/shard_map/all_to_all | solution.py:42
  85.9 0.9 copy.73
  86.9 0.0 all-gather.5.cloned.1.call-update
  86.9 0.2 reduce-scatter.3.cloned.1.call-start
  87.1 4.0 %all-gather.3.cloned.1.call-done = bf16[8,2,768,256]{3,2,0,1:T(8,128)(2,1)} async-done(((bf16[1,2,768,256]{3,2,0,1:T(8,128)(2,1)}), bf16[8,2,768,256]{3,2,0,1:T(8,128)(2,1)}) %all-gather.3.cloned.1.call-update) | async-done | bytes 6291472 | tf_op jit(solution)/shard_map/all_gather | solution.py:46
  91.2 0.0 copy-done.2
  91.2 5.6 %convolution_bitcast_fusion.1 = f32[2,768,128]{2,1,0:T(8,128)} fusion(bf16[8,2,768,256]{3,2,0,1:T(8,128)(2,1)} %all-gather.3.cloned.1.call-done, bf16[2,8,256,128]{3,2,1,0:T(8,128)(2,1)S(1)} %bitcast.86), kind=kOutput, calls=%fused_computation.11 | convolution fusion | flops 805306368 | bytes 8126464 | tf_op jit(solution)/shard_map/jesd,ejdf->esf/dot_general | solution.py:52
  96.8 2.7 convolution_bitcast_fusion.2
  99.4 37.7 %all-gather.5.cloned.1.call-done = bf16[8,2,768,256]{3,2,0,1:T(8,128)(2,1)} async-done(((bf16[1,2,768,256]{3,2,0,1:T(8,128)(2,1)}), bf16[8,2,768,256]{3,2,0,1:T(8,128)(2,1)}) %all-gather.5.cloned.1.call-update) | async-done | bytes 6291472 | tf_op jit(solution)/shard_map/all_gather | solution.py:47
  137.1 5.5 %multiply_convert_fusion = (bf16[2,768,128]{2,1,0:T(8,128)(2,1)S(1)}, bf16[2,768,128]{2,1,0:T(8,128)(2,1)S(1)}, bf16[2,768,128]{2,1,0:T(8,128)(2,1)S(1)}) fusion(f32[2,768,128]{2,1,0:T(8,128)} %convolution_bitcast_fusion.2, f32[2,768,128]{2,1,0:T(8,128)} %convolution_bitcast_fusion.1, bf16[8,2,768,256]{3,2,0,1:T(8,128)(2,1)} %all-gather.5.cloned.1.call-done, ...), kind=kOutput, calls=%fused_computation.21 | convolution fusion | flops 808255488 | bytes 10092544 | tf_op jit(solution)/shard_map/jesd,efjd->esf/dot_general | solution.py:57
  142.7 0.0 copy-start.8
  142.7 0.0 copy-start.5
  142.7 0.7 copy-done.8
  143.4 4.4 %convolution_convert_fusion = bf16[2,768,2048]{2,1,0:T(8,128)(2,1)} fusion(bf16[2,768,128]{2,1,0:T(8,128)(2,1)S(1)} %get-tuple-element.32, bf16[2,128,2048]{2,1,0:T(8,128)(2,1)S(1)} %copy-done.10), kind=kOutput, calls=%fused_computation.5 | convolution fusion | flops 808452096 | bytes 7733248 | tf_op jit(solution)/shard_map/esf,efd->esd/dot_general | solution.py:56
  147.8 0.0 reduce-scatter.3.cloned.1.call-update
  147.8 0.0 reduce-scatter.5.cloned.1.call-start
  147.9 1.8 fusion.19
  149.7 4.4 %add_convert_fusion = bf16[2,768,2048]{2,1,0:T(8,128)(2,1)} fusion(f32[2,768,2048]{2,1,0:T(8,128)S(1)} %fusion.19, bf16[2,768,128]{2,1,0:T(8,128)(2,1)S(1)} %get-tuple-element.30, bf16[2,2048,128]{2,1,0:T(8,128)(2,1)S(1)} %copy-done.2), kind=kOutput, calls=%fused_computation.1 | convolution fusion | flops 811597824 | bytes 20316160 | tf_op jit(solution)/shard_map/esf,edf->esd/dot_general | solution.py:76
  154.1 0.0 reduce-scatter.5.cloned.1.call-update
  154.2 39.0 %reduce-scatter.3.cloned.1.call-done = bf16[2,768,256]{2,1,0:T(8,128)(2,1)} async-done(((bf16[2,768,2048]{2,1,0:T(8,128)(2,1)}), bf16[2,768,256]{2,1,0:T(8,128)(2,1)}) %reduce-scatter.3.cloned.1.call-update) | async-done | bytes 786448 | tf_op jit(solution)/shard_map/reduce_scatter | solution.py:80
  193.1 2.8 copy.71
  195.9 10.1 %all-to-all-start.1 = ((bf16[2,768,256]{2,0,1:T(2,128)(2,1)}), bf16[2,768,256]{2,0,1:T(2,128)(2,1)S(1)}, u32[]{:S(2)}, u32[]{:S(2)}) async-start(bf16[2,768,256]{2,0,1:T(2,128)(2,1)} %copy.71), calls=%async_computation.2 | async-start | bytes 1572864 | tf_op jit(solution)/shard_map/all_to_all | solution.py:84
  206.1 0.7 convert_element_type.88
  206.7 0.1 mul.65
  206.9 33.7 %reduce-scatter.5.cloned.1.call-done = bf16[2,768,256]{2,1,0:T(8,128)(2,1)} async-done(((bf16[2,768,2048]{2,1,0:T(8,128)(2,1)}), bf16[2,768,256]{2,1,0:T(8,128)(2,1)}) %reduce-scatter.5.cloned.1.call-update) | async-done | bytes 786448 | tf_op jit(solution)/shard_map/reduce_scatter | solution.py:81
  240.6 2.9 copy.75
  243.5 0.0 all-to-all-done.1
  243.5 10.1 %all-to-all-start.3 = ((bf16[2,768,256]{2,0,1:T(2,128)(2,1)}), bf16[2,768,256]{2,0,1:T(2,128)(2,1)}, u32[]{:S(2)}, u32[]{:S(2)}) async-start(bf16[2,768,256]{2,0,1:T(2,128)(2,1)} %copy.75), calls=%async_computation.5 | async-start | bytes 1572864 | tf_op jit(solution)/shard_map/all_to_all | solution.py:85
  253.6 6.7 %fusion.8 = f32[2,128,8,256]{1,3,2,0:T(8,128)} fusion(bf16[8,2,768,256]{3,2,0,1:T(8,128)(2,1)} %all-gather.5.cloned.1.call-done, bf16[2,768,128]{2,1,0:T(8,128)(2,1)S(1)} %copy-done.9), kind=kOutput, calls=%fused_computation.26 | convolution fusion | flops 805306368 | bytes 8781824 | tf_op jit(solution)/shard_map/esf,jesd->efjd/dot_general | solution.py:64
  260.2 3.0 copy.83
  263.3 6.8 %fusion.10 = f32[2,8,256,128]{3,2,1,0:T(8,128)} fusion(bf16[8,2,768,256]{3,2,0,1:T(8,128)(2,1)} %all-gather.3.cloned.1.call-done, bf16[2,768,128]{2,1,0:T(8,128)(2,1)} %copy-done.7), kind=kOutput, calls=%fused_computation.28 | convolution fusion | flops 805306368 | bytes 8781824 | tf_op jit(solution)/shard_map/jesd,esf->ejdf/dot_general | solution.py:70
  270.1 0.0 slice-done.1
  270.1 3.9 %fusion.12 = f32[2,8,256,128]{3,2,1,0:T(8,128)} fusion(bf16[8,2,768,256]{3,2,0,1:T(8,128)(2,1)S(1)} %bitcast.82, bf16[2,768,128]{2,1,0:T(8,128)(2,1)S(1)} %copy-done.6), kind=kOutput, calls=%fused_computation.30 | convolution fusion | flops 805306368 | bytes 8781824 | tf_op jit(solution)/shard_map/jesd,esf->ejdf/dot_general | solution.py:67
  274.0 0.1 copy.72
  274.2 3.9 %gather_fusion = bf16[1024,256]{1,0:T(8,128)(2,1)S(1)} fusion(bf16[1536,256]{1,0:T(8,128)(2,1)S(1)} %bitcast.83, s32[1024]{0:T(1024)S(1)} %broadcast_clamp_fusion), kind=kCustom, calls=%fused_computation | custom fusion | bytes 1052672 | tf_op jit(solution)/shard_map/gather | solution.py:95
  278.1 0.0 copy-done.13
  278.1 0.2 fusion.6
  278.3 24.7 %psum.7 = f32[128,8]{1,0:T(8,128)S(1)} all-reduce(f32[128,8]{1,0:T(8,128)S(1)} %fusion.6), channel_id=1, replica_groups=mesh['dp'=32,'et'=8] {'et'}, use_global_device_ids=true, to_apply=%region_6.7 | all-reduce | flops 1024 | bytes 8192 | tf_op jit(solution)/shard_map/psum | solution.py:99
  303.1 0.7 copy.82
  303.7 1.0 convolution_convert_fusion.3
  304.7 0.0 all-to-all-done.3
  304.7 1.2 copy.76
  305.9 0.1 copy.77
  306.0 1.1 convolution_convert_fusion.4
  (30 shorter events, 0.1 us)
Async XLA Ops:
  7.2 89.6 %copy-start = (bf16[2,2048,128]{2,1,0:T(8,128)(2,1)S(1)}, bf16[2,2048,128]{2,1,0:T(8,128)(2,1)}, u32[]{:S(2)}) copy-start(bf16[2,2048,128]{2,1,0:T(8,128)(2,1)} %param.11) | copy-start | bytes 3145732
  7.2 43.6 %copy-start.15 = (bf16[128,8]{0,1:T(8,128)(2,1)S(1)}, bf16[128,8]{0,1:T(8,128)(2,1)}, u32[]{:S(2)}) copy-start(bf16[128,8]{0,1:T(8,128)(2,1)} %param.10) | copy-start | bytes 6148
  7.2 51.7 %copy-start.14 = (bf16[128,256]{1,0:T(8,128)(2,1)S(1)}, bf16[128,256]{1,0:T(8,128)(2,1)}, u32[]{:S(2)}) copy-start(bf16[128,256]{1,0:T(8,128)(2,1)} %param.8) | copy-start | bytes 196612
  7.2 84.0 %all-gather.3.cloned.1.call-start = ((), (), s32[]{:S(2)}) async-start(), calls=%async_computation.6 | async-start | bytes 7077888 | tf_op jit(solution)/shard_map/all_gather | solution.py:46
  8.2 83.0 %copy-start.2 = (bf16[2,2048,128]{2,1,0:T(8,128)(2,1)S(1)}, bf16[2,2048,128]{2,1,0:T(8,128)(2,1)}, u32[]{:S(2)}) copy-start(bf16[2,2048,128]{2,1,0:T(8,128)(2,1)} %param.12) | copy-start | bytes 3145732
  14.6 36.1 %copy-start.11 = (pred[1536,128]{1,0:T(8,128)(4,1)}, pred[1536,128]{1,0:T(8,128)(4,1)S(1)}, u32[]{:S(2)}) copy-start(pred[1536,128]{1,0:T(8,128)(4,1)S(1)} %fusion) | copy-start | bytes 589828
  50.7 86.4 %all-gather.5.cloned.1.call-start = ((), (), s32[]{:S(2)}) async-start(), calls=%async_computation.8 | async-start | bytes 7077888 | tf_op jit(solution)/shard_map/all_gather | solution.py:47
  86.9 106.2 %reduce-scatter.3.cloned.1.call-start = ((), (), s32[]{:S(2)}) async-start(), calls=%async_computation.7 | async-start | bytes 7077888 | tf_op jit(solution)/shard_map/reduce_scatter | solution.py:80
  91.2 5.6 %copy-start.1 = (bf16[8,2,768,256]{3,2,0,1:T(8,128)(2,1)S(1)}, bf16[8,2,768,256]{3,2,0,1:T(8,128)(2,1)}, u32[]{:S(2)}) copy-start(bf16[8,2,768,256]{3,2,0,1:T(8,128)(2,1)} %all-gather.3.cloned.1.call-done) | copy-start | bytes 18874372
  137.1 6.3 %copy-start.10 = (bf16[2,128,2048]{2,1,0:T(8,128)(2,1)S(1)}, bf16[2,128,2048]{2,1,0:T(8,128)(2,1)}, u32[]{:S(2)}) copy-start(bf16[2,128,2048]{2,1,0:T(8,128)(2,1)} %param.13) | copy-start | bytes 3145732
  142.7 0.7 copy-start.8
  142.7 5.2 %copy-start.5 = (bf16[2,768,128]{2,1,0:T(8,128)(2,1)}, bf16[2,768,128]{2,1,0:T(8,128)(2,1)S(1)}, u32[]{:S(2)}) copy-start(bf16[2,768,128]{2,1,0:T(8,128)(2,1)S(1)} %get-tuple-element.31) | copy-start | bytes 1179652
  142.7 11.4 %copy-start.7 = (bf16[2,768,128]{2,1,0:T(8,128)(2,1)}, bf16[2,768,128]{2,1,0:T(8,128)(2,1)S(1)}, u32[]{:S(2)}) copy-start(bf16[2,768,128]{2,1,0:T(8,128)(2,1)S(1)} %get-tuple-element.30) | copy-start | bytes 1179652
  147.8 92.8 %reduce-scatter.5.cloned.1.call-start = ((), (), s32[]{:S(2)}) async-start(), calls=%async_computation.9 | async-start | bytes 7077888 | tf_op jit(solution)/shard_map/reduce_scatter | solution.py:81
  154.1 99.4 %copy-start.9 = (bf16[2,768,128]{2,1,0:T(8,128)(2,1)S(1)}, bf16[2,768,128]{2,1,0:T(8,128)(2,1)}, u32[]{:S(2)}) copy-start(bf16[2,768,128]{2,1,0:T(8,128)(2,1)} %copy-done.8) | copy-start | bytes 1179652
  195.9 47.6 %all-to-all-start.1 = ((bf16[2,768,256]{2,0,1:T(2,128)(2,1)}), bf16[2,768,256]{2,0,1:T(2,128)(2,1)S(1)}, u32[]{:S(2)}, u32[]{:S(2)}) async-start(bf16[2,768,256]{2,0,1:T(2,128)(2,1)} %copy.71), calls=%async_computation.2 | async-start | bytes 1572864 | tf_op jit(solution)/shard_map/all_to_all | solution.py:84
  243.5 16.7 %copy-start.3 = (bf16[2,768,256]{2,0,1:T(2,128)(2,1)}, bf16[2,768,256]{2,0,1:T(2,128)(2,1)S(1)}, u32[]{:S(2)}) copy-start(bf16[2,768,256]{2,0,1:T(2,128)(2,1)S(1)} %all-to-all-done.1) | copy-start | bytes 2359300
  243.5 61.2 %all-to-all-start.3 = ((bf16[2,768,256]{2,0,1:T(2,128)(2,1)}), bf16[2,768,256]{2,0,1:T(2,128)(2,1)}, u32[]{:S(2)}, u32[]{:S(2)}) async-start(bf16[2,768,256]{2,0,1:T(2,128)(2,1)} %copy.75), calls=%async_computation.5 | async-start | bytes 1572864 | tf_op jit(solution)/shard_map/all_to_all | solution.py:85
  260.2 9.9 %slice-start = ((s8[6291456]{0:T(1024)(128)(4,1)}), s8[2097152]{0:T(1024)(128)(4,1)S(1)}, s32[]{:S(2)}) async-start(s8[6291456]{0:T(1024)(128)(4,1)} %bitcast.81), calls=%async_computation.10 | async-start | bytes 4194304
  263.3 6.8 %slice-start.1 = ((s8[6291456]{0:T(1024)(128)(4,1)}), s8[4194304]{0:T(1024)(128)(4,1)S(1)}, s32[]{:S(2)}) async-start(s8[6291456]{0:T(1024)(128)(4,1)} %bitcast.81), calls=%async_computation.11 | async-start | bytes 8388608
  263.3 6.8 %copy-start.6 = (bf16[2,768,128]{2,1,0:T(8,128)(2,1)S(1)}, bf16[2,768,128]{2,1,0:T(8,128)(2,1)}, u32[]{:S(2)}) copy-start(bf16[2,768,128]{2,1,0:T(8,128)(2,1)} %copy-done.5) | copy-start | bytes 1179652
  270.1 3.9 %copy-start.4 = (bf16[2,768,256]{2,0,1:T(2,128)(2,1)S(1)}, bf16[2,768,256]{2,0,1:T(2,128)(2,1)}, u32[]{:S(2)}) copy-start(bf16[2,768,256]{2,0,1:T(2,128)(2,1)} %copy-done.3) | copy-start | bytes 2359300
  274.0 4.1 %copy-start.13 = (f32[128,256]{1,0:T(8,128)S(1)}, f32[128,256]{1,0:T(8,128)}, u32[]{:S(2)}) copy-start(f32[128,256]{1,0:T(8,128)} %convert_element_type.88) | copy-start | bytes 393220
  274.0 32.0 %copy-start.12 = (pred[1536,128]{1,0:T(8,128)(4,1)S(1)}, pred[1536,128]{1,0:T(8,128)(4,1)}, u32[]{:S(2)}) copy-start(pred[1536,128]{1,0:T(8,128)(4,1)} %copy-done.11) | copy-start | bytes 589828
Sparse Core Ops, SparseCore 0:
  50.8 40.3 all-gather.2
  93.6 43.4 all-gather.4
  147.9 45.1 reduce-scatter.2
  195.5 45.0 reduce-scatter.4

commit v2 on v1

--- a/solution.py
+++ b/solution.py
@@ -26,25 +26,21 @@
     slots = experts * capacity
     places = places_in_block(expert_ids, experts)
     slot_index = (expert_ids.reshape(-1) * capacity + places).reshape(tok_rows, per_token)
-    match = slot_index[None, :, :] == jnp.arange(slots, dtype=jnp.int32)[:, None, None]
-    select = jnp.any(match, axis=2).astype(jnp.bfloat16)
+    by_pair = slot_index.T
+    match = by_pair[None, :, :] == jnp.arange(slots, dtype=jnp.int32)[:, None, None]
+    select = jnp.any(match, axis=1).astype(jnp.bfloat16)
     gate_select = jnp.sum(
-        jnp.where(match, route_gates[None, :, :].astype(jnp.float32), 0.0), axis=2
+        jnp.where(match, route_gates.T[None, :, :].astype(jnp.float32), 0.0), axis=1
     ).astype(jnp.bfloat16)
     picked = jnp.dot(select, tokens, preferred_element_type=jnp.float32).astype(jnp.bfloat16)
     scaled = jnp.dot(gate_select, cotangent, preferred_element_type=jnp.float32).astype(
         jnp.bfloat16
     )
-    expert_in_part, expert_cot_part = (
-        lax.all_to_all(
-            picked.reshape(experts, capacity, width), "dp", split_axis=0, concat_axis=1, tiled=True
-        ),
-        lax.all_to_all(
-            scaled.reshape(experts, capacity, width), "dp", split_axis=0, concat_axis=1, tiled=True
-        ),
-    )
-    expert_in = lax.all_gather(expert_in_part, "et", axis=0)
-    expert_cot = lax.all_gather(expert_cot_part, "et", axis=0)
+    routed = jnp.stack([picked, scaled]).reshape(2, experts, capacity, width)
+    routed = lax.all_to_all(routed, "dp", split_axis=1, concat_axis=2, tiled=True)
+    gathered = lax.all_gather(routed, "et", axis=0)
+    expert_in = gathered[:, 0]
+    expert_cot = gathered[:, 1]
     gate_w = gate_proj.reshape(local_experts, shards, width, units)
     up_w = up_proj.reshape(local_experts, shards, width, units)
     down_w = down_proj.reshape(local_experts, units, shards, width)

time: 314 us -> 329 us (1.048)
  waiting for transfers between devices: 114 us -> 140 us
  blocking collectives: 85.2 us -> 75.4 us
    all_gather x2 -> x1, waiting for transfers between devices: 41.7 us -> 66.7 us  [local(): gathered = lax.all_gather(routed, 'et', axis=0)]
    all_to_all x2 -> x1, blocking collectives: 60.5 us -> 50.7 us  [local(): lax.all_to_all(routed, 'dp', split_axis=1, concat_axis=2, tiled=True)]
    dot_general x1, matrix products: 5.53 us -> 2 us  [local(): jnp.einsum('jesd,efjd->esf', expert_cot, down_w, preferred_element_type=j...]
  transfers between devices with their start and end apart: 6 -> 5, of which waited for: 4 -> 3; matrix products, arithmetic and copies ran while one was open for 18% -> 12% of each run, Pallas kernels for 0% -> 0%
where the time goes in v2:
time: 329 us
  waiting for transfers between devices  140 us (43%)
  blocking collectives  75.4 us (23%)
  matrix products  46.6 us (14%)
  starting transfers between devices  20.5 us (6%)
  local copies, waits for them, and re-layouts  16.7 us (5%)
  other arithmetic  15.5 us (5%)
  between operations  14.1 us (4%)
    all_gather x1, waiting for transfers between devices, local(): gathered = lax.all_gather(routed, 'et', axis=0)  66.7 us
    all_to_all x1, blocking collectives, local(): lax.all_to_all(routed, 'dp', split_axis=1, concat_axis=2, tiled=True)  50.7 us
    reduce_scatter x1, waiting for transfers between devices, local(): lax.psum_scatter(out_part.astype(jnp.bfloat16), 'et', scatter_dimension=2...  39.3 us
    reduce_scatter x1, waiting for transfers between devices, local(): lax.psum_scatter(in_part.astype(jnp.bfloat16), 'et', scatter_dimension=2,...  33.8 us
    psum x1, blocking collectives, local(): grad_gates = lax.psum(gate_part, 'et')  24.7 us
    all_to_all x1, starting transfers between devices, local(): lax.all_to_all(out_sum, 'dp', split_axis=1, concat_axis=0, tiled=True)  10.1 us
    all_to_all x1, starting transfers between devices, local(): lax.all_to_all(in_sum, 'dp', split_axis=1, concat_axis=0, tiled=True)  10.1 us
    reduce_sum x1, other arithmetic, local(): jnp.sum(jnp.where(match, route_gates.T[None, :, :].astype(jnp.float32), 0...  8.15 us
  transfers between devices with their start and end apart: 5, of which 3 were waited for; matrix products, arithmetic and copies ran while one was open for 12% of the time, Pallas kernels for 0%

profile of v2, /device:TPU:2, one launch (start us, length us, event | category | flops | bytes accessed | tf_op | source)
XLA Modules:
  0.0 328.7 jit_solution(484087539045145669)
XLA Ops:
  7.2 0.0 copy-start
  7.2 0.0 all-gather.2.cloned.1.call-start
  7.2 0.8 convert_bitcast_fusion
  8.0 0.8 copy.65
  8.8 0.1 eq.28
  8.9 0.6 fusion.12
  9.5 0.1 convert_element_type.78
  9.6 5.6 %fusion = pred[1536,128]{1,0:T(8,128)(4,1)S(1)} fusion(s32[8,128]{1,0:T(8,128)S(1)} %copy.67), kind=kLoop, calls=%fused_computation.6 | loop fusion | flops 2949120 | bytes 200704 | tf_op jit(solution)/shard_map/reduce_or | solution.py:31
  15.2 0.0 copy-start.11
  15.2 8.1 %select_reduce_fusion = bf16[1536,128]{1,0:T(8,128)(2,1)S(1)} fusion(f32[8,128]{1,0:T(8,128)S(1)} %convert_bitcast_fusion, s32[8,128]{1,0:T(8,128)S(1)} %copy.67), kind=kLoop, calls=%fused_computation.4 | loop fusion | flops 4521984 | bytes 401408 | tf_op jit(solution)/shard_map/reduce_sum | solution.py:32
  23.4 1.2 convolution_convert_fusion.1
  24.6 0.0 copy-start.9
  24.6 1.3 convolution_convert_fusion.2
  25.9 0.0 copy-done.11
  25.9 0.1 pad_maximum_fusion
  26.1 50.7 %all_to_all.45 = bf16[2,64,24,256]{3,2,0,1:T(8,128)(2,1)S(1)} all-to-all(bf16[2,64,24,256]{3,2,0,1:T(8,128)(2,1)S(1)} %pad_maximum_fusion), channel_id=1, replica_groups=mesh['dp'=32,'et'=8] {'dp'}, dimensions={1} | all-to-all | bytes 3145728 | tf_op jit(solution)/shard_map/all_to_all | solution.py:40
  76.8 1.2 copy.70
  78.0 0.0 all-gather.2.cloned.1.call-update
  78.0 0.2 reduce-scatter.3.cloned.1.call-start
  78.3 66.7 %all-gather.2.cloned.1.call-done = bf16[8,2,2,768,256]{4,3,0,2,1:T(8,128)(2,1)} async-done(((bf16[1,2,2,768,256]{4,3,0,2,1:T(8,128)(2,1)}), bf16[8,2,2,768,256]{4,3,0,2,1:T(8,128)(2,1)}) %all-gather.2.cloned.1.call-update) | async-done | bytes 12582928 | tf_op jit(solution)/shard_map/all_gather | solution.py:41
  144.9 0.0 copy-done.9
  145.0 4.7 %fusion.9 = f32[2,768,128]{2,1,0:T(8,128)S(1)} fusion(bf16[2,8,256,128]{3,2,1,0:T(8,128)(2,1)S(1)} %bitcast.108, bf16[8,2,2,768,256]{4,3,0,2,1:T(8,128)(2,1)} %all-gather.2.cloned.1.call-done), kind=kOutput, calls=%fused_computation.20 | convolution fusion | flops 805306368 | bytes 8126464 | tf_op jit(solution)/shard_map/jesd,ejdf->esf/dot_general | solution.py:48
  149.7 0.0 copy-done
  149.7 0.0 copy-start.10
  149.7 5.2 %fusion.8 = f32[2,768,128]{2,1,0:T(8,128)S(1)} fusion(bf16[2,8,256,128]{3,2,1,0:T(8,128)(2,1)S(1)} %bitcast.96, bf16[8,2,2,768,256]{4,3,0,2,1:T(8,128)(2,1)} %all-gather.2.cloned.1.call-done), kind=kOutput, calls=%fused_computation.19 | convolution fusion | flops 805306368 | bytes 8126464 | tf_op jit(solution)/shard_map/jesd,ejdf->esf/dot_general | solution.py:47
  154.9 0.0 copy-done.2
  154.9 0.0 copy-done.10
  154.9 2.0 multiply_convert_fusion
  156.9 0.0 copy-start.8
  157.0 0.0 copy-start.5
  157.0 0.0 copy-start.7
  157.0 0.7 copy-done.8
  157.7 4.4 %convolution_convert_fusion = bf16[2,768,2048]{2,1,0:T(8,128)(2,1)} fusion(bf16[2,768,128]{2,1,0:T(8,128)(2,1)S(1)} %get-tuple-element.32, bf16[2,128,2048]{2,1,0:T(8,128)(2,1)S(1)} %copy-done.10), kind=kOutput, calls=%fused_computation.9 | convolution fusion | flops 808452096 | bytes 7733248 | tf_op jit(solution)/shard_map/esf,efd->esd/dot_general | solution.py:52
  162.1 0.0 reduce-scatter.3.cloned.1.call-update
  162.1 0.0 reduce-scatter.5.cloned.1.call-start
  162.2 1.8 fusion.24
  164.0 0.0 copy-done.7
  164.0 4.4 %add_convert_fusion = bf16[2,768,2048]{2,1,0:T(8,128)(2,1)} fusion(f32[2,768,2048]{2,1,0:T(8,128)S(1)} %fusion.24, bf16[2,768,128]{2,1,0:T(8,128)(2,1)S(1)} %get-tuple-element.30, bf16[2,2048,128]{2,1,0:T(8,128)(2,1)S(1)} %copy-done.9), kind=kOutput, calls=%fused_computation.1 | convolution fusion | flops 811597824 | bytes 20316160 | tf_op jit(solution)/shard_map/esf,edf->esd/dot_general | solution.py:72
  168.4 0.0 reduce-scatter.5.cloned.1.call-update
  168.4 39.3 %reduce-scatter.3.cloned.1.call-done = bf16[2,768,256]{2,1,0:T(8,128)(2,1)} async-done(((bf16[2,768,2048]{2,1,0:T(8,128)(2,1)}), bf16[2,768,256]{2,1,0:T(8,128)(2,1)}) %reduce-scatter.3.cloned.1.call-update) | async-done | bytes 786448 | tf_op jit(solution)/shard_map/reduce_scatter | solution.py:76
  207.7 2.8 copy.71
  210.5 10.1 %all-to-all-start.1 = ((bf16[2,768,256]{2,0,1:T(2,128)(2,1)}), bf16[2,768,256]{2,0,1:T(2,128)(2,1)S(1)}, u32[]{:S(2)}, u32[]{:S(2)}) async-start(bf16[2,768,256]{2,0,1:T(2,128)(2,1)} %copy.71), calls=%async_computation.2 | async-start | bytes 1572864 | tf_op jit(solution)/shard_map/all_to_all | solution.py:80
  220.7 0.7 convert_element_type.91
  221.3 0.1 mul.64
  221.5 33.8 %reduce-scatter.5.cloned.1.call-done = bf16[2,768,256]{2,1,0:T(8,128)(2,1)} async-done(((bf16[2,768,2048]{2,1,0:T(8,128)(2,1)}), bf16[2,768,256]{2,1,0:T(8,128)(2,1)}) %reduce-scatter.5.cloned.1.call-update) | async-done | bytes 786448 | tf_op jit(solution)/shard_map/reduce_scatter | solution.py:77
  255.3 2.9 copy.74
  258.2 0.0 all-to-all-done.1
  258.2 10.1 %all-to-all-start.2 = ((bf16[2,768,256]{2,0,1:T(2,128)(2,1)}), bf16[2,768,256]{2,0,1:T(2,128)(2,1)}, u32[]{:S(2)}, u32[]{:S(2)}) async-start(bf16[2,768,256]{2,0,1:T(2,128)(2,1)} %copy.74), calls=%async_computation.4 | async-start | bytes 1572864 | tf_op jit(solution)/shard_map/all_to_all | solution.py:81
  268.3 5.5 %fusion.1 = f32[2,128,8,256]{1,3,2,0:T(8,128)S(1)} fusion(bf16[8,2,2,768,256]{4,3,0,2,1:T(8,128)(2,1)} %all-gather.2.cloned.1.call-done, bf16[2,768,128]{2,1,0:T(8,128)(2,1)} %copy-done.8), kind=kOutput, calls=%fused_computation.7 | convolution fusion | flops 805306368 | bytes 8781824 | tf_op jit(solution)/shard_map/esf,jesd->efjd/dot_general | solution.py:60
  273.8 1.8 copy.82
  275.6 0.0 copy-done.3
  275.6 6.7 %fusion.4 = f32[2,8,256,128]{3,2,1,0:T(8,128)} fusion(bf16[8,2,2,768,256]{4,3,0,2,1:T(8,128)(2,1)} %all-gather.2.cloned.1.call-done, bf16[2,768,128]{2,1,0:T(8,128)(2,1)} %copy-done.7), kind=kOutput, calls=%fused_computation.12 | convolution fusion | flops 805306368 | bytes 8781824 | tf_op jit(solution)/shard_map/jesd,esf->ejdf/dot_general | solution.py:66
  282.3 6.7 %fusion.5 = f32[2,8,256,128]{3,2,1,0:T(8,128)} fusion(bf16[8,2,2,768,256]{4,3,0,2,1:T(8,128)(2,1)} %all-gather.2.cloned.1.call-done, bf16[2,768,128]{2,1,0:T(8,128)(2,1)S(1)} %copy-done.6), kind=kOutput, calls=%fused_computation.13 | convolution fusion | flops 805306368 | bytes 8781824 | tf_op jit(solution)/shard_map/jesd,esf->ejdf/dot_general | solution.py:63
  289.1 0.1 copy.72
  289.2 3.9 %gather_fusion = bf16[1024,256]{1,0:T(8,128)(2,1)S(1)} fusion(bf16[1536,256]{1,0:T(8,128)(2,1)S(1)} %bitcast.97, s32[1024]{0:T(1024)S(1)} %broadcast_clamp_fusion), kind=kCustom, calls=%fused_computation | custom fusion | bytes 1052672 | tf_op jit(solution)/shard_map/gather | solution.py:91
  293.2 0.0 copy-done.13
  293.2 0.2 fusion.15
  293.4 24.7 %psum.7 = f32[128,8]{1,0:T(8,128)S(1)} all-reduce(f32[128,8]{1,0:T(8,128)S(1)} %fusion.15), channel_id=1, replica_groups=mesh['dp'=32,'et'=8] {'et'}, use_global_device_ids=true, to_apply=%region_6.7 | all-reduce | flops 1024 | bytes 8192 | tf_op jit(solution)/shard_map/psum | solution.py:95
  318.1 0.7 copy.81
  318.8 1.0 convolution_convert_fusion.3
  319.7 0.0 all-to-all-done.2
  319.7 1.2 copy.75
  321.0 0.1 copy.76
  321.1 1.1 convolution_convert_fusion.4
  (19 shorter events, 0.1 us)
Async XLA Ops:
  7.2 142.5 %copy-start = (bf16[2,2048,128]{2,1,0:T(8,128)(2,1)S(1)}, bf16[2,2048,128]{2,1,0:T(8,128)(2,1)}, u32[]{:S(2)}) copy-start(bf16[2,2048,128]{2,1,0:T(8,128)(2,1)} %param.11) | copy-start | bytes 3145732
  7.2 137.8 %all-gather.2.cloned.1.call-start = ((), (), s32[]{:S(2)}) async-start(), calls=%async_computation.5 | async-start | bytes 14155776 | tf_op jit(solution)/shard_map/all_gather | solution.py:41
  15.2 10.7 %copy-start.11 = (pred[1536,128]{1,0:T(8,128)(4,1)}, pred[1536,128]{1,0:T(8,128)(4,1)S(1)}, u32[]{:S(2)}) copy-start(pred[1536,128]{1,0:T(8,128)(4,1)S(1)} %fusion) | copy-start | bytes 589828
  24.6 120.4 %copy-start.9 = (bf16[2,2048,128]{2,1,0:T(8,128)(2,1)S(1)}, bf16[2,2048,128]{2,1,0:T(8,128)(2,1)}, u32[]{:S(2)}) copy-start(bf16[2,2048,128]{2,1,0:T(8,128)(2,1)} %param.12) | copy-start | bytes 3145732
  78.0 129.7 %reduce-scatter.3.cloned.1.call-start = ((), (), s32[]{:S(2)}) async-start(), calls=%async_computation.6 | async-start | bytes 7077888 | tf_op jit(solution)/shard_map/reduce_scatter | solution.py:76
  144.9 10.0 %copy-start.2 = (bf16[8,2,2,768,256]{4,3,0,2,1:T(8,128)(2,1)S(1)}, bf16[8,2,2,768,256]{4,3,0,2,1:T(8,128)(2,1)}, u32[]{:S(2)}) copy-start(bf16[8,2,2,768,256]{4,3,0,2,1:T(8,128)(2,1)} %all-gather.2.cloned.1.call-done) | copy-start | bytes 37748740
  149.7 5.3 %copy-start.10 = (bf16[2,128,2048]{2,1,0:T(8,128)(2,1)S(1)}, bf16[2,128,2048]{2,1,0:T(8,128)(2,1)}, u32[]{:S(2)}) copy-start(bf16[2,128,2048]{2,1,0:T(8,128)(2,1)} %param.13) | copy-start | bytes 3145732
  156.9 0.7 copy-start.8
  157.0 5.2 %copy-start.5 = (bf16[2,768,128]{2,1,0:T(8,128)(2,1)}, bf16[2,768,128]{2,1,0:T(8,128)(2,1)S(1)}, u32[]{:S(2)}) copy-start(bf16[2,768,128]{2,1,0:T(8,128)(2,1)S(1)} %get-tuple-element.31) | copy-start | bytes 1179652
  157.0 7.0 %copy-start.7 = (bf16[2,768,128]{2,1,0:T(8,128)(2,1)}, bf16[2,768,128]{2,1,0:T(8,128)(2,1)S(1)}, u32[]{:S(2)}) copy-start(bf16[2,768,128]{2,1,0:T(8,128)(2,1)S(1)} %get-tuple-element.30) | copy-start | bytes 1179652
  162.1 93.2 %reduce-scatter.5.cloned.1.call-start = ((), (), s32[]{:S(2)}) async-start(), calls=%async_computation.7 | async-start | bytes 7077888 | tf_op jit(solution)/shard_map/reduce_scatter | solution.py:77
  168.4 52.3 %copy-start.14 = (bf16[128,256]{1,0:T(8,128)(2,1)S(1)}, bf16[128,256]{1,0:T(8,128)(2,1)}, u32[]{:S(2)}) copy-start(bf16[128,256]{1,0:T(8,128)(2,1)} %param.8) | copy-start | bytes 196612
  210.5 47.7 %all-to-all-start.1 = ((bf16[2,768,256]{2,0,1:T(2,128)(2,1)}), bf16[2,768,256]{2,0,1:T(2,128)(2,1)S(1)}, u32[]{:S(2)}, u32[]{:S(2)}) async-start(bf16[2,768,256]{2,0,1:T(2,128)(2,1)} %copy.71), calls=%async_computation.2 | async-start | bytes 1572864 | tf_op jit(solution)/shard_map/all_to_all | solution.py:80
  258.2 17.4 %copy-start.3 = (bf16[2,768,256]{2,0,1:T(2,128)(2,1)}, bf16[2,768,256]{2,0,1:T(2,128)(2,1)S(1)}, u32[]{:S(2)}) copy-start(bf16[2,768,256]{2,0,1:T(2,128)(2,1)S(1)} %all-to-all-done.1) | copy-start | bytes 2359300
  258.2 61.5 %all-to-all-start.2 = ((bf16[2,768,256]{2,0,1:T(2,128)(2,1)}), bf16[2,768,256]{2,0,1:T(2,128)(2,1)}, u32[]{:S(2)}, u32[]{:S(2)}) async-start(bf16[2,768,256]{2,0,1:T(2,128)(2,1)} %copy.74), calls=%async_computation.4 | async-start | bytes 1572864 | tf_op jit(solution)/shard_map/all_to_all | solution.py:81
  275.6 6.7 %copy-start.6 = (bf16[2,768,128]{2,1,0:T(8,128)(2,1)S(1)}, bf16[2,768,128]{2,1,0:T(8,128)(2,1)}, u32[]{:S(2)}) copy-start(bf16[2,768,128]{2,1,0:T(8,128)(2,1)} %copy-done.5) | copy-start | bytes 1179652
  282.3 6.8 %copy-start.4 = (bf16[2,768,256]{2,0,1:T(2,128)(2,1)S(1)}, bf16[2,768,256]{2,0,1:T(2,128)(2,1)}, u32[]{:S(2)}) copy-start(bf16[2,768,256]{2,0,1:T(2,128)(2,1)} %copy-done.3) | copy-start | bytes 2359300
  282.3 10.8 %copy-start.13 = (f32[128,256]{1,0:T(8,128)S(1)}, f32[128,256]{1,0:T(8,128)}, u32[]{:S(2)}) copy-start(f32[128,256]{1,0:T(8,128)} %convert_element_type.91) | copy-start | bytes 393220
  289.1 32.0 %copy-start.12 = (pred[1536,128]{1,0:T(8,128)(4,1)S(1)}, pred[1536,128]{1,0:T(8,128)(4,1)}, u32[]{:S(2)}) copy-start(pred[1536,128]{1,0:T(8,128)(4,1)} %copy-done.11) | copy-start | bytes 589828
  289.1 33.0 %copy-start.1 = (bf16[2,2048,128]{2,1,0:T(8,128)(2,1)S(1)}, bf16[2,2048,128]{2,1,0:T(8,128)(2,1)}, u32[]{:S(2)}) copy-start(bf16[2,2048,128]{2,1,0:T(8,128)(2,1)} %param.11) | copy-start | bytes 3145732
Sparse Core Ops, SparseCore 0:
  78.2 66.7 all-gather.1
  162.2 45.4 reduce-scatter.2
  210.3 44.9 reduce-scatter.4

commit v3 on v1

--- a/solution.py
+++ b/solution.py
@@ -26,10 +26,20 @@
     slots = experts * capacity
     places = places_in_block(expert_ids, experts)
     slot_index = (expert_ids.reshape(-1) * capacity + places).reshape(tok_rows, per_token)
-    match = slot_index[None, :, :] == jnp.arange(slots, dtype=jnp.int32)[:, None, None]
-    select = jnp.any(match, axis=2).astype(jnp.bfloat16)
-    gate_select = jnp.sum(
-        jnp.where(match, route_gates[None, :, :].astype(jnp.float32), 0.0), axis=2
+    pairs = tok_rows * per_token
+    pair_slot = (
+        slot_index.reshape(pairs, 1) == jnp.arange(slots, dtype=jnp.int32)[None, :]
+    ).astype(jnp.bfloat16)
+    owner = (
+        lax.broadcasted_iota(jnp.int32, (tok_rows, pairs), 1) // per_token
+        == lax.broadcasted_iota(jnp.int32, (tok_rows, pairs), 0)
+    )
+    gate_owner = jnp.where(owner, route_gates.reshape(1, pairs), jnp.zeros((), jnp.bfloat16))
+    select = jnp.einsum(
+        "tp,ps->st", owner.astype(jnp.bfloat16), pair_slot, preferred_element_type=jnp.float32
+    ).astype(jnp.bfloat16)
+    gate_select = jnp.einsum(
+        "tp,ps->st", gate_owner, pair_slot, preferred_element_type=jnp.float32
     ).astype(jnp.bfloat16)
     picked = jnp.dot(select, tokens, preferred_element_type=jnp.float32).astype(jnp.bfloat16)
     scaled = jnp.dot(gate_select, cotangent, preferred_element_type=jnp.float32).astype(
@@ -76,10 +86,13 @@
     in_part = in_part + jnp.einsum(
         "esf,edf->esd", grad_pre_up, up_proj, preferred_element_type=jnp.float32
     )
-    out_sum, in_sum = (
-        lax.psum_scatter(out_part.astype(jnp.bfloat16), "et", scatter_dimension=2, tiled=True),
-        lax.psum_scatter(in_part.astype(jnp.bfloat16), "et", scatter_dimension=2, tiled=True),
+    out_sum = lax.psum_scatter(
+        out_part.astype(jnp.bfloat16), "et", scatter_dimension=2, tiled=True
     )
+    in_part, grad_gate_w, grad_up_w, grad_down = lax.optimization_barrier(
+        (in_part.astype(jnp.bfloat16), grad_gate_w, grad_up_w, grad_down)
+    )
+    in_sum = lax.psum_scatter(in_part, "et", scatter_dimension=2, tiled=True)
     back_out, back_grad = (
         lax.all_to_all(out_sum, "dp", split_axis=1, concat_axis=0, tiled=True),
         lax.all_to_all(in_sum, "dp", split_axis=1, concat_axis=0, tiled=True),

time: 314 us -> 296 us (0.943)
  other arithmetic: 14.6 us -> 1.76 us
  waiting for transfers between devices: 114 us -> 105 us
    reduce_scatter x1, waiting for transfers between devices: 39 us -> 22.3 us  [local(): lax.psum_scatter(out_part.astype(jnp.bfloat16), 'et', scatter_dimension=2...]
    reduce_sum x1 -> x0, other arithmetic: 8.15 us -> none  [local(): jnp.sum(jnp.where(match, route_gates[None, :, :].astype(jnp.float32), 0.0...]
    all_gather x1, waiting for transfers between devices: 4.05 us -> 10.9 us  [local(): expert_in = lax.all_gather(expert_in_part, 'et', axis=0)]
    reduce_or x1 -> x0, other arithmetic: 5.58 us -> none  [local(): select = jnp.any(match, axis=2).astype(jnp.bfloat16)]
  transfers between devices with their start and end apart: 6 -> 6, of which waited for: 4 -> 4; matrix products, arithmetic and copies ran while one was open for 18% -> 17% of each run, Pallas kernels for 0% -> 0%
where the time goes in v3:
time: 296 us; the launch traced here: 295 us
  waiting for transfers between devices  105 us (35%)
  blocking collectives  86 us (29%)
  matrix products  46.7 us (16%)
  starting transfers between devices  20.8 us (7%)
  local copies, waits for them, and re-layouts  20.4 us (7%)
  between operations  14.1 us (5%)
    all_gather x1, waiting for transfers between devices, local(): expert_cot = lax.all_gather(expert_cot_part, 'et', axis=0)  37.7 us
    reduce_scatter x1, waiting for transfers between devices, local(): in_sum = lax.psum_scatter(in_part, 'et', scatter_dimension=2, tiled=True)  34.5 us
    all_to_all x1, blocking collectives, local(): lax.all_to_all(picked.reshape(experts, capacity, width), 'dp', split_axis...  33.9 us
    all_to_all x1, blocking collectives, local(): lax.all_to_all(scaled.reshape(experts, capacity, width), 'dp', split_axis...  26.7 us
    psum x1, blocking collectives, local(): grad_gates = lax.psum(gate_part, 'et')  25.5 us
    reduce_scatter x1, waiting for transfers between devices, local(): lax.psum_scatter(out_part.astype(jnp.bfloat16), 'et', scatter_dimension=2...  22.3 us
    all_gather x1, waiting for transfers between devices, local(): expert_in = lax.all_gather(expert_in_part, 'et', axis=0)  10.9 us
    all_to_all x1, starting transfers between devices, local(): lax.all_to_all(in_sum, 'dp', split_axis=1, concat_axis=0, tiled=True)  10.3 us
  transfers between devices with their start and end apart: 6, of which 4 were waited for; matrix products, arithmetic and copies ran while one was open for 17% of the time, Pallas kernels for 0%

profile of v3, /device:TPU:2, one launch (start us, length us, event | category | flops | bytes accessed | tf_op | source)
XLA Modules:
  0.0 295.2 jit_solution(13721810918180096629)
XLA Ops:
  7.2 0.0 copy-start
  7.2 0.0 copy-start.14
  7.2 0.0 all-gather.3.cloned.1.call-start
  7.3 0.9 copy.48
  8.1 0.1 reshape.103
  8.2 0.0 copy-start.16
  8.2 0.6 fusion.15
  8.8 1.3 fusion.11
  10.1 0.0 copy-done.14
  10.1 0.0 copy-start.13
  10.1 0.3 convolution_convert_fusion.2
  10.5 33.9 %all_to_all.60 = bf16[64,24,256]{2,1,0:T(8,128)(2,1)S(1)} all-to-all(bf16[64,24,256]{2,1,0:T(8,128)(2,1)S(1)} %bitcast.93), channel_id=1, replica_groups=mesh['dp'=32,'et'=8] {'dp'}, dimensions={0} | all-to-all | bytes 1572864 | tf_op jit(solution)/shard_map/all_to_all | solution.py:49
  44.4 0.9 copy.50
  45.3 0.0 all-gather.3.cloned.1.call-update
  45.3 0.0 all-gather.5.cloned.1.call-start
  45.4 0.1 copy.49
  45.5 0.1 broadcast_in_dim.18
  45.6 1.2 fusion.8
  46.9 0.3 convolution_convert_fusion.1
  47.2 26.7 %all_to_all.61 = bf16[64,24,256]{2,1,0:T(8,128)(2,1)S(1)} all-to-all(bf16[64,24,256]{2,1,0:T(8,128)(2,1)S(1)} %bitcast.94), channel_id=1, replica_groups=mesh['dp'=32,'et'=8] {'dp'}, dimensions={0} | all-to-all | bytes 1572864 | tf_op jit(solution)/shard_map/all_to_all | solution.py:52
  73.9 0.9 copy.53
  74.8 0.0 all-gather.5.cloned.1.call-update
  74.9 0.0 reduce-scatter.3.cloned.1.call-start
  74.9 10.9 %all-gather.3.cloned.1.call-done = bf16[8,2,768,256]{3,2,0,1:T(8,128)(2,1)} async-done(((bf16[1,2,768,256]{3,2,0,1:T(8,128)(2,1)}), bf16[8,2,768,256]{3,2,0,1:T(8,128)(2,1)}) %all-gather.3.cloned.1.call-update) | async-done | bytes 6291472 | tf_op jit(solution)/shard_map/all_gather | solution.py:56
  85.8 5.6 %convolution_bitcast_fusion.1 = f32[2,768,128]{2,1,0:T(8,128)} fusion(bf16[8,2,768,256]{3,2,0,1:T(8,128)(2,1)} %all-gather.3.cloned.1.call-done, bf16[2,8,256,128]{3,2,1,0:T(8,128)(2,1)S(1)} %bitcast.86), kind=kOutput, calls=%fused_computation.16 | convolution fusion | flops 805306368 | bytes 8126464 | tf_op jit(solution)/shard_map/jesd,ejdf->esf/dot_general | solution.py:62
  91.4 0.0 copy-done
  91.4 0.0 copy-done.1
  91.4 2.7 convolution_bitcast_fusion.2
  94.1 37.7 %all-gather.5.cloned.1.call-done = bf16[8,2,768,256]{3,2,0,1:T(8,128)(2,1)} async-done(((bf16[1,2,768,256]{3,2,0,1:T(8,128)(2,1)}), bf16[8,2,768,256]{3,2,0,1:T(8,128)(2,1)}) %all-gather.5.cloned.1.call-update) | async-done | bytes 6291472 | tf_op jit(solution)/shard_map/all_gather | solution.py:57
  131.7 5.7 %multiply_convert_fusion = (bf16[2,768,128]{2,1,0:T(8,128)(2,1)}, bf16[2,768,128]{2,1,0:T(8,128)(2,1)S(1)}, bf16[2,768,128]{2,1,0:T(8,128)(2,1)S(1)}) fusion(f32[2,768,128]{2,1,0:T(8,128)} %convolution_bitcast_fusion.2, f32[2,768,128]{2,1,0:T(8,128)S(1)} %copy-done.11, bf16[8,2,768,256]{3,2,0,1:T(8,128)(2,1)} %all-gather.5.cloned.1.call-done, ...), kind=kOutput, calls=%fused_computation.26 | convolution fusion | flops 808255488 | bytes 10092544 | tf_op jit(solution)/shard_map/jesd,efjd->esf/dot_general | solution.py:67
  137.4 0.7 copy-done.9
  138.2 4.4 %convolution_convert_fusion = bf16[2,768,2048]{2,1,0:T(8,128)(2,1)} fusion(bf16[2,768,128]{2,1,0:T(8,128)(2,1)S(1)} %get-tuple-element.34, bf16[2,128,2048]{2,1,0:T(8,128)(2,1)S(1)} %copy-done.10), kind=kOutput, calls=%fused_computation.4 | convolution fusion | flops 808452096 | bytes 7733248 | tf_op jit(solution)/shard_map/esf,efd->esd/dot_general | solution.py:66
  142.6 0.0 reduce-scatter.3.cloned.1.call-update
  142.6 0.2 reduce-scatter.5.cloned.1.call-start
  142.8 0.0 slice-start
  142.9 5.6 %fusion.21 = f32[2,128,8,256]{1,3,2,0:T(8,128)S(1)} fusion(bf16[8,2,768,256]{3,2,0,1:T(8,128)(2,1)} %all-gather.5.cloned.1.call-done, bf16[2,768,128]{2,1,0:T(8,128)(2,1)} %copy-done.9), kind=kOutput, calls=%fused_computation.33 | convolution fusion | flops 805306368 | bytes 8781824 | tf_op jit(solution)/shard_map/esf,jesd->efjd/dot_general | solution.py:74
  148.5 0.0 slice-start.1
  148.5 6.8 %fusion.23 = f32[2,8,256,128]{3,2,1,0:T(8,128)} fusion(bf16[8,2,768,256]{3,2,0,1:T(8,128)(2,1)} %all-gather.3.cloned.1.call-done, bf16[2,768,128]{2,1,0:T(8,128)(2,1)} %get-tuple-element.32), kind=kOutput, calls=%fused_computation.35 | convolution fusion | flops 805306368 | bytes 8781824 | tf_op jit(solution)/shard_map/jesd,esf->ejdf/dot_general | solution.py:80
  155.3 0.0 slice-done.1
  155.3 4.0 %fusion.25 = f32[2,8,256,128]{3,2,1,0:T(8,128)} fusion(bf16[8,2,768,256]{3,2,0,1:T(8,128)(2,1)S(1)} %bitcast.82, bf16[2,768,128]{2,1,0:T(8,128)(2,1)S(1)} %get-tuple-element.33), kind=kOutput, calls=%fused_computation.37 | convolution fusion | flops 805306368 | bytes 8781824 | tf_op jit(solution)/shard_map/jesd,esf->ejdf/dot_general | solution.py:77
  159.3 1.8 fusion.42
  161.1 4.5 %add_convert_fusion = bf16[2,768,2048]{2,1,0:T(8,128)(2,1)} fusion(f32[2,768,2048]{2,1,0:T(8,128)S(1)} %fusion.42, bf16[2,768,128]{2,1,0:T(8,128)(2,1)S(1)} %copy-done.8, bf16[2,2048,128]{2,1,0:T(8,128)(2,1)S(1)} %copy-done.3), kind=kOutput, calls=%fused_computation.1 | convolution fusion | flops 811597824 | bytes 20316160 | tf_op jit(solution)/shard_map/esf,edf->esd/dot_general | solution.py:86
  165.6 0.0 reduce-scatter.5.cloned.1.call-update
  165.6 22.3 %reduce-scatter.3.cloned.1.call-done = bf16[2,768,256]{2,1,0:T(8,128)(2,1)} async-done(((bf16[2,768,2048]{2,1,0:T(8,128)(2,1)}), bf16[2,768,256]{2,1,0:T(8,128)(2,1)}) %reduce-scatter.3.cloned.1.call-update) | async-done | bytes 786448 | tf_op jit(solution)/shard_map/reduce_scatter | solution.py:89
  187.9 3.0 %copy.51 = bf16[2,768,256]{2,0,1:T(2,128)(2,1)} copy(bf16[2,768,256]{2,1,0:T(8,128)(2,1)} %reduce-scatter.3.cloned.1.call-done) | data formatting | bytes 1572864 | tf_op jit(solution)/shard_map/reduce_scatter | solution.py:89
  190.9 10.2 %all-to-all-start.1 = ((bf16[2,768,256]{2,0,1:T(2,128)(2,1)}), bf16[2,768,256]{2,0,1:T(2,128)(2,1)}, u32[]{:S(2)}, u32[]{:S(2)}) async-start(bf16[2,768,256]{2,0,1:T(2,128)(2,1)} %copy.51), calls=%async_computation.2 | async-start | bytes 1572864 | tf_op jit(solution)/shard_map/all_to_all | solution.py:97
  201.1 34.5 %reduce-scatter.5.cloned.1.call-done = bf16[2,768,256]{2,1,0:T(8,128)(2,1)} async-done(((bf16[2,768,2048]{2,1,0:T(8,128)(2,1)}), bf16[2,768,256]{2,1,0:T(8,128)(2,1)}) %reduce-scatter.5.cloned.1.call-update) | async-done | bytes 786448 | tf_op jit(solution)/shard_map/reduce_scatter | solution.py:95
  235.7 2.8 copy.59
  238.5 0.0 all-to-all-done.1
  238.5 10.3 %all-to-all-start.3 = ((bf16[2,768,256]{2,0,1:T(2,128)(2,1)}), bf16[2,768,256]{2,0,1:T(2,128)(2,1)}, u32[]{:S(2)}, u32[]{:S(2)}) async-start(bf16[2,768,256]{2,0,1:T(2,128)(2,1)} %copy.59), calls=%async_computation.5 | async-start | bytes 1572864 | tf_op jit(solution)/shard_map/all_to_all | solution.py:98
  248.8 1.5 convert_element_type.85
  250.3 0.7 copy.62
  251.0 0.9 mul.72
  252.0 1.8 copy.64
  253.8 1.3 copy.52
  255.1 3.9 %gather_fusion = bf16[1024,256]{1,0:T(8,128)(2,1)S(1)} fusion(bf16[1536,256]{1,0:T(8,128)(2,1)S(1)} %bitcast.83, s32[1024]{0:T(1024)S(1)} %broadcast_clamp_fusion), kind=kCustom, calls=%fused_computation | custom fusion | bytes 1052672 | tf_op jit(solution)/shard_map/gather | solution.py:108
  259.1 0.2 fusion.18
  259.3 25.5 %psum.7 = f32[128,8]{1,0:T(8,128)S(1)} all-reduce(f32[128,8]{1,0:T(8,128)S(1)} %fusion.18), channel_id=1, replica_groups=mesh['dp'=32,'et'=8] {'et'}, use_global_device_ids=true, to_apply=%region_4.5 | all-reduce | flops 1024 | bytes 8192 | tf_op jit(solution)/shard_map/psum | solution.py:112
  284.8 0.7 copy.63
  285.5 1.0 convolution_convert_fusion.4
  286.4 0.0 all-to-all-done.3
  286.4 1.2 copy.60
  287.7 0.1 copy.61
  287.7 1.0 convolution_convert_fusion.3
  (35 shorter events, 0.1 us)
Async XLA Ops:
  7.2 84.2 %copy-start = (bf16[2,2048,128]{2,1,0:T(8,128)(2,1)S(1)}, bf16[2,2048,128]{2,1,0:T(8,128)(2,1)}, u32[]{:S(2)}) copy-start(bf16[2,2048,128]{2,1,0:T(8,128)(2,1)} %param.11) | copy-start | bytes 3145732
  7.2 2.9 copy-start.14
  7.2 78.6 %all-gather.3.cloned.1.call-start = ((), (), s32[]{:S(2)}) async-start(), calls=%async_computation.6 | async-start | bytes 7077888 | tf_op jit(solution)/shard_map/all_gather | solution.py:56
  8.2 37.2 %copy-start.16 = (bf16[128,8]{0,1:T(8,128)(2,1)S(1)}, bf16[128,8]{0,1:T(8,128)(2,1)}, u32[]{:S(2)}) copy-start(bf16[128,8]{0,1:T(8,128)(2,1)} %param.10) | copy-start | bytes 6148
  10.1 35.2 %copy-start.4 = (bf16[1536,128]{1,0:T(8,128)(2,1)}, bf16[1536,128]{1,0:T(8,128)(2,1)S(1)}, u32[]{:S(2)}) copy-start(bf16[1536,128]{1,0:T(8,128)(2,1)S(1)} %fusion.11) | copy-start | bytes 1179652
  10.1 36.7 %copy-start.13 = (bf16[128,256]{1,0:T(8,128)(2,1)S(1)}, bf16[128,256]{1,0:T(8,128)(2,1)}, u32[]{:S(2)}) copy-start(bf16[128,256]{1,0:T(8,128)(2,1)} %param.8) | copy-start | bytes 196612
  45.3 40.5 %copy-start.2 = (bf16[2,2048,128]{2,1,0:T(8,128)(2,1)S(1)}, bf16[2,2048,128]{2,1,0:T(8,128)(2,1)}, u32[]{:S(2)}) copy-start(bf16[2,2048,128]{2,1,0:T(8,128)(2,1)} %param.12) | copy-start | bytes 3145732
  45.3 86.4 %all-gather.5.cloned.1.call-start = ((), (), s32[]{:S(2)}) async-start(), calls=%async_computation.8 | async-start | bytes 7077888 | tf_op jit(solution)/shard_map/all_gather | solution.py:57
  46.9 28.0 %copy-start.6 = (bf16[1536,128]{1,0:T(8,128)(2,1)}, bf16[1536,128]{1,0:T(8,128)(2,1)S(1)}, u32[]{:S(2)}) copy-start(bf16[1536,128]{1,0:T(8,128)(2,1)S(1)} %fusion.8) | copy-start | bytes 1179652
  74.9 113.1 %reduce-scatter.3.cloned.1.call-start = ((), (), s32[]{:S(2)}) async-start(), calls=%async_computation.7 | async-start | bytes 7077888 | tf_op jit(solution)/shard_map/reduce_scatter | solution.py:89
  85.8 5.6 %copy-start.1 = (bf16[8,2,768,256]{3,2,0,1:T(8,128)(2,1)S(1)}, bf16[8,2,768,256]{3,2,0,1:T(8,128)(2,1)}, u32[]{:S(2)}) copy-start(bf16[8,2,768,256]{3,2,0,1:T(8,128)(2,1)} %all-gather.3.cloned.1.call-done) | copy-start | bytes 18874372
  85.8 45.9 %copy-start.10 = (bf16[2,128,2048]{2,1,0:T(8,128)(2,1)S(1)}, bf16[2,128,2048]{2,1,0:T(8,128)(2,1)}, u32[]{:S(2)}) copy-start(bf16[2,128,2048]{2,1,0:T(8,128)(2,1)} %param.13) | copy-start | bytes 3145732
  91.4 40.3 %copy-start.11 = (f32[2,768,128]{2,1,0:T(8,128)S(1)}, f32[2,768,128]{2,1,0:T(8,128)}, u32[]{:S(2)}) copy-start(f32[2,768,128]{2,1,0:T(8,128)} %convolution_bitcast_fusion.1) | copy-start | bytes 2359300
  137.4 0.7 copy-start.9
  142.6 93.0 %reduce-scatter.5.cloned.1.call-start = ((), (), s32[]{:S(2)}) async-start(), calls=%async_computation.9 | async-start | bytes 7077888 | tf_op jit(solution)/shard_map/reduce_scatter | solution.py:95
  142.8 12.5 %slice-start = ((s8[6291456]{0:T(1024)(128)(4,1)}), s8[4194304]{0:T(1024)(128)(4,1)S(1)}, s32[]{:S(2)}) async-start(s8[6291456]{0:T(1024)(128)(4,1)} %bitcast.81), calls=%async_computation.10 | async-start | bytes 8388608
  148.5 6.8 %slice-start.1 = ((s8[6291456]{0:T(1024)(128)(4,1)}), s8[2097152]{0:T(1024)(128)(4,1)S(1)}, s32[]{:S(2)}) async-start(s8[6291456]{0:T(1024)(128)(4,1)} %bitcast.81), calls=%async_computation.11 | async-start | bytes 4194304
  159.3 1.8 copy-start.3
  159.3 1.8 copy-start.8
  165.6 84.7 %copy-start.15 = (s32[128,8]{0,1:T(8,128)S(1)}, s32[128,8]{0,1:T(8,128)}, u32[]{:S(2)}) copy-start(s32[128,8]{0,1:T(8,128)} %param.9) | copy-start | bytes 12292
  190.9 47.5 %all-to-all-start.1 = ((bf16[2,768,256]{2,0,1:T(2,128)(2,1)}), bf16[2,768,256]{2,0,1:T(2,128)(2,1)}, u32[]{:S(2)}, u32[]{:S(2)}) async-start(bf16[2,768,256]{2,0,1:T(2,128)(2,1)} %copy.51), calls=%async_computation.2 | async-start | bytes 1572864 | tf_op jit(solution)/shard_map/all_to_all | solution.py:97
  238.5 47.0 %copy-start.7 = (bf16[1536,128]{1,0:T(8,128)(2,1)S(1)}, bf16[1536,128]{1,0:T(8,128)(2,1)}, u32[]{:S(2)}) copy-start(bf16[1536,128]{1,0:T(8,128)(2,1)} %copy-done.6) | copy-start | bytes 1179652
  238.5 47.9 %all-to-all-start.3 = ((bf16[2,768,256]{2,0,1:T(2,128)(2,1)}), bf16[2,768,256]{2,0,1:T(2,128)(2,1)}, u32[]{:S(2)}, u32[]{:S(2)}) async-start(bf16[2,768,256]{2,0,1:T(2,128)(2,1)} %copy.59), calls=%async_computation.5 | async-start | bytes 1572864 | tf_op jit(solution)/shard_map/all_to_all | solution.py:98
  253.8 5.3 %copy-start.12 = (f32[128,256]{1,0:T(8,128)S(1)}, f32[128,256]{1,0:T(8,128)}, u32[]{:S(2)}) copy-start(f32[128,256]{1,0:T(8,128)} %convert_element_type.85) | copy-start | bytes 393220
  253.8 33.9 %copy-start.5 = (bf16[1536,128]{1,0:T(8,128)(2,1)S(1)}, bf16[1536,128]{1,0:T(8,128)(2,1)}, u32[]{:S(2)}) copy-start(bf16[1536,128]{1,0:T(8,128)(2,1)} %copy-done.4) | copy-start | bytes 1179652
Sparse Core Ops, SparseCore 0:
  45.4 40.3 all-gather.2
  88.2 43.4 all-gather.4
  142.7 45.1 reduce-scatter.2
  190.3 45.2 reduce-scatter.4

commit v4 on v3

--- a/solution.py
+++ b/solution.py
@@ -15,7 +15,7 @@
     return jnp.sum(before * onehot.astype(jnp.float32), axis=1).astype(jnp.int32)
 
 
-def local(tokens, cotangent, expert_ids, route_gates, gate_proj, up_proj, down_proj):
+def layer(tokens, cotangent, expert_ids, route_gates, gate_proj, up_proj, down_proj):
     groups = lax.axis_size("dp")
     shards = lax.axis_size("et")
     local_experts, features, units = gate_proj.shape
@@ -63,7 +63,12 @@
     sigmoid_gate = jax.nn.sigmoid(pre_gate)
     silu_gate = pre_gate * sigmoid_gate
     hidden = (silu_gate * pre_up).astype(jnp.bfloat16)
-    out_part = jnp.einsum("esf,efd->esd", hidden, down_proj, preferred_element_type=jnp.float32)
+    out_part = jnp.einsum(
+        "esf,efd->esd", hidden, down_proj, preferred_element_type=jnp.float32
+    ).astype(jnp.bfloat16)
+    pre_gate, pre_up, hidden = lax.optimization_barrier((pre_gate, pre_up, hidden))
+    sigmoid_gate = jax.nn.sigmoid(pre_gate)
+    silu_gate = pre_gate * sigmoid_gate
     grad_hidden = jnp.einsum(
         "jesd,efjd->esf", expert_cot, down_w, preferred_element_type=jnp.float32
     )
@@ -87,7 +92,7 @@
         "esf,edf->esd", grad_pre_up, up_proj, preferred_element_type=jnp.float32
     )
     out_sum = lax.psum_scatter(
-        out_part.astype(jnp.bfloat16), "et", scatter_dimension=2, tiled=True
+        out_part, "et", scatter_dimension=2, tiled=True
     )
     in_part, grad_gate_w, grad_up_w, grad_down = lax.optimization_barrier(
         (in_part.astype(jnp.bfloat16), grad_gate_w, grad_up_w, grad_down)
@@ -131,4 +136,4 @@
         P("dp", None, "et"),
         P("dp", "et", None),
     )
-    return jax.shard_map(local, mesh=mesh, in_specs=in_specs, out_specs=out_specs, check_vma=False)
+    return jax.shard_map(layer, mesh=mesh, in_specs=in_specs, out_specs=out_specs, check_vma=False)

time: 296 us -> 287 us (0.970)
  waiting for transfers between devices: 105 us -> 101 us
  matrix products: 46.7 us -> 43 us
    all_gather x2, waiting for transfers between devices: 48.6 us -> 44 us  [the longest x1 33.1 us: layer(): expert_cot = lax.all_gather(expert_cot_part, 'et', axis=0)]
    dot_general x15, matrix products: 46.1 us -> 42.5 us  [the longest x1 5.6 us: layer(): jnp.einsum('esf,jesd->efjd', hidden, expert_cot, preferred_element_type=j...]
  transfers between devices with their start and end apart: 6 -> 6, of which waited for: 4 -> 4; matrix products, arithmetic and copies ran while one was open for 17% -> 20% of each run, Pallas kernels for 0% -> 0%
where the time goes in v4:
time: 287 us
  waiting for transfers between devices  101 us (35%)
  blocking collectives  86 us (30%)
  matrix products  43 us (15%)
  starting transfers between devices  20.7 us (7%)
  local copies, waits for them, and re-layouts  20.2 us (7%)
  between operations  14.1 us (5%)
    reduce_scatter x1, waiting for transfers between devices, layer(): in_sum = lax.psum_scatter(in_part, 'et', scatter_dimension=2, tiled=True)  34.7 us
    all_to_all x1, blocking collectives, layer(): lax.all_to_all(picked.reshape(experts, capacity, width), 'dp', split_axis...  33.9 us
    all_gather x1, waiting for transfers between devices, layer(): expert_cot = lax.all_gather(expert_cot_part, 'et', axis=0)  33.1 us
    all_to_all x1, blocking collectives, layer(): lax.all_to_all(scaled.reshape(experts, capacity, width), 'dp', split_axis...  26.7 us
    psum x1, blocking collectives, layer(): grad_gates = lax.psum(gate_part, 'et')  25.5 us
    reduce_scatter x1, waiting for transfers between devices, layer(): out_sum = lax.psum_scatter(out_part, 'et', scatter_dimension=2, tiled=True)  22.1 us
    all_gather x1, waiting for transfers between devices, layer(): expert_in = lax.all_gather(expert_in_part, 'et', axis=0)  10.9 us
    all_to_all x1, starting transfers between devices, layer(): lax.all_to_all(in_sum, 'dp', split_axis=1, concat_axis=0, tiled=True)  10.2 us
  transfers between devices with their start and end apart: 6, of which 4 were waited for; matrix products, arithmetic and copies ran while one was open for 20% of the time, Pallas kernels for 0%

profile of v4, /device:TPU:2, one launch (start us, length us, event | category | flops | bytes accessed | tf_op | source)
XLA Modules:
  0.0 286.7 jit_solution(14367164278534399842)
XLA Ops:
  7.2 0.0 copy-start
  7.2 0.0 all-gather.3.cloned.1.call-start
  7.3 0.9 copy.48
  8.1 0.1 reshape.103
  8.2 0.0 copy-start.13
  8.2 0.6 fusion.15
  8.8 1.3 fusion.11
  10.1 0.0 copy-start.10
  10.1 0.3 convolution_convert_fusion.2
  10.5 33.9 %all_to_all.60 = bf16[64,24,256]{2,1,0:T(8,128)(2,1)S(1)} all-to-all(bf16[64,24,256]{2,1,0:T(8,128)(2,1)S(1)} %bitcast.93), channel_id=1, replica_groups=mesh['dp'=32,'et'=8] {'dp'}, dimensions={0} | all-to-all | bytes 1572864 | tf_op jit(solution)/shard_map/all_to_all | solution.py:49
  44.3 0.9 copy.50
  45.3 0.0 all-gather.3.cloned.1.call-update
  45.3 0.0 all-gather.5.cloned.1.call-start
  45.4 0.0 copy-done.13
  45.4 0.1 copy.49
  45.5 0.1 broadcast_in_dim.18
  45.6 1.2 fusion.8
  46.9 0.3 convolution_convert_fusion.1
  47.2 26.7 %all_to_all.61 = bf16[64,24,256]{2,1,0:T(8,128)(2,1)S(1)} all-to-all(bf16[64,24,256]{2,1,0:T(8,128)(2,1)S(1)} %bitcast.94), channel_id=1, replica_groups=mesh['dp'=32,'et'=8] {'dp'}, dimensions={0} | all-to-all | bytes 1572864 | tf_op jit(solution)/shard_map/all_to_all | solution.py:52
  73.9 0.9 copy.53
  74.8 0.0 all-gather.5.cloned.1.call-update
  74.8 0.0 reduce-scatter.3.cloned.1.call-start
  74.9 10.9 %all-gather.3.cloned.1.call-done = bf16[8,2,768,256]{3,2,0,1:T(8,128)(2,1)} async-done(((bf16[1,2,768,256]{3,2,0,1:T(8,128)(2,1)}), bf16[8,2,768,256]{3,2,0,1:T(8,128)(2,1)}) %all-gather.3.cloned.1.call-update) | async-done | bytes 6291472 | tf_op jit(solution)/shard_map/all_gather | solution.py:56
  85.8 0.0 copy-done.2
  85.8 4.7 %convolution_bitcast_fusion.2 = f32[2,768,128]{2,1,0:T(8,128)S(1)} fusion(bf16[8,2,768,256]{3,2,0,1:T(8,128)(2,1)} %all-gather.3.cloned.1.call-done, bf16[2,8,256,128]{3,2,1,0:T(8,128)(2,1)S(1)} %bitcast.86), kind=kOutput, calls=%fused_computation.17 | convolution fusion | flops 805306368 | bytes 8126464 | tf_op jit(solution)/shard_map/jesd,ejdf->esf/dot_general | solution.py:61
  90.5 0.0 copy-start.8
  90.5 0.0 copy-start.7
  90.6 2.7 multiply_convert_fusion.2
  93.2 0.7 copy-done.6
  94.0 4.4 %convolution_convert_fusion = bf16[2,768,2048]{2,1,0:T(8,128)(2,1)} fusion(bf16[2,768,128]{2,1,0:T(8,128)(2,1)S(1)} %get-tuple-element.15, bf16[2,128,2048]{2,1,0:T(8,128)(2,1)S(1)} %copy-done.7), kind=kOutput, calls=%fused_computation.4 | convolution fusion | flops 808452096 | bytes 7733248 | tf_op jit(solution)/shard_map/esf,efd->esd/dot_general | solution.py:66
  98.4 0.0 reduce-scatter.3.cloned.1.call-update
  98.4 0.2 reduce-scatter.5.cloned.1.call-start
  98.6 33.1 %all-gather.5.cloned.1.call-done = bf16[8,2,768,256]{3,2,0,1:T(8,128)(2,1)} async-done(((bf16[1,2,768,256]{3,2,0,1:T(8,128)(2,1)}), bf16[8,2,768,256]{3,2,0,1:T(8,128)(2,1)}) %all-gather.5.cloned.1.call-update) | async-done | bytes 6291472 | tf_op jit(solution)/shard_map/all_gather | solution.py:57
  131.7 5.6 %fusion.20 = f32[2,128,8,256]{1,3,2,0:T(8,128)S(1)} fusion(bf16[8,2,768,256]{3,2,0,1:T(8,128)(2,1)} %all-gather.5.cloned.1.call-done, bf16[2,768,128]{2,1,0:T(8,128)(2,1)} %copy-done.6), kind=kOutput, calls=%fused_computation.32 | convolution fusion | flops 805306368 | bytes 8781824 | tf_op jit(solution)/shard_map/esf,jesd->efjd/dot_general | solution.py:79
  137.3 0.0 slice-start.1
  137.3 5.5 %multiply_convert_fusion = (bf16[2,768,128]{2,1,0:T(8,128)(2,1)S(1)}, bf16[2,768,128]{2,1,0:T(8,128)(2,1)S(1)}) fusion(f32[2,768,128]{2,1,0:T(8,128)} %copy-done.8, f32[2,768,128]{2,1,0:T(8,128)} %get-tuple-element.13, bf16[8,2,768,256]{3,2,0,1:T(8,128)(2,1)} %all-gather.5.cloned.1.call-done, bf16[2,16,8,8,256]{4,3,2,1,0:T(8,128)(2,1)} %bitcast.97), kind=kOutput, calls=%fused_computation.26 | convolution fusion | flops 807862272 | bytes 9699328 | tf_op jit(solution)/shard_map/jesd,efjd->esf/dot_general | solution.py:72
  142.9 0.0 slice-done
  142.9 0.0 slice-done.1
  142.9 4.0 %fusion.22 = f32[2,8,256,128]{3,2,1,0:T(8,128)} fusion(bf16[8,2,768,256]{3,2,0,1:T(8,128)(2,1)S(1)} %bitcast.82, bf16[2,768,128]{2,1,0:T(8,128)(2,1)S(1)} %get-tuple-element.38), kind=kOutput, calls=%fused_computation.34 | convolution fusion | flops 805306368 | bytes 8781824 | tf_op jit(solution)/shard_map/jesd,esf->ejdf/dot_general | solution.py:85
  146.9 4.0 %fusion.24 = f32[2,8,256,128]{3,2,1,0:T(8,128)} fusion(bf16[8,2,768,256]{3,2,0,1:T(8,128)(2,1)S(1)} %bitcast.82, bf16[2,768,128]{2,1,0:T(8,128)(2,1)S(1)} %get-tuple-element.39), kind=kOutput, calls=%fused_computation.36 | convolution fusion | flops 805306368 | bytes 8781824 | tf_op jit(solution)/shard_map/jesd,esf->ejdf/dot_general | solution.py:82
  150.9 1.8 fusion.41
  152.7 4.7 %add_convert_fusion = bf16[2,768,2048]{2,1,0:T(8,128)(2,1)} fusion(f32[2,768,2048]{2,1,0:T(8,128)S(1)} %fusion.41, bf16[2,768,128]{2,1,0:T(8,128)(2,1)S(1)} %get-tuple-element.38, bf16[2,2048,128]{2,1,0:T(8,128)(2,1)S(1)} %copy-done), kind=kOutput, calls=%fused_computation.1 | convolution fusion | flops 811597824 | bytes 20316160 | tf_op jit(solution)/shard_map/esf,edf->esd/dot_general | solution.py:91
  157.4 0.0 reduce-scatter.5.cloned.1.call-update
  157.4 22.1 %reduce-scatter.3.cloned.1.call-done = bf16[2,768,256]{2,1,0:T(8,128)(2,1)} async-done(((bf16[2,768,2048]{2,1,0:T(8,128)(2,1)}), bf16[2,768,256]{2,1,0:T(8,128)(2,1)}) %reduce-scatter.3.cloned.1.call-update) | async-done | bytes 786448 | tf_op jit(solution)/shard_map/reduce_scatter | solution.py:94
  179.5 2.8 copy.51
  182.3 10.2 %all-to-all-start.1 = ((bf16[2,768,256]{2,0,1:T(2,128)(2,1)}), bf16[2,768,256]{2,0,1:T(2,128)(2,1)}, u32[]{:S(2)}, u32[]{:S(2)}) async-start(bf16[2,768,256]{2,0,1:T(2,128)(2,1)} %copy.51), calls=%async_computation.2 | async-start | bytes 1572864 | tf_op jit(solution)/shard_map/all_to_all | solution.py:102
  192.5 34.7 %reduce-scatter.5.cloned.1.call-done = bf16[2,768,256]{2,1,0:T(8,128)(2,1)} async-done(((bf16[2,768,2048]{2,1,0:T(8,128)(2,1)}), bf16[2,768,256]{2,1,0:T(8,128)(2,1)}) %reduce-scatter.5.cloned.1.call-update) | async-done | bytes 786448 | tf_op jit(solution)/shard_map/reduce_scatter | solution.py:100
  227.2 2.8 copy.59
  230.0 0.0 all-to-all-done.1
  230.0 10.2 %all-to-all-start.3 = ((bf16[2,768,256]{2,0,1:T(2,128)(2,1)}), bf16[2,768,256]{2,0,1:T(2,128)(2,1)}, u32[]{:S(2)}, u32[]{:S(2)}) async-start(bf16[2,768,256]{2,0,1:T(2,128)(2,1)} %copy.59), calls=%async_computation.5 | async-start | bytes 1572864 | tf_op jit(solution)/shard_map/all_to_all | solution.py:103
  240.3 1.5 convert_element_type.85
  241.8 0.7 copy.62
  242.5 0.9 mul.76
  243.5 1.8 copy.64
  245.3 1.3 copy.52
  246.6 3.9 %gather_fusion = bf16[1024,256]{1,0:T(8,128)(2,1)S(1)} fusion(bf16[1536,256]{1,0:T(8,128)(2,1)S(1)} %bitcast.83, s32[1024]{0:T(1024)S(1)} %broadcast_clamp_fusion), kind=kCustom, calls=%fused_computation | custom fusion | bytes 1052672 | tf_op jit(solution)/shard_map/gather | solution.py:113
  250.6 0.2 fusion.18
  250.8 25.5 %psum.7 = f32[128,8]{1,0:T(8,128)S(1)} all-reduce(f32[128,8]{1,0:T(8,128)S(1)} %fusion.18), channel_id=1, replica_groups=mesh['dp'=32,'et'=8] {'et'}, use_global_device_ids=true, to_apply=%region_4.5 | all-reduce | flops 1024 | bytes 8192 | tf_op jit(solution)/shard_map/psum | solution.py:117
  276.3 0.7 copy.63
  277.0 1.0 convolution_convert_fusion.4
  277.9 0.0 all-to-all-done.3
  277.9 1.2 copy.60
  279.2 0.1 copy.61
  279.2 1.0 convolution_convert_fusion.3
  (29 shorter events, 0.1 us)
Async XLA Ops:
  7.2 83.3 %copy-start = (bf16[2,2048,128]{2,1,0:T(8,128)(2,1)S(1)}, bf16[2,2048,128]{2,1,0:T(8,128)(2,1)}, u32[]{:S(2)}) copy-start(bf16[2,2048,128]{2,1,0:T(8,128)(2,1)} %param.12) | copy-start | bytes 3145732
  7.2 2.9 %copy-start.11 = (bf16[128,256]{1,0:T(8,128)(2,1)S(1)}, bf16[128,256]{1,0:T(8,128)(2,1)}, u32[]{:S(2)}) copy-start(bf16[128,256]{1,0:T(8,128)(2,1)} %param.7) | copy-start | bytes 196612
  7.2 78.6 %all-gather.3.cloned.1.call-start = ((), (), s32[]{:S(2)}) async-start(), calls=%async_computation.6 | async-start | bytes 7077888 | tf_op jit(solution)/shard_map/all_gather | solution.py:56
  8.2 37.1 %copy-start.13 = (bf16[128,8]{0,1:T(8,128)(2,1)S(1)}, bf16[128,8]{0,1:T(8,128)(2,1)}, u32[]{:S(2)}) copy-start(bf16[128,8]{0,1:T(8,128)(2,1)} %param.10) | copy-start | bytes 6148
  10.1 36.7 %copy-start.10 = (bf16[128,256]{1,0:T(8,128)(2,1)S(1)}, bf16[128,256]{1,0:T(8,128)(2,1)}, u32[]{:S(2)}) copy-start(bf16[128,256]{1,0:T(8,128)(2,1)} %param.8) | copy-start | bytes 196612
  45.3 40.5 %copy-start.2 = (bf16[2,2048,128]{2,1,0:T(8,128)(2,1)S(1)}, bf16[2,2048,128]{2,1,0:T(8,128)(2,1)}, u32[]{:S(2)}) copy-start(bf16[2,2048,128]{2,1,0:T(8,128)(2,1)} %param.11) | copy-start | bytes 3145732
  45.3 86.4 %all-gather.5.cloned.1.call-start = ((), (), s32[]{:S(2)}) async-start(), calls=%async_computation.8 | async-start | bytes 7077888 | tf_op jit(solution)/shard_map/all_gather | solution.py:57
  46.9 43.6 %copy-start.4 = (bf16[1536,128]{1,0:T(8,128)(2,1)}, bf16[1536,128]{1,0:T(8,128)(2,1)S(1)}, u32[]{:S(2)}) copy-start(bf16[1536,128]{1,0:T(8,128)(2,1)S(1)} %fusion.8) | copy-start | bytes 1179652
  74.8 104.6 %reduce-scatter.3.cloned.1.call-start = ((), (), s32[]{:S(2)}) async-start(), calls=%async_computation.7 | async-start | bytes 7077888 | tf_op jit(solution)/shard_map/reduce_scatter | solution.py:94
  85.8 4.8 %copy-start.1 = (bf16[8,2,768,256]{3,2,0,1:T(8,128)(2,1)S(1)}, bf16[8,2,768,256]{3,2,0,1:T(8,128)(2,1)}, u32[]{:S(2)}) copy-start(bf16[8,2,768,256]{3,2,0,1:T(8,128)(2,1)} %all-gather.3.cloned.1.call-done) | copy-start | bytes 18874372
  90.5 2.7 copy-start.8
  90.5 3.4 %copy-start.7 = (bf16[2,128,2048]{2,1,0:T(8,128)(2,1)S(1)}, bf16[2,128,2048]{2,1,0:T(8,128)(2,1)}, u32[]{:S(2)}) copy-start(bf16[2,128,2048]{2,1,0:T(8,128)(2,1)} %param.13) | copy-start | bytes 3145732
  93.2 0.7 copy-start.6
  98.4 128.8 %reduce-scatter.5.cloned.1.call-start = ((), (), s32[]{:S(2)}) async-start(), calls=%async_computation.9 | async-start | bytes 7077888 | tf_op jit(solution)/shard_map/reduce_scatter | solution.py:100
  131.7 11.2 %slice-start = ((s8[6291456]{0:T(1024)(128)(4,1)}), s8[4194304]{0:T(1024)(128)(4,1)S(1)}, s32[]{:S(2)}) async-start(s8[6291456]{0:T(1024)(128)(4,1)} %bitcast.81), calls=%async_computation.10 | async-start | bytes 8388608
  137.3 5.6 %slice-start.1 = ((s8[6291456]{0:T(1024)(128)(4,1)}), s8[2097152]{0:T(1024)(128)(4,1)S(1)}, s32[]{:S(2)}) async-start(s8[6291456]{0:T(1024)(128)(4,1)} %bitcast.81), calls=%async_computation.11 | async-start | bytes 4194304
  146.9 4.0 %copy-start.3 = (bf16[2,2048,128]{2,1,0:T(8,128)(2,1)S(1)}, bf16[2,2048,128]{2,1,0:T(8,128)(2,1)}, u32[]{:S(2)}) copy-start(bf16[2,2048,128]{2,1,0:T(8,128)(2,1)} %param.11) | copy-start | bytes 3145732
  157.4 84.4 %copy-start.12 = (s32[128,8]{0,1:T(8,128)S(1)}, s32[128,8]{0,1:T(8,128)}, u32[]{:S(2)}) copy-start(s32[128,8]{0,1:T(8,128)} %param.9) | copy-start | bytes 12292
  182.3 47.8 %all-to-all-start.1 = ((bf16[2,768,256]{2,0,1:T(2,128)(2,1)}), bf16[2,768,256]{2,0,1:T(2,128)(2,1)}, u32[]{:S(2)}, u32[]{:S(2)}) async-start(bf16[2,768,256]{2,0,1:T(2,128)(2,1)} %copy.51), calls=%async_computation.2 | async-start | bytes 1572864 | tf_op jit(solution)/shard_map/all_to_all | solution.py:102
  230.0 47.9 %all-to-all-start.3 = ((bf16[2,768,256]{2,0,1:T(2,128)(2,1)}), bf16[2,768,256]{2,0,1:T(2,128)(2,1)}, u32[]{:S(2)}, u32[]{:S(2)}) async-start(bf16[2,768,256]{2,0,1:T(2,128)(2,1)} %copy.59), calls=%async_computation.5 | async-start | bytes 1572864 | tf_op jit(solution)/shard_map/all_to_all | solution.py:103
  245.3 5.3 %copy-start.9 = (f32[128,256]{1,0:T(8,128)S(1)}, f32[128,256]{1,0:T(8,128)}, u32[]{:S(2)}) copy-start(f32[128,256]{1,0:T(8,128)} %convert_element_type.85) | copy-start | bytes 393220
  245.3 31.7 %copy-start.5 = (bf16[1536,128]{1,0:T(8,128)(2,1)S(1)}, bf16[1536,128]{1,0:T(8,128)(2,1)}, u32[]{:S(2)}) copy-start(bf16[1536,128]{1,0:T(8,128)(2,1)} %copy-done.4) | copy-start | bytes 1179652
Sparse Core Ops, SparseCore 0:
  45.4 40.3 all-gather.2
  88.2 43.4 all-gather.4
  134.3 45.1 reduce-scatter.2
  181.9 45.2 reduce-scatter.4

commit v5 on v4

--- a/solution.py
+++ b/solution.py
@@ -98,10 +98,8 @@
         (in_part.astype(jnp.bfloat16), grad_gate_w, grad_up_w, grad_down)
     )
     in_sum = lax.psum_scatter(in_part, "et", scatter_dimension=2, tiled=True)
-    back_out, back_grad = (
-        lax.all_to_all(out_sum, "dp", split_axis=1, concat_axis=0, tiled=True),
-        lax.all_to_all(in_sum, "dp", split_axis=1, concat_axis=0, tiled=True),
-    )
+    back_out = lax.all_to_all(out_sum, "dp", split_axis=1, concat_axis=0, tiled=True)
+    back_grad = lax.all_to_all(in_sum, "dp", split_axis=1, concat_axis=0, tiled=True)
     back_out = back_out.reshape(slots, width)
     back_grad = back_grad.reshape(slots, width)
     mixed = jnp.einsum(

time: 287 us -> 287 us (level)
  no operation moved by 1% of the time
where the time goes in v5:
time: 287 us
  waiting for transfers between devices  101 us (35%)
  blocking collectives  86 us (30%)
  matrix products  43 us (15%)
  starting transfers between devices  20.7 us (7%)
  local copies, waits for them, and re-layouts  20.2 us (7%)
  between operations  14.1 us (5%)
    reduce_scatter x1, waiting for transfers between devices, layer(): in_sum = lax.psum_scatter(in_part, 'et', scatter_dimension=2, tiled=True)  34.7 us
    all_to_all x1, blocking collectives, layer(): lax.all_to_all(picked.reshape(experts, capacity, width), 'dp', split_axis...  33.9 us
    all_gather x1, waiting for transfers between devices, layer(): expert_cot = lax.all_gather(expert_cot_part, 'et', axis=0)  33.1 us
    all_to_all x1, blocking collectives, layer(): lax.all_to_all(scaled.reshape(experts, capacity, width), 'dp', split_axis...  26.7 us
    psum x1, blocking collectives, layer(): grad_gates = lax.psum(gate_part, 'et')  25.5 us
    reduce_scatter x1, waiting for transfers between devices, layer(): out_sum = lax.psum_scatter(out_part, 'et', scatter_dimension=2, tiled=True)  22.1 us
    all_gather x1, waiting for transfers between devices, layer(): expert_in = lax.all_gather(expert_in_part, 'et', axis=0)  10.9 us
    all_to_all x1, starting transfers between devices, layer(): lax.all_to_all(in_sum, 'dp', split_axis=1, concat_axis=0, tiled=True)  10.2 us
  transfers between devices with their start and end apart: 6, of which 4 were waited for; matrix products, arithmetic and copies ran while one was open for 20% of the time, Pallas kernels for 0%

profile of v5, /device:TPU:2, one launch (start us, length us, event | category | flops | bytes accessed | tf_op | source)
XLA Modules:
  0.0 286.7 jit_solution(14367164278534399842)
XLA Ops:
  7.2 0.0 copy-start
  7.2 0.0 all-gather.3.cloned.1.call-start
  7.3 0.9 copy.48
  8.1 0.1 reshape.103
  8.2 0.0 copy-start.13
  8.2 0.6 fusion.15
  8.8 1.3 fusion.11
  10.1 0.0 copy-start.10
  10.1 0.3 convolution_convert_fusion.2
  10.5 33.9 %all_to_all.60 = bf16[64,24,256]{2,1,0:T(8,128)(2,1)S(1)} all-to-all(bf16[64,24,256]{2,1,0:T(8,128)(2,1)S(1)} %bitcast.93), channel_id=1, replica_groups=mesh['dp'=32,'et'=8] {'dp'}, dimensions={0} | all-to-all | bytes 1572864 | tf_op jit(solution)/shard_map/all_to_all | solution.py:49
  44.3 0.9 copy.50
  45.3 0.0 all-gather.3.cloned.1.call-update
  45.3 0.0 all-gather.5.cloned.1.call-start
  45.4 0.0 copy-done.13
  45.4 0.1 copy.49
  45.5 0.1 broadcast_in_dim.18
  45.6 1.2 fusion.8
  46.9 0.3 convolution_convert_fusion.1
  47.2 26.7 %all_to_all.61 = bf16[64,24,256]{2,1,0:T(8,128)(2,1)S(1)} all-to-all(bf16[64,24,256]{2,1,0:T(8,128)(2,1)S(1)} %bitcast.94), channel_id=1, replica_groups=mesh['dp'=32,'et'=8] {'dp'}, dimensions={0} | all-to-all | bytes 1572864 | tf_op jit(solution)/shard_map/all_to_all | solution.py:52
  73.9 0.9 copy.53
  74.8 0.0 all-gather.5.cloned.1.call-update
  74.8 0.0 reduce-scatter.3.cloned.1.call-start
  74.9 10.9 %all-gather.3.cloned.1.call-done = bf16[8,2,768,256]{3,2,0,1:T(8,128)(2,1)} async-done(((bf16[1,2,768,256]{3,2,0,1:T(8,128)(2,1)}), bf16[8,2,768,256]{3,2,0,1:T(8,128)(2,1)}) %all-gather.3.cloned.1.call-update) | async-done | bytes 6291472 | tf_op jit(solution)/shard_map/all_gather | solution.py:56
  85.8 0.0 copy-done.2
  85.8 4.7 %convolution_bitcast_fusion.2 = f32[2,768,128]{2,1,0:T(8,128)S(1)} fusion(bf16[8,2,768,256]{3,2,0,1:T(8,128)(2,1)} %all-gather.3.cloned.1.call-done, bf16[2,8,256,128]{3,2,1,0:T(8,128)(2,1)S(1)} %bitcast.86), kind=kOutput, calls=%fused_computation.17 | convolution fusion | flops 805306368 | bytes 8126464 | tf_op jit(solution)/shard_map/jesd,ejdf->esf/dot_general | solution.py:61
  90.5 0.0 copy-start.8
  90.5 0.0 copy-start.7
  90.6 2.7 multiply_convert_fusion.2
  93.2 0.7 copy-done.6
  94.0 4.4 %convolution_convert_fusion = bf16[2,768,2048]{2,1,0:T(8,128)(2,1)} fusion(bf16[2,768,128]{2,1,0:T(8,128)(2,1)S(1)} %get-tuple-element.15, bf16[2,128,2048]{2,1,0:T(8,128)(2,1)S(1)} %copy-done.7), kind=kOutput, calls=%fused_computation.4 | convolution fusion | flops 808452096 | bytes 7733248 | tf_op jit(solution)/shard_map/esf,efd->esd/dot_general | solution.py:66
  98.4 0.0 reduce-scatter.3.cloned.1.call-update
  98.4 0.2 reduce-scatter.5.cloned.1.call-start
  98.6 33.1 %all-gather.5.cloned.1.call-done = bf16[8,2,768,256]{3,2,0,1:T(8,128)(2,1)} async-done(((bf16[1,2,768,256]{3,2,0,1:T(8,128)(2,1)}), bf16[8,2,768,256]{3,2,0,1:T(8,128)(2,1)}) %all-gather.5.cloned.1.call-update) | async-done | bytes 6291472 | tf_op jit(solution)/shard_map/all_gather | solution.py:57
  131.7 5.6 %fusion.20 = f32[2,128,8,256]{1,3,2,0:T(8,128)S(1)} fusion(bf16[8,2,768,256]{3,2,0,1:T(8,128)(2,1)} %all-gather.5.cloned.1.call-done, bf16[2,768,128]{2,1,0:T(8,128)(2,1)} %copy-done.6), kind=kOutput, calls=%fused_computation.32 | convolution fusion | flops 805306368 | bytes 8781824 | tf_op jit(solution)/shard_map/esf,jesd->efjd/dot_general | solution.py:79
  137.3 0.0 slice-start.1
  137.3 5.5 %multiply_convert_fusion = (bf16[2,768,128]{2,1,0:T(8,128)(2,1)S(1)}, bf16[2,768,128]{2,1,0:T(8,128)(2,1)S(1)}) fusion(f32[2,768,128]{2,1,0:T(8,128)} %copy-done.8, f32[2,768,128]{2,1,0:T(8,128)} %get-tuple-element.13, bf16[8,2,768,256]{3,2,0,1:T(8,128)(2,1)} %all-gather.5.cloned.1.call-done, bf16[2,16,8,8,256]{4,3,2,1,0:T(8,128)(2,1)} %bitcast.97), kind=kOutput, calls=%fused_computation.26 | convolution fusion | flops 807862272 | bytes 9699328 | tf_op jit(solution)/shard_map/jesd,efjd->esf/dot_general | solution.py:72
  142.9 0.0 slice-done
  142.9 0.0 slice-done.1
  142.9 4.0 %fusion.22 = f32[2,8,256,128]{3,2,1,0:T(8,128)} fusion(bf16[8,2,768,256]{3,2,0,1:T(8,128)(2,1)S(1)} %bitcast.82, bf16[2,768,128]{2,1,0:T(8,128)(2,1)S(1)} %get-tuple-element.38), kind=kOutput, calls=%fused_computation.34 | convolution fusion | flops 805306368 | bytes 8781824 | tf_op jit(solution)/shard_map/jesd,esf->ejdf/dot_general | solution.py:85
  146.9 4.0 %fusion.24 = f32[2,8,256,128]{3,2,1,0:T(8,128)} fusion(bf16[8,2,768,256]{3,2,0,1:T(8,128)(2,1)S(1)} %bitcast.82, bf16[2,768,128]{2,1,0:T(8,128)(2,1)S(1)} %get-tuple-element.39), kind=kOutput, calls=%fused_computation.36 | convolution fusion | flops 805306368 | bytes 8781824 | tf_op jit(solution)/shard_map/jesd,esf->ejdf/dot_general | solution.py:82
  150.9 1.8 fusion.41
  152.7 4.7 %add_convert_fusion = bf16[2,768,2048]{2,1,0:T(8,128)(2,1)} fusion(f32[2,768,2048]{2,1,0:T(8,128)S(1)} %fusion.41, bf16[2,768,128]{2,1,0:T(8,128)(2,1)S(1)} %get-tuple-element.38, bf16[2,2048,128]{2,1,0:T(8,128)(2,1)S(1)} %copy-done), kind=kOutput, calls=%fused_computation.1 | convolution fusion | flops 811597824 | bytes 20316160 | tf_op jit(solution)/shard_map/esf,edf->esd/dot_general | solution.py:91
  157.4 0.0 reduce-scatter.5.cloned.1.call-update
  157.4 22.1 %reduce-scatter.3.cloned.1.call-done = bf16[2,768,256]{2,1,0:T(8,128)(2,1)} async-done(((bf16[2,768,2048]{2,1,0:T(8,128)(2,1)}), bf16[2,768,256]{2,1,0:T(8,128)(2,1)}) %reduce-scatter.3.cloned.1.call-update) | async-done | bytes 786448 | tf_op jit(solution)/shard_map/reduce_scatter | solution.py:94
  179.5 2.8 copy.51
  182.3 10.2 %all-to-all-start.1 = ((bf16[2,768,256]{2,0,1:T(2,128)(2,1)}), bf16[2,768,256]{2,0,1:T(2,128)(2,1)}, u32[]{:S(2)}, u32[]{:S(2)}) async-start(bf16[2,768,256]{2,0,1:T(2,128)(2,1)} %copy.51), calls=%async_computation.2 | async-start | bytes 1572864 | tf_op jit(solution)/shard_map/all_to_all | solution.py:101
  192.5 34.7 %reduce-scatter.5.cloned.1.call-done = bf16[2,768,256]{2,1,0:T(8,128)(2,1)} async-done(((bf16[2,768,2048]{2,1,0:T(8,128)(2,1)}), bf16[2,768,256]{2,1,0:T(8,128)(2,1)}) %reduce-scatter.5.cloned.1.call-update) | async-done | bytes 786448 | tf_op jit(solution)/shard_map/reduce_scatter | solution.py:100
  227.2 2.8 copy.59
  230.0 0.0 all-to-all-done.1
  230.0 10.2 %all-to-all-start.3 = ((bf16[2,768,256]{2,0,1:T(2,128)(2,1)}), bf16[2,768,256]{2,0,1:T(2,128)(2,1)}, u32[]{:S(2)}, u32[]{:S(2)}) async-start(bf16[2,768,256]{2,0,1:T(2,128)(2,1)} %copy.59), calls=%async_computation.5 | async-start | bytes 1572864 | tf_op jit(solution)/shard_map/all_to_all | solution.py:102
  240.3 1.5 convert_element_type.85
  241.8 0.7 copy.62
  242.5 0.9 mul.76
  243.5 1.8 copy.64
  245.3 1.3 copy.52
  246.6 3.9 %gather_fusion = bf16[1024,256]{1,0:T(8,128)(2,1)S(1)} fusion(bf16[1536,256]{1,0:T(8,128)(2,1)S(1)} %bitcast.83, s32[1024]{0:T(1024)S(1)} %broadcast_clamp_fusion), kind=kCustom, calls=%fused_computation | custom fusion | bytes 1052672 | tf_op jit(solution)/shard_map/gather | solution.py:111
  250.6 0.2 fusion.18
  250.8 25.5 %psum.7 = f32[128,8]{1,0:T(8,128)S(1)} all-reduce(f32[128,8]{1,0:T(8,128)S(1)} %fusion.18), channel_id=1, replica_groups=mesh['dp'=32,'et'=8] {'et'}, use_global_device_ids=true, to_apply=%region_4.5 | all-reduce | flops 1024 | bytes 8192 | tf_op jit(solution)/shard_map/psum | solution.py:115
  276.3 0.7 copy.63
  277.0 1.0 convolution_convert_fusion.4
  277.9 0.0 all-to-all-done.3
  277.9 1.2 copy.60
  279.2 0.1 copy.61
  279.2 1.0 convolution_convert_fusion.3
  (29 shorter events, 0.1 us)
Async XLA Ops:
  7.2 83.3 %copy-start = (bf16[2,2048,128]{2,1,0:T(8,128)(2,1)S(1)}, bf16[2,2048,128]{2,1,0:T(8,128)(2,1)}, u32[]{:S(2)}) copy-start(bf16[2,2048,128]{2,1,0:T(8,128)(2,1)} %param.12) | copy-start | bytes 3145732
  7.2 2.9 %copy-start.11 = (bf16[128,256]{1,0:T(8,128)(2,1)S(1)}, bf16[128,256]{1,0:T(8,128)(2,1)}, u32[]{:S(2)}) copy-start(bf16[128,256]{1,0:T(8,128)(2,1)} %param.7) | copy-start | bytes 196612
  7.2 78.6 %all-gather.3.cloned.1.call-start = ((), (), s32[]{:S(2)}) async-start(), calls=%async_computation.6 | async-start | bytes 7077888 | tf_op jit(solution)/shard_map/all_gather | solution.py:56
  8.2 37.1 %copy-start.13 = (bf16[128,8]{0,1:T(8,128)(2,1)S(1)}, bf16[128,8]{0,1:T(8,128)(2,1)}, u32[]{:S(2)}) copy-start(bf16[128,8]{0,1:T(8,128)(2,1)} %param.10) | copy-start | bytes 6148
  10.1 36.7 %copy-start.10 = (bf16[128,256]{1,0:T(8,128)(2,1)S(1)}, bf16[128,256]{1,0:T(8,128)(2,1)}, u32[]{:S(2)}) copy-start(bf16[128,256]{1,0:T(8,128)(2,1)} %param.8) | copy-start | bytes 196612
  45.3 40.5 %copy-start.2 = (bf16[2,2048,128]{2,1,0:T(8,128)(2,1)S(1)}, bf16[2,2048,128]{2,1,0:T(8,128)(2,1)}, u32[]{:S(2)}) copy-start(bf16[2,2048,128]{2,1,0:T(8,128)(2,1)} %param.11) | copy-start | bytes 3145732
  45.3 86.4 %all-gather.5.cloned.1.call-start = ((), (), s32[]{:S(2)}) async-start(), calls=%async_computation.8 | async-start | bytes 7077888 | tf_op jit(solution)/shard_map/all_gather | solution.py:57
  46.9 43.6 %copy-start.4 = (bf16[1536,128]{1,0:T(8,128)(2,1)}, bf16[1536,128]{1,0:T(8,128)(2,1)S(1)}, u32[]{:S(2)}) copy-start(bf16[1536,128]{1,0:T(8,128)(2,1)S(1)} %fusion.8) | copy-start | bytes 1179652
  74.8 104.6 %reduce-scatter.3.cloned.1.call-start = ((), (), s32[]{:S(2)}) async-start(), calls=%async_computation.7 | async-start | bytes 7077888 | tf_op jit(solution)/shard_map/reduce_scatter | solution.py:94
  85.8 4.8 %copy-start.1 = (bf16[8,2,768,256]{3,2,0,1:T(8,128)(2,1)S(1)}, bf16[8,2,768,256]{3,2,0,1:T(8,128)(2,1)}, u32[]{:S(2)}) copy-start(bf16[8,2,768,256]{3,2,0,1:T(8,128)(2,1)} %all-gather.3.cloned.1.call-done) | copy-start | bytes 18874372
  90.5 2.7 copy-start.8
  90.5 3.4 %copy-start.7 = (bf16[2,128,2048]{2,1,0:T(8,128)(2,1)S(1)}, bf16[2,128,2048]{2,1,0:T(8,128)(2,1)}, u32[]{:S(2)}) copy-start(bf16[2,128,2048]{2,1,0:T(8,128)(2,1)} %param.13) | copy-start | bytes 3145732
  93.2 0.7 copy-start.6
  98.4 128.8 %reduce-scatter.5.cloned.1.call-start = ((), (), s32[]{:S(2)}) async-start(), calls=%async_computation.9 | async-start | bytes 7077888 | tf_op jit(solution)/shard_map/reduce_scatter | solution.py:100
  131.7 11.2 %slice-start = ((s8[6291456]{0:T(1024)(128)(4,1)}), s8[4194304]{0:T(1024)(128)(4,1)S(1)}, s32[]{:S(2)}) async-start(s8[6291456]{0:T(1024)(128)(4,1)} %bitcast.81), calls=%async_computation.10 | async-start | bytes 8388608
  137.3 5.6 %slice-start.1 = ((s8[6291456]{0:T(1024)(128)(4,1)}), s8[2097152]{0:T(1024)(128)(4,1)S(1)}, s32[]{:S(2)}) async-start(s8[6291456]{0:T(1024)(128)(4,1)} %bitcast.81), calls=%async_computation.11 | async-start | bytes 4194304
  146.9 4.0 %copy-start.3 = (bf16[2,2048,128]{2,1,0:T(8,128)(2,1)S(1)}, bf16[2,2048,128]{2,1,0:T(8,128)(2,1)}, u32[]{:S(2)}) copy-start(bf16[2,2048,128]{2,1,0:T(8,128)(2,1)} %param.11) | copy-start | bytes 3145732
  157.4 84.4 %copy-start.12 = (s32[128,8]{0,1:T(8,128)S(1)}, s32[128,8]{0,1:T(8,128)}, u32[]{:S(2)}) copy-start(s32[128,8]{0,1:T(8,128)} %param.9) | copy-start | bytes 12292
  182.3 47.8 %all-to-all-start.1 = ((bf16[2,768,256]{2,0,1:T(2,128)(2,1)}), bf16[2,768,256]{2,0,1:T(2,128)(2,1)}, u32[]{:S(2)}, u32[]{:S(2)}) async-start(bf16[2,768,256]{2,0,1:T(2,128)(2,1)} %copy.51), calls=%async_computation.2 | async-start | bytes 1572864 | tf_op jit(solution)/shard_map/all_to_all | solution.py:101
  230.0 47.9 %all-to-all-start.3 = ((bf16[2,768,256]{2,0,1:T(2,128)(2,1)}), bf16[2,768,256]{2,0,1:T(2,128)(2,1)}, u32[]{:S(2)}, u32[]{:S(2)}) async-start(bf16[2,768,256]{2,0,1:T(2,128)(2,1)} %copy.59), calls=%async_computation.5 | async-start | bytes 1572864 | tf_op jit(solution)/shard_map/all_to_all | solution.py:102
  245.3 5.3 %copy-start.9 = (f32[128,256]{1,0:T(8,128)S(1)}, f32[128,256]{1,0:T(8,128)}, u32[]{:S(2)}) copy-start(f32[128,256]{1,0:T(8,128)} %convert_element_type.85) | copy-start | bytes 393220
  245.3 31.7 %copy-start.5 = (bf16[1536,128]{1,0:T(8,128)(2,1)S(1)}, bf16[1536,128]{1,0:T(8,128)(2,1)}, u32[]{:S(2)}) copy-start(bf16[1536,128]{1,0:T(8,128)(2,1)} %copy-done.4) | copy-start | bytes 1179652
Sparse Core Ops, SparseCore 0:
  45.4 40.3 all-gather.2
  88.2 43.4 all-gather.4
  134.3 45.1 reduce-scatter.2
  181.9 45.2 reduce-scatter.4

commit v6 on v5

--- a/solution.py
+++ b/solution.py
@@ -112,7 +112,12 @@
         jnp.float32
     )
     gate_part = jnp.sum(cotangent.astype(jnp.float32)[:, None, :] * out_rows, axis=2)
-    grad_gates = lax.psum(gate_part, "et")
+    grad_gates = gate_part
+    step = 1
+    while step < shards:
+        swap = [(i, i ^ step) for i in range(shards)]
+        grad_gates = grad_gates + lax.ppermute(grad_gates, "et", swap)
+        step *= 2
     return (mixed, grad_tokens, grad_gates, grad_gate_w, grad_up_w, grad_down)
 
 

time: 287 us -> 275 us (0.958)
  blocking collectives: 86 us -> 60.5 us
  waiting for transfers between devices: 101 us -> 113 us
  local copies, waits for them, and re-layouts: 20.2 us -> 16.7 us
    psum x1 -> x0, blocking collectives: 25.5 us -> none  [layer(): grad_gates = lax.psum(gate_part, 'et')]
    all_to_all x1, waiting for transfers between devices: 0.01 us -> 9.25 us  [layer(): lax.all_to_all(in_sum, 'dp', split_axis=1, concat_axis=0, tiled=True)]
  transfers between devices with their start and end apart: 6 -> 9, of which waited for: 4 -> 6; matrix products, arithmetic and copies ran while one was open for 20% -> 22% of each run, Pallas kernels for 0% -> 0%
where the time goes in v6:
time: 275 us
  waiting for transfers between devices  113 us (41%)
  blocking collectives  60.5 us (22%)
  matrix products  44.6 us (16%)
  starting transfers between devices  23.1 us (8%)
  local copies, waits for them, and re-layouts  16.7 us (6%)
  between operations  14.1 us (5%)
  other arithmetic  3.33 us (1%)
    reduce_scatter x1, waiting for transfers between devices, layer(): in_sum = lax.psum_scatter(in_part, 'et', scatter_dimension=2, tiled=True)  34.5 us
    all_gather x1, waiting for transfers between devices, layer(): expert_cot = lax.all_gather(expert_cot_part, 'et', axis=0)  33.9 us
    all_to_all x1, blocking collectives, layer(): lax.all_to_all(picked.reshape(experts, capacity, width), 'dp', split_axis...  33.9 us
    all_to_all x1, blocking collectives, layer(): lax.all_to_all(scaled.reshape(experts, capacity, width), 'dp', split_axis...  26.7 us
    reduce_scatter x1, waiting for transfers between devices, layer(): out_sum = lax.psum_scatter(out_part, 'et', scatter_dimension=2, tiled=True)  21.5 us
    all_gather x1, waiting for transfers between devices, layer(): expert_in = lax.all_gather(expert_in_part, 'et', axis=0)  10.9 us
    all_to_all x1, starting transfers between devices, layer(): lax.all_to_all(out_sum, 'dp', split_axis=1, concat_axis=0, tiled=True)  10.1 us
    all_to_all x1, starting transfers between devices, layer(): lax.all_to_all(in_sum, 'dp', split_axis=1, concat_axis=0, tiled=True)  10 us
  transfers between devices with their start and end apart: 9, of which 6 were waited for; matrix products, arithmetic and copies ran while one was open for 22% of the time, Pallas kernels for 0%

profile of v6, /device:TPU:2, one launch (start us, length us, event | category | flops | bytes accessed | tf_op | source)
XLA Modules:
  0.0 274.9 jit_solution(17354827081399207850)
XLA Ops:
  7.2 0.0 copy-start
  7.2 0.0 all-gather.3.cloned.1.call-start
  7.3 0.9 copy.48
  8.1 0.1 reshape.103
  8.2 0.0 copy-start.13
  8.2 0.6 fusion.15
  8.8 1.3 fusion.11
  10.1 0.0 copy-start.9
  10.1 0.3 convolution_convert_fusion.2
  10.5 33.9 %all_to_all.60 = bf16[64,24,256]{2,1,0:T(8,128)(2,1)S(1)} all-to-all(bf16[64,24,256]{2,1,0:T(8,128)(2,1)S(1)} %bitcast.94), channel_id=1, replica_groups=mesh['dp'=32,'et'=8] {'dp'}, dimensions={0} | all-to-all | bytes 1572864 | tf_op jit(solution)/shard_map/all_to_all | solution.py:49
  44.4 0.9 copy.50
  45.3 0.0 all-gather.3.cloned.1.call-update
  45.3 0.0 all-gather.5.cloned.1.call-start
  45.4 0.1 copy.49
  45.5 0.1 broadcast_in_dim.18
  45.6 1.2 fusion.8
  46.9 0.3 convolution_convert_fusion.1
  47.2 26.7 %all_to_all.61 = bf16[64,24,256]{2,1,0:T(8,128)(2,1)S(1)} all-to-all(bf16[64,24,256]{2,1,0:T(8,128)(2,1)S(1)} %bitcast.95), channel_id=1, replica_groups=mesh['dp'=32,'et'=8] {'dp'}, dimensions={0} | all-to-all | bytes 1572864 | tf_op jit(solution)/shard_map/all_to_all | solution.py:52
  73.9 0.9 copy.53
  74.8 0.0 all-gather.5.cloned.1.call-update
  74.9 0.0 reduce-scatter.3.cloned.1.call-start
  74.9 10.9 %all-gather.3.cloned.1.call-done = bf16[8,2,768,256]{3,2,0,1:T(8,128)(2,1)} async-done(((bf16[1,2,768,256]{3,2,0,1:T(8,128)(2,1)}), bf16[8,2,768,256]{3,2,0,1:T(8,128)(2,1)}) %all-gather.3.cloned.1.call-update) | async-done | bytes 6291472 | tf_op jit(solution)/shard_map/all_gather | solution.py:56
  85.8 4.7 %convolution_bitcast_fusion.2 = f32[2,768,128]{2,1,0:T(8,128)S(1)} fusion(bf16[8,2,768,256]{3,2,0,1:T(8,128)(2,1)} %all-gather.3.cloned.1.call-done, bf16[2,8,256,128]{3,2,1,0:T(8,128)(2,1)S(1)} %bitcast.86), kind=kOutput, calls=%fused_computation.17 | convolution fusion | flops 805306368 | bytes 8126464 | tf_op jit(solution)/shard_map/jesd,ejdf->esf/dot_general | solution.py:61
  90.5 0.0 copy-start.7
  90.5 0.0 copy-start.6
  90.6 2.7 multiply_convert_fusion.2
  93.2 4.4 %convolution_convert_fusion = bf16[2,768,2048]{2,1,0:T(8,128)(2,1)} fusion(bf16[2,768,128]{2,1,0:T(8,128)(2,1)S(1)} %get-tuple-element.15, bf16[2,128,2048]{2,1,0:T(8,128)(2,1)S(1)} %copy-done.6), kind=kOutput, calls=%fused_computation.4 | convolution fusion | flops 808452096 | bytes 7733248 | tf_op jit(solution)/shard_map/esf,efd->esd/dot_general | solution.py:66
  97.6 0.0 reduce-scatter.3.cloned.1.call-update
  97.6 0.2 reduce-scatter.5.cloned.1.call-start
  97.9 33.9 %all-gather.5.cloned.1.call-done = bf16[8,2,768,256]{3,2,0,1:T(8,128)(2,1)} async-done(((bf16[1,2,768,256]{3,2,0,1:T(8,128)(2,1)}), bf16[8,2,768,256]{3,2,0,1:T(8,128)(2,1)}) %all-gather.5.cloned.1.call-update) | async-done | bytes 6291472 | tf_op jit(solution)/shard_map/all_gather | solution.py:57
  131.8 6.8 %fusion.20 = f32[2,128,8,256]{1,3,2,0:T(8,128)} fusion(bf16[8,2,768,256]{3,2,0,1:T(8,128)(2,1)} %all-gather.5.cloned.1.call-done, bf16[2,768,128]{2,1,0:T(8,128)(2,1)S(1)} %get-tuple-element.15), kind=kOutput, calls=%fused_computation.32 | convolution fusion | flops 805306368 | bytes 8781824 | tf_op jit(solution)/shard_map/esf,jesd->efjd/dot_general | solution.py:79
  138.6 4.9 %multiply_convert_fusion = (bf16[2,768,128]{2,1,0:T(8,128)(2,1)S(1)}, bf16[2,768,128]{2,1,0:T(8,128)(2,1)S(1)}) fusion(f32[2,768,128]{2,1,0:T(8,128)S(1)} %copy-done.8, f32[2,768,128]{2,1,0:T(8,128)S(1)} %copy-done.14, bf16[8,2,768,256]{3,2,0,1:T(8,128)(2,1)} %all-gather.5.cloned.1.call-done, bf16[2,16,8,8,256]{4,3,2,1,0:T(8,128)(2,1)S(1)} %bitcast.98), kind=kOutput, calls=%fused_computation.26 | convolution fusion | flops 807862272 | bytes 9699328 | tf_op jit(solution)/shard_map/jesd,efjd->esf/dot_general | solution.py:72
  143.5 4.0 %fusion.22 = f32[2,8,256,128]{3,2,1,0:T(8,128)} fusion(bf16[8,2,768,256]{3,2,0,1:T(8,128)(2,1)S(1)} %bitcast.82, bf16[2,768,128]{2,1,0:T(8,128)(2,1)S(1)} %get-tuple-element.38), kind=kOutput, calls=%fused_computation.34 | convolution fusion | flops 805306368 | bytes 8781824 | tf_op jit(solution)/shard_map/jesd,esf->ejdf/dot_general | solution.py:85
  147.4 4.0 %fusion.24 = f32[2,8,256,128]{3,2,1,0:T(8,128)} fusion(bf16[8,2,768,256]{3,2,0,1:T(8,128)(2,1)S(1)} %bitcast.82, bf16[2,768,128]{2,1,0:T(8,128)(2,1)S(1)} %get-tuple-element.39), kind=kOutput, calls=%fused_computation.36 | convolution fusion | flops 805306368 | bytes 8781824 | tf_op jit(solution)/shard_map/jesd,esf->ejdf/dot_general | solution.py:82
  151.4 1.8 fusion.41
  153.2 4.7 %add_convert_fusion = bf16[2,768,2048]{2,1,0:T(8,128)(2,1)} fusion(f32[2,768,2048]{2,1,0:T(8,128)S(1)} %fusion.41, bf16[2,768,128]{2,1,0:T(8,128)(2,1)S(1)} %get-tuple-element.38, bf16[2,2048,128]{2,1,0:T(8,128)(2,1)S(1)} %copy-done), kind=kOutput, calls=%fused_computation.1 | convolution fusion | flops 811597824 | bytes 20316160 | tf_op jit(solution)/shard_map/esf,edf->esd/dot_general | solution.py:91
  157.9 0.0 reduce-scatter.5.cloned.1.call-update
  157.9 21.5 %reduce-scatter.3.cloned.1.call-done = bf16[2,768,256]{2,1,0:T(8,128)(2,1)} async-done(((bf16[2,768,2048]{2,1,0:T(8,128)(2,1)}), bf16[2,768,256]{2,1,0:T(8,128)(2,1)}) %reduce-scatter.3.cloned.1.call-update) | async-done | bytes 786448 | tf_op jit(solution)/shard_map/reduce_scatter | solution.py:94
  179.5 2.8 %copy.51 = bf16[2,768,256]{2,0,1:T(2,128)(2,1)} copy(bf16[2,768,256]{2,1,0:T(8,128)(2,1)} %reduce-scatter.3.cloned.1.call-done) | data formatting | bytes 1572864 | tf_op jit(solution)/shard_map/reduce_scatter | solution.py:94
  182.3 10.1 %all-to-all-start.1 = ((bf16[2,768,256]{2,0,1:T(2,128)(2,1)}), bf16[2,768,256]{2,0,1:T(2,128)(2,1)S(1)}, u32[]{:S(2)}, u32[]{:S(2)}) async-start(bf16[2,768,256]{2,0,1:T(2,128)(2,1)} %copy.51), calls=%async_computation.2 | async-start | bytes 1572864 | tf_op jit(solution)/shard_map/all_to_all | solution.py:101
  192.4 34.5 %reduce-scatter.5.cloned.1.call-done = bf16[2,768,256]{2,1,0:T(8,128)(2,1)} async-done(((bf16[2,768,2048]{2,1,0:T(8,128)(2,1)}), bf16[2,768,256]{2,1,0:T(8,128)(2,1)}) %reduce-scatter.5.cloned.1.call-update) | async-done | bytes 786448 | tf_op jit(solution)/shard_map/reduce_scatter | solution.py:100
  227.0 2.8 %copy.59 = bf16[2,768,256]{2,0,1:T(2,128)(2,1)} copy(bf16[2,768,256]{2,1,0:T(8,128)(2,1)} %reduce-scatter.5.cloned.1.call-done) | data formatting | bytes 1572864 | tf_op jit(solution)/shard_map/reduce_scatter | solution.py:100
  229.8 0.0 all-to-all-done.1
  229.8 10.0 %all-to-all-start.3 = ((bf16[2,768,256]{2,0,1:T(2,128)(2,1)}), bf16[2,768,256]{2,0,1:T(2,128)(2,1)S(1)}, u32[]{:S(2)}, u32[]{:S(2)}) async-start(bf16[2,768,256]{2,0,1:T(2,128)(2,1)} %copy.59), calls=%async_computation.5 | async-start | bytes 1572864 | tf_op jit(solution)/shard_map/all_to_all | solution.py:102
  239.8 0.7 convert_element_type.85
  240.5 0.1 copy.62
  240.6 0.1 mul.76
  240.7 0.1 copy.52
  240.8 3.9 %gather_fusion = bf16[1024,256]{1,0:T(8,128)(2,1)S(1)} fusion(bf16[1536,256]{1,0:T(8,128)(2,1)S(1)} %bitcast.83, s32[1024]{0:T(1024)S(1)} %broadcast_clamp_fusion), kind=kCustom, calls=%fused_computation | custom fusion | bytes 1052672 | tf_op jit(solution)/shard_map/gather | solution.py:111
  244.8 1.8 fusion.18
  246.5 0.0 collective-permute-start
  246.6 2.9 %copy.64 = f32[2,128,2048]{2,1,0:T(8,128)} copy(f32[2,128,2048]{1,2,0:T(8,128)} %bitcast.85) | data formatting | bytes 4194304
  249.4 0.0 collective-permute-done
  249.4 0.8 add.63
  250.3 0.1 collective-permute-start.1
  250.4 2.0 convolution_convert_fusion.4
  252.3 9.3 %all-to-all-done.3 = bf16[2,768,256]{2,0,1:T(2,128)(2,1)S(1)} async-done(((bf16[2,768,256]{2,0,1:T(2,128)(2,1)}), bf16[2,768,256]{2,0,1:T(2,128)(2,1)S(1)}, u32[]{:S(2)}, u32[]{:S(2)}) %all-to-all-start.3) | async-done | bytes 786464 | tf_op jit(solution)/shard_map/all_to_all | solution.py:102
  261.6 0.1 copy.60
  261.7 0.1 copy.61
  261.8 0.0 collective-permute-done.1
  261.8 2.5 collective-permute-start.2
  264.3 1.0 convolution_convert_fusion.3
  265.3 2.4 collective-permute-done.2
  267.7 0.7 copy.63
  (39 shorter events, 0.1 us)
Async XLA Ops:
  7.2 83.4 %copy-start = (bf16[2,2048,128]{2,1,0:T(8,128)(2,1)S(1)}, bf16[2,2048,128]{2,1,0:T(8,128)(2,1)}, u32[]{:S(2)}) copy-start(bf16[2,2048,128]{2,1,0:T(8,128)(2,1)} %param.12) | copy-start | bytes 3145732
  7.2 2.9 %copy-start.11 = (bf16[128,256]{1,0:T(8,128)(2,1)S(1)}, bf16[128,256]{1,0:T(8,128)(2,1)}, u32[]{:S(2)}) copy-start(bf16[128,256]{1,0:T(8,128)(2,1)} %param.7) | copy-start | bytes 196612
  7.2 78.6 %all-gather.3.cloned.1.call-start = ((), (), s32[]{:S(2)}) async-start(), calls=%async_computation.6 | async-start | bytes 7077888 | tf_op jit(solution)/shard_map/all_gather | solution.py:56
  8.2 37.2 %copy-start.13 = (bf16[128,8]{0,1:T(8,128)(2,1)S(1)}, bf16[128,8]{0,1:T(8,128)(2,1)}, u32[]{:S(2)}) copy-start(bf16[128,8]{0,1:T(8,128)(2,1)} %param.10) | copy-start | bytes 6148
  10.1 35.2 %copy-start.3 = (bf16[1536,128]{1,0:T(8,128)(2,1)}, bf16[1536,128]{1,0:T(8,128)(2,1)S(1)}, u32[]{:S(2)}) copy-start(bf16[1536,128]{1,0:T(8,128)(2,1)S(1)} %fusion.11) | copy-start | bytes 1179652
  10.1 36.7 %copy-start.9 = (bf16[128,256]{1,0:T(8,128)(2,1)S(1)}, bf16[128,256]{1,0:T(8,128)(2,1)}, u32[]{:S(2)}) copy-start(bf16[128,256]{1,0:T(8,128)(2,1)} %param.8) | copy-start | bytes 196612
  45.3 40.5 %copy-start.2 = (bf16[2,2048,128]{2,1,0:T(8,128)(2,1)S(1)}, bf16[2,2048,128]{2,1,0:T(8,128)(2,1)}, u32[]{:S(2)}) copy-start(bf16[2,2048,128]{2,1,0:T(8,128)(2,1)} %param.11) | copy-start | bytes 3145732
  45.3 86.4 %all-gather.5.cloned.1.call-start = ((), (), s32[]{:S(2)}) async-start(), calls=%async_computation.8 | async-start | bytes 7077888 | tf_op jit(solution)/shard_map/all_gather | solution.py:57
  46.9 28.0 %copy-start.5 = (bf16[1536,128]{1,0:T(8,128)(2,1)}, bf16[1536,128]{1,0:T(8,128)(2,1)S(1)}, u32[]{:S(2)}) copy-start(bf16[1536,128]{1,0:T(8,128)(2,1)S(1)} %fusion.8) | copy-start | bytes 1179652
  74.9 104.6 %reduce-scatter.3.cloned.1.call-start = ((), (), s32[]{:S(2)}) async-start(), calls=%async_computation.7 | async-start | bytes 7077888 | tf_op jit(solution)/shard_map/reduce_scatter | solution.py:94
  85.8 4.8 %copy-start.1 = (bf16[8,2,768,256]{3,2,0,1:T(8,128)(2,1)S(1)}, bf16[8,2,768,256]{3,2,0,1:T(8,128)(2,1)}, u32[]{:S(2)}) copy-start(bf16[8,2,768,256]{3,2,0,1:T(8,128)(2,1)} %all-gather.3.cloned.1.call-done) | copy-start | bytes 18874372
  90.5 2.7 copy-start.7
  90.5 2.7 copy-start.6
  97.6 129.3 %reduce-scatter.5.cloned.1.call-start = ((), (), s32[]{:S(2)}) async-start(), calls=%async_computation.9 | async-start | bytes 7077888 | tf_op jit(solution)/shard_map/reduce_scatter | solution.py:100
  131.7 6.8 %copy-start.8 = (f32[2,768,128]{2,1,0:T(8,128)S(1)}, f32[2,768,128]{2,1,0:T(8,128)}, u32[]{:S(2)}) copy-start(f32[2,768,128]{2,1,0:T(8,128)} %copy-done.7) | copy-start | bytes 2359300
  131.7 6.8 %copy-start.14 = (f32[2,768,128]{2,1,0:T(8,128)S(1)}, f32[2,768,128]{2,1,0:T(8,128)}, u32[]{:S(2)}) copy-start(f32[2,768,128]{2,1,0:T(8,128)} %get-tuple-element.13) | copy-start | bytes 2359300
  131.7 11.7 %slice-start = ((s8[6291456]{0:T(1024)(128)(4,1)}), s8[4194304]{0:T(1024)(128)(4,1)S(1)}, s32[]{:S(2)}) async-start(s8[6291456]{0:T(1024)(128)(4,1)} %bitcast.81), calls=%async_computation.10 | async-start | bytes 8388608
  138.6 4.9 %slice-start.1 = ((s8[6291456]{0:T(1024)(128)(4,1)}), s8[2097152]{0:T(1024)(128)(4,1)S(1)}, s32[]{:S(2)}) async-start(s8[6291456]{0:T(1024)(128)(4,1)} %bitcast.81), calls=%async_computation.11 | async-start | bytes 4194304
  157.9 81.9 %copy-start.10 = (bf16[128,256]{1,0:T(8,128)(2,1)S(1)}, bf16[128,256]{1,0:T(8,128)(2,1)}, u32[]{:S(2)}) copy-start(bf16[128,256]{1,0:T(8,128)(2,1)} %param.8) | copy-start | bytes 196612
  157.9 82.6 %copy-start.12 = (s32[128,8]{0,1:T(8,128)S(1)}, s32[128,8]{0,1:T(8,128)}, u32[]{:S(2)}) copy-start(s32[128,8]{0,1:T(8,128)} %param.9) | copy-start | bytes 12292
  182.3 47.5 %all-to-all-start.1 = ((bf16[2,768,256]{2,0,1:T(2,128)(2,1)}), bf16[2,768,256]{2,0,1:T(2,128)(2,1)S(1)}, u32[]{:S(2)}, u32[]{:S(2)}) async-start(bf16[2,768,256]{2,0,1:T(2,128)(2,1)} %copy.51), calls=%async_computation.2 | async-start | bytes 1572864 | tf_op jit(solution)/shard_map/all_to_all | solution.py:101
  229.8 31.8 %all-to-all-start.3 = ((bf16[2,768,256]{2,0,1:T(2,128)(2,1)}), bf16[2,768,256]{2,0,1:T(2,128)(2,1)S(1)}, u32[]{:S(2)}, u32[]{:S(2)}) async-start(bf16[2,768,256]{2,0,1:T(2,128)(2,1)} %copy.59), calls=%async_computation.5 | async-start | bytes 1572864 | tf_op jit(solution)/shard_map/all_to_all | solution.py:102
  240.8 23.5 %copy-start.4 = (bf16[1536,128]{1,0:T(8,128)(2,1)S(1)}, bf16[1536,128]{1,0:T(8,128)(2,1)}, u32[]{:S(2)}) copy-start(bf16[1536,128]{1,0:T(8,128)(2,1)} %copy-done.3) | copy-start | bytes 1179652
  246.5 2.9 %collective-permute-start = (f32[128,8]{1,0:T(8,128)}, f32[128,8]{1,0:T(8,128)S(1)}, u32[]{:S(2)}, u32[]{:S(2)}) collective-permute-start(f32[128,8]{1,0:T(8,128)} %fusion.18), channel_id=1, source_target_pairs={{0,1},{1,0},{2,3},{3,2},{4,5},{5,4},{6,7},{7,6},{8,9},{9,8},{10,11... | collective-permute-start | bytes 12296 | tf_op jit(solution)/shard_map/ppermute | solution.py:119
  250.3 11.5 %collective-permute-start.1 = (f32[128,8]{1,0:T(8,128)S(1)}, f32[128,8]{1,0:T(8,128)S(1)}, u32[]{:S(2)}, u32[]{:S(2)}) collective-permute-start(f32[128,8]{1,0:T(8,128)S(1)} %add.63), channel_id=1, source_target_pairs={{0,2},{1,3},{2,0},{3,1},{4,6},{5,7},{6,4},{7,5},{8,10},{9,11},{10,... | collective-permute-start | bytes 12296 | tf_op jit(solution)/shard_map/ppermute | solution.py:119
  261.8 5.9 %collective-permute-start.2 = (f32[128,8]{1,0:T(8,128)S(1)}, f32[128,8]{1,0:T(8,128)S(1)}, u32[]{:S(2)}, u32[]{:S(2)}) collective-permute-start(f32[128,8]{1,0:T(8,128)S(1)} %add.64), channel_id=1, source_target_pairs={{0,4},{1,5},{2,6},{3,7},{4,0},{5,1},{6,2},{7,3},{8,12},{9,13},{10,... | collective-permute-start | bytes 12296 | tf_op jit(solution)/shard_map/ppermute | solution.py:119
Sparse Core Ops, SparseCore 0:
  45.4 40.3 all-gather.2
  88.2 43.4 all-gather.4
  134.3 45.1 reduce-scatter.2
  181.9 45.0 reduce-scatter.4

commit v7 on v6

--- a/solution.py
+++ b/solution.py
@@ -54,7 +54,14 @@
         ),
     )
     expert_in = lax.all_gather(expert_in_part, "et", axis=0)
-    expert_cot = lax.all_gather(expert_cot_part, "et", axis=0)
+    me = lax.axis_index("et")
+    pieces = [expert_cot_part] + [
+        lax.ppermute(expert_cot_part, "et", [(i, (i + s) % shards) for i in range(shards)])
+        for s in range(1, shards)
+    ]
+    expert_cot = jnp.take(
+        jnp.stack(pieces), (me - jnp.arange(shards)) % shards, axis=0
+    )
     gate_w = gate_proj.reshape(local_experts, shards, width, units)
     up_w = up_proj.reshape(local_experts, shards, width, units)
     down_w = down_proj.reshape(local_experts, units, shards, width)

time: 275 us -> 338 us (1.23)
  waiting for transfers between devices: 113 us -> 138 us
  starting transfers between devices: 23.1 us -> 43.9 us
  local copies, waits for them, and re-layouts: 16.7 us -> 31.2 us
  blocking collectives: 60.5 us -> 66.7 us
    ppermute x0 -> x7, waiting for transfers between devices: none -> 49.7 us  [layer(): lax.ppermute(expert_cot_part, 'et', [(i, (i + s) % shards) for i in range...]
    all_gather x1 -> x0, waiting for transfers between devices: 33.9 us -> none  [layer(): expert_cot = lax.all_gather(expert_cot_part, 'et', axis=0)]
    all_gather x1, waiting for transfers between devices: 10.9 us -> 40.4 us  [layer(): expert_in = lax.all_gather(expert_in_part, 'et', axis=0)]
    reduce_scatter x1, waiting for transfers between devices: 21.5 us -> 0.02 us  [layer(): out_sum = lax.psum_scatter(out_part, 'et', scatter_dimension=2, tiled=True)]
    ppermute x0 -> x7, starting transfers between devices: none -> 21.1 us  [layer(): lax.ppermute(expert_cot_part, 'et', [(i, (i + s) % shards) for i in range...]
    unnamed x38 -> x49, local copies, waits for them, and re-layouts: 4.61 us -> 12.4 us
    gather x0 -> x1, local copies, waits for them, and re-layouts: none -> 6.49 us  [layer(): jnp.take(jnp.stack(pieces), (me - jnp.arange(shards)) % shards, axis=0)]
    all_to_all x1, blocking collectives: 26.7 us -> 32.8 us  [layer(): lax.all_to_all(scaled.reshape(experts, capacity, width), 'dp', split_axis...]
  transfers between devices with their start and end apart: 9 -> 15, of which waited for: 6 -> 7; matrix products, arithmetic and copies ran while one was open for 22% -> 17% of each run, Pallas kernels for 0% -> 0%
where the time goes in v7:
time: 338 us
  waiting for transfers between devices  138 us (41%)
  blocking collectives  66.7 us (20%)
  starting transfers between devices  43.9 us (13%)
  matrix products  43.7 us (13%)
  local copies, waits for them, and re-layouts  31.2 us (9%)
  between operations  14.2 us (4%)
    ppermute x7, waiting for transfers between devices, layer(): lax.ppermute(expert_cot_part, 'et', [(i, (i + s) % shards) for i in range...  49.7 us
    all_gather x1, waiting for transfers between devices, layer(): expert_in = lax.all_gather(expert_in_part, 'et', axis=0)  40.4 us
    reduce_scatter x1, waiting for transfers between devices, layer(): in_sum = lax.psum_scatter(in_part, 'et', scatter_dimension=2, tiled=True)  34.1 us
    all_to_all x1, blocking collectives, layer(): lax.all_to_all(picked.reshape(experts, capacity, width), 'dp', split_axis...  33.9 us
    all_to_all x1, blocking collectives, layer(): lax.all_to_all(scaled.reshape(experts, capacity, width), 'dp', split_axis...  32.8 us
    ppermute x7, starting transfers between devices, layer(): lax.ppermute(expert_cot_part, 'et', [(i, (i + s) % shards) for i in range...  21.1 us
    unnamed x49, local copies, waits for them, and re-layouts  12.4 us
    all_to_all x1, waiting for transfers between devices, layer(): lax.all_to_all(in_sum, 'dp', split_axis=1, concat_axis=0, tiled=True)  12.1 us
  transfers between devices with their start and end apart: 15, of which 7 were waited for; matrix products, arithmetic and copies ran while one was open for 17% of the time, Pallas kernels for 0%

profile of v7, /device:TPU:2, one launch (start us, length us, event | category | flops | bytes accessed | tf_op | source)
XLA Modules:
  0.0 337.7 jit_solution(7636562379150159759)
XLA Ops:
  7.3 0.9 copy.65
  8.1 0.1 reshape.157
  8.2 0.6 fusion.17
  8.8 1.3 fusion.13
  10.1 0.3 convolution_convert_fusion.2
  10.5 33.9 %all_to_all.63 = bf16[64,24,256]{2,1,0:T(8,128)(2,1)S(1)} all-to-all(bf16[64,24,256]{2,1,0:T(8,128)(2,1)S(1)} %bitcast.117), channel_id=1, replica_groups=mesh['dp'=32,'et'=8] {'dp'}, dimensions={0} | all-to-all | bytes 1572864 | tf_op jit(solution)/shard_map/all_to_all | solution.py:49
  44.3 0.9 copy.67
  45.4 40.4 %all-gather.2.cloned.1.call-done = bf16[8,2,768,256]{3,2,0,1:T(8,128)(2,1)} async-done(((bf16[1,2,768,256]{3,2,0,1:T(8,128)(2,1)}), bf16[8,2,768,256]{3,2,0,1:T(8,128)(2,1)}) %all-gather.2.cloned.1.call-update) | async-done | bytes 6291472 | tf_op jit(solution)/shard_map/all_gather | solution.py:56
  85.8 4.7 %convolution_bitcast_fusion.2 = f32[2,768,128]{2,1,0:T(8,128)S(1)} fusion(bf16[8,2,768,256]{3,2,0,1:T(8,128)(2,1)} %all-gather.2.cloned.1.call-done, bf16[2,8,256,128]{3,2,1,0:T(8,128)(2,1)S(1)} %bitcast.102), kind=kOutput, calls=%fused_computation.21 | convolution fusion | flops 805306368 | bytes 8126464 | tf_op jit(solution)/shard_map/jesd,ejdf->esf/dot_general | solution.py:68
  90.5 2.7 multiply_convert_fusion.2
  93.2 0.8 copy-done.8
  94.0 4.4 %convolution_convert_fusion = bf16[2,768,2048]{2,1,0:T(8,128)(2,1)} fusion(bf16[2,768,128]{2,1,0:T(8,128)(2,1)S(1)} %get-tuple-element.15, bf16[2,128,2048]{2,1,0:T(8,128)(2,1)S(1)} %copy-done.6), kind=kOutput, calls=%fused_computation.8 | convolution fusion | flops 808452096 | bytes 7733248 | tf_op jit(solution)/shard_map/esf,efd->esd/dot_general | solution.py:73
  98.5 0.1 copy.66
  98.6 0.1 broadcast_in_dim.28
  98.7 1.3 fusion.10
  100.0 0.3 convolution_convert_fusion.1
  100.3 32.8 %all_to_all.64 = bf16[64,24,256]{2,1,0:T(8,128)(2,1)S(1)} all-to-all(bf16[64,24,256]{2,1,0:T(8,128)(2,1)S(1)} %bitcast.118), channel_id=1, replica_groups=mesh['dp'=32,'et'=8] {'dp'}, dimensions={0} | all-to-all | bytes 1572864 | tf_op jit(solution)/shard_map/all_to_all | solution.py:52
  133.2 0.6 collective-permute-start.1
  133.9 1.1 collective-permute-start.2
  135.0 2.5 collective-permute-start.6
  137.6 0.5 collective-permute-start.5
  138.0 0.9 constant_dynamic-update-slice_fusion
  139.0 20.2 %collective-permute-done = bf16[2,768,256]{2,1,0:T(8,128)(2,1)S(1)} collective-permute-done((bf16[2,768,256]{2,1,0:T(8,128)(2,1)S(1)}, bf16[2,768,256]{2,1,0:T(8,128)(2,1)S(1)}, u32[]{:S(2)}, u32[]{:S(2)}) %collective-permute-start) | collective-permute-done | bytes 786464 | tf_op jit(solution)/shard_map/ppermute | solution.py:59
  159.2 0.7 collective-permute-start.3
  159.9 0.9 bitcast_dynamic-update-slice_fusion.6
  160.8 15.6 %collective-permute-start.4 = (bf16[2,768,256]{2,1,0:T(8,128)(2,1)S(1)}, bf16[2,768,256]{2,1,0:T(8,128)(2,1)S(1)}, u32[]{:S(2)}, u32[]{:S(2)}) collective-permute-start(bf16[2,768,256]{2,1,0:T(8,128)(2,1)S(1)} %bitcast.110), channel_id=1, source_target_pairs={{0,5},{1,6},{2,7},{3,0},{4,1},{5,2},{6,3},{7,4},{8,13},{9,14},{10,... | collective-permute-start | bytes 2359304 | tf_op jit(solution)/shard_map/ppermute | solution.py:59
  176.4 0.9 bitcast_dynamic-update-slice_fusion.5
  177.4 15.6 %collective-permute-done.2 = bf16[2,768,256]{2,1,0:T(8,128)(2,1)S(1)} collective-permute-done((bf16[2,768,256]{2,1,0:T(8,128)(2,1)S(1)}, bf16[2,768,256]{2,1,0:T(8,128)(2,1)S(1)}, u32[]{:S(2)}, u32[]{:S(2)}) %collective-permute-start.2) | collective-permute-done | bytes 786464 | tf_op jit(solution)/shard_map/ppermute | solution.py:59
  192.9 0.9 bitcast_dynamic-update-slice_fusion.4
  193.9 0.9 bitcast_dynamic-update-slice_fusion.3
  194.8 14.0 %collective-permute-done.4 = bf16[2,768,256]{2,1,0:T(8,128)(2,1)S(1)} collective-permute-done((bf16[2,768,256]{2,1,0:T(8,128)(2,1)S(1)}, bf16[2,768,256]{2,1,0:T(8,128)(2,1)S(1)}, u32[]{:S(2)}, u32[]{:S(2)}) %collective-permute-start.4) | collective-permute-done | bytes 786464 | tf_op jit(solution)/shard_map/ppermute | solution.py:59
  208.8 1.0 bitcast_dynamic-update-slice_fusion.2
  209.8 0.9 bitcast_dynamic-update-slice_fusion.1
  210.7 1.0 bitcast_dynamic-update-slice_fusion
  211.7 6.5 %gather_fusion = bf16[8,2,768,256]{3,2,1,0:T(8,128)(2,1)} fusion(bf16[8,2,768,256]{3,2,1,0:T(8,128)(2,1)} %bitcast_dynamic-update-slice_fusion, s32[1024]{0:T(1024)S(1)} %pad_clamp_fusion), kind=kCustom, calls=%fused_computation | custom fusion | bytes 12582944 | tf_op jit(solution)/shard_map/jit(_take)/gather | solution.py:62
  218.2 5.6 %multiply_convert_fusion = (bf16[2,768,128]{2,1,0:T(8,128)(2,1)S(1)}, bf16[2,768,128]{2,1,0:T(8,128)(2,1)S(1)}) fusion(f32[2,768,128]{2,1,0:T(8,128)} %copy-done.7, f32[2,768,128]{2,1,0:T(8,128)} %get-tuple-element.13, bf16[2,16,8,8,256]{4,3,2,1,0:T(8,128)(2,1)} %bitcast.122, bf16[8,2,768,256]{3,2,1,0:T(8,128)(2,1)} %gather_fusion, ...), kind=kOutput, calls=%fused_computation.37 | convolution fusion | flops 811008000 | bytes 9699336 | tf_op jit(solution)/shard_map/jesd,efjd->esf/dot_general | solution.py:79
  223.8 3.9 %fusion.23 = f32[2,8,256,128]{3,2,1,0:T(8,128)} fusion(bf16[8,2,768,256]{3,2,0,1:T(8,128)(2,1)S(1)} %bitcast.97, bf16[2,768,128]{2,1,0:T(8,128)(2,1)S(1)} %get-tuple-element.44), kind=kOutput, calls=%fused_computation.44 | convolution fusion | flops 805306368 | bytes 8781824 | tf_op jit(solution)/shard_map/jesd,esf->ejdf/dot_general | solution.py:92
  227.7 3.9 %fusion.25 = f32[2,8,256,128]{3,2,1,0:T(8,128)} fusion(bf16[8,2,768,256]{3,2,0,1:T(8,128)(2,1)S(1)} %bitcast.97, bf16[2,768,128]{2,1,0:T(8,128)(2,1)S(1)} %get-tuple-element.45), kind=kOutput, calls=%fused_computation.46 | convolution fusion | flops 805306368 | bytes 8781824 | tf_op jit(solution)/shard_map/jesd,esf->ejdf/dot_general | solution.py:89
  231.6 1.8 fusion.45
  233.4 0.4 slice-done.3
  233.8 0.1 copy-done.9
  233.8 4.6 %fusion = f32[2,128,8,256]{1,3,2,0:T(8,128)} fusion(bf16[2,768,128]{2,1,0:T(8,128)(2,1)S(1)} %copy-done.9, bf16[8,2,768,256]{3,2,1,0:T(8,128)(2,1)S(1)} %bitcast.101, pred[8]{0:T(512)(128)(4,1)S(1)} %compare_and_fusion), kind=kOutput, calls=%fused_computation.3 | convolution fusion | flops 808452096 | bytes 8781832 | tf_op jit(solution)/shard_map/esf,jesd->efjd/dot_general | solution.py:86
  238.5 4.4 %add_convert_fusion = bf16[2,768,2048]{2,1,0:T(8,128)(2,1)} fusion(f32[2,768,2048]{2,1,0:T(8,128)S(1)} %fusion.45, bf16[2,768,128]{2,1,0:T(8,128)(2,1)S(1)} %get-tuple-element.44, bf16[2,2048,128]{2,1,0:T(8,128)(2,1)S(1)} %copy-done), kind=kOutput, calls=%fused_computation.2 | convolution fusion | flops 811597824 | bytes 20316160 | tf_op jit(solution)/shard_map/esf,edf->esd/dot_general | solution.py:98
  242.9 2.8 copy.68
  245.8 10.1 %all-to-all-start.1 = ((bf16[2,768,256]{2,0,1:T(2,128)(2,1)}), bf16[2,768,256]{2,0,1:T(2,128)(2,1)S(1)}, u32[]{:S(2)}, u32[]{:S(2)}) async-start(bf16[2,768,256]{2,0,1:T(2,128)(2,1)} %copy.68), calls=%async_computation.2 | async-start | bytes 1572864 | tf_op jit(solution)/shard_map/all_to_all | solution.py:108
  255.9 34.1 %reduce-scatter.5.cloned.1.call-done = bf16[2,768,256]{2,1,0:T(8,128)(2,1)} async-done(((bf16[2,768,2048]{2,1,0:T(8,128)(2,1)}), bf16[2,768,256]{2,1,0:T(8,128)(2,1)}) %reduce-scatter.5.cloned.1.call-update) | async-done | bytes 786448 | tf_op jit(solution)/shard_map/reduce_scatter | solution.py:107
  290.0 2.8 copy.78
  292.8 9.8 %all-to-all-start.3 = ((bf16[2,768,256]{2,0,1:T(2,128)(2,1)}), bf16[2,768,256]{2,0,1:T(2,128)(2,1)S(1)}, u32[]{:S(2)}, u32[]{:S(2)}) async-start(bf16[2,768,256]{2,0,1:T(2,128)(2,1)} %copy.78), calls=%async_computation.5 | async-start | bytes 1572864 | tf_op jit(solution)/shard_map/all_to_all | solution.py:109
  302.7 0.1 copy.81
  302.8 0.1 mul.76
  303.0 0.1 copy.69
  303.1 3.9 %gather_fusion.1 = bf16[1024,256]{1,0:T(8,128)(2,1)S(1)} fusion(bf16[1536,256]{1,0:T(8,128)(2,1)S(1)} %bitcast.98, s32[1024]{0:T(1024)S(1)} %broadcast_clamp_fusion), kind=kCustom, calls=%fused_computation.1 | custom fusion | bytes 1052672 | tf_op jit(solution)/shard_map/gather | solution.py:118
  307.0 0.2 fusion.20
  307.2 0.1 collective-permute-start.7
  307.3 2.9 copy.83
  310.2 0.1 collective-permute-start.8
  310.3 2.0 convolution_convert_fusion.4
  312.3 12.1 %all-to-all-done.3 = bf16[2,768,256]{2,0,1:T(2,128)(2,1)S(1)} async-done(((bf16[2,768,256]{2,0,1:T(2,128)(2,1)}), bf16[2,768,256]{2,0,1:T(2,128)(2,1)S(1)}, u32[]{:S(2)}, u32[]{:S(2)}) %all-to-all-start.3) | async-done | bytes 786464 | tf_op jit(solution)/shard_map/all_to_all | solution.py:109
  324.4 0.1 copy.79
  324.5 0.1 copy.80
  324.6 2.5 collective-permute-start.9
  327.1 2.0 convolution_convert_fusion.3
  329.1 1.4 collective-permute-done.9
  330.5 0.7 copy.82
  (67 shorter events, 0.5 us)
Async XLA Ops:
  7.2 83.3 %copy-start = (bf16[2,2048,128]{2,1,0:T(8,128)(2,1)S(1)}, bf16[2,2048,128]{2,1,0:T(8,128)(2,1)}, u32[]{:S(2)}) copy-start(bf16[2,2048,128]{2,1,0:T(8,128)(2,1)} %param.12) | copy-start | bytes 3145732
  7.2 2.9 copy-start.12
  7.2 78.6 %all-gather.2.cloned.1.call-start = ((), (), s32[]{:S(2)}) async-start(), calls=%async_computation.6 | async-start | bytes 7077888 | tf_op jit(solution)/shard_map/all_gather | solution.py:56
  8.2 77.6 %copy-start.2 = (bf16[2,2048,128]{2,1,0:T(8,128)(2,1)S(1)}, bf16[2,2048,128]{2,1,0:T(8,128)(2,1)}, u32[]{:S(2)}) copy-start(bf16[2,2048,128]{2,1,0:T(8,128)(2,1)} %param.11) | copy-start | bytes 3145732
  10.1 35.2 %copy-start.4 = (bf16[1536,128]{1,0:T(8,128)(2,1)}, bf16[1536,128]{1,0:T(8,128)(2,1)S(1)}, u32[]{:S(2)}) copy-start(bf16[1536,128]{1,0:T(8,128)(2,1)S(1)} %fusion.13) | copy-start | bytes 1179652
  45.3 197.6 %reduce-scatter.3.cloned.1.call-start = ((), (), s32[]{:S(2)}) async-start(), calls=%async_computation.7 | async-start | bytes 7077888 | tf_op jit(solution)/shard_map/reduce_scatter | solution.py:101
  85.8 4.8 %copy-start.1 = (bf16[8,2,768,256]{3,2,0,1:T(8,128)(2,1)S(1)}, bf16[8,2,768,256]{3,2,0,1:T(8,128)(2,1)}, u32[]{:S(2)}) copy-start(bf16[8,2,768,256]{3,2,0,1:T(8,128)(2,1)} %all-gather.2.cloned.1.call-done) | copy-start | bytes 18874372
  90.5 2.7 copy-start.7
  90.5 3.5 %copy-start.6 = (bf16[2,128,2048]{2,1,0:T(8,128)(2,1)S(1)}, bf16[2,128,2048]{2,1,0:T(8,128)(2,1)}, u32[]{:S(2)}) copy-start(bf16[2,128,2048]{2,1,0:T(8,128)(2,1)} %param.13) | copy-start | bytes 3145732
  93.2 0.8 copy-start.8
  94.0 4.5 %copy-start.14 = (bf16[128,8]{0,1:T(8,128)(2,1)S(1)}, bf16[128,8]{0,1:T(8,128)(2,1)}, u32[]{:S(2)}) copy-start(bf16[128,8]{0,1:T(8,128)(2,1)} %param.10) | copy-start | bytes 6148
  98.4 1.6 copy-start.10
  98.4 191.6 %reduce-scatter.5.cloned.1.call-start = ((), (), s32[]{:S(2)}) async-start(), calls=%async_computation.8 | async-start | bytes 7077888 | tf_op jit(solution)/shard_map/reduce_scatter | solution.py:107
  100.0 33.2 %copy-start.5 = (bf16[1536,128]{1,0:T(8,128)(2,1)}, bf16[1536,128]{1,0:T(8,128)(2,1)S(1)}, u32[]{:S(2)}) copy-start(bf16[1536,128]{1,0:T(8,128)(2,1)S(1)} %fusion.10) | copy-start | bytes 1179652
  133.2 26.0 %collective-permute-start = (bf16[2,768,256]{2,1,0:T(8,128)(2,1)S(1)}, bf16[2,768,256]{2,1,0:T(8,128)(2,1)S(1)}, u32[]{:S(2)}, u32[]{:S(2)}) collective-permute-start(bf16[2,768,256]{2,1,0:T(8,128)(2,1)S(1)} %bitcast.103), channel_id=1, source_target_pairs={{0,1},{1,2},{2,3},{3,4},{4,5},{5,6},{6,7},{7,0},{8,9},{9,10},{10,1... | collective-permute-start | bytes 2359304 | tf_op jit(solution)/shard_map/ppermute | solution.py:59
  133.2 27.6 %collective-permute-start.1 = (bf16[2,768,256]{2,1,0:T(8,128)(2,1)S(1)}, bf16[2,768,256]{2,1,0:T(8,128)(2,1)S(1)}, u32[]{:S(2)}, u32[]{:S(2)}) collective-permute-start(bf16[2,768,256]{2,1,0:T(8,128)(2,1)S(1)} %bitcast.104), channel_id=1, source_target_pairs={{0,2},{1,3},{2,4},{3,5},{4,6},{5,7},{6,0},{7,1},{8,10},{9,11},{10,... | collective-permute-start | bytes 2359304 | tf_op jit(solution)/shard_map/ppermute | solution.py:59
  133.9 59.1 %collective-permute-start.2 = (bf16[2,768,256]{2,1,0:T(8,128)(2,1)S(1)}, bf16[2,768,256]{2,1,0:T(8,128)(2,1)S(1)}, u32[]{:S(2)}, u32[]{:S(2)}) collective-permute-start(bf16[2,768,256]{2,1,0:T(8,128)(2,1)S(1)} %bitcast.105), channel_id=1, source_target_pairs={{0,3},{1,4},{2,5},{3,6},{4,7},{5,0},{6,1},{7,2},{8,11},{9,12},{10,... | collective-permute-start | bytes 2359304 | tf_op jit(solution)/shard_map/ppermute | solution.py:59
  135.0 75.7 %collective-permute-start.6 = (bf16[2,768,256]{2,1,0:T(8,128)(2,1)S(1)}, bf16[2,768,256]{2,1,0:T(8,128)(2,1)S(1)}, u32[]{:S(2)}, u32[]{:S(2)}) collective-permute-start(bf16[2,768,256]{2,1,0:T(8,128)(2,1)S(1)} %bitcast.106), channel_id=1, source_target_pairs={{0,7},{1,0},{2,1},{3,2},{4,3},{5,4},{6,5},{7,6},{8,15},{9,8},{10,9... | collective-permute-start | bytes 2359304 | tf_op jit(solution)/shard_map/ppermute | solution.py:59
  137.6 72.2 %collective-permute-start.5 = (bf16[2,768,256]{2,1,0:T(8,128)(2,1)S(1)}, bf16[2,768,256]{2,1,0:T(8,128)(2,1)S(1)}, u32[]{:S(2)}, u32[]{:S(2)}) collective-permute-start(bf16[2,768,256]{2,1,0:T(8,128)(2,1)S(1)} %bitcast.107), channel_id=1, source_target_pairs={{0,6},{1,7},{2,0},{3,1},{4,2},{5,3},{6,4},{7,5},{8,14},{9,15},{10,... | collective-permute-start | bytes 2359304 | tf_op jit(solution)/shard_map/ppermute | solution.py:59
  159.2 34.7 %collective-permute-start.3 = (bf16[2,768,256]{2,1,0:T(8,128)(2,1)S(1)}, bf16[2,768,256]{2,1,0:T(8,128)(2,1)S(1)}, u32[]{:S(2)}, u32[]{:S(2)}) collective-permute-start(bf16[2,768,256]{2,1,0:T(8,128)(2,1)S(1)} %bitcast.109), channel_id=1, source_target_pairs={{0,4},{1,5},{2,6},{3,7},{4,0},{5,1},{6,2},{7,3},{8,12},{9,13},{10,... | collective-permute-start | bytes 2359304 | tf_op jit(solution)/shard_map/ppermute | solution.py:59
  160.8 48.0 %collective-permute-start.4 = (bf16[2,768,256]{2,1,0:T(8,128)(2,1)S(1)}, bf16[2,768,256]{2,1,0:T(8,128)(2,1)S(1)}, u32[]{:S(2)}, u32[]{:S(2)}) collective-permute-start(bf16[2,768,256]{2,1,0:T(8,128)(2,1)S(1)} %bitcast.110), channel_id=1, source_target_pairs={{0,5},{1,6},{2,7},{3,0},{4,1},{5,2},{6,3},{7,4},{8,13},{9,14},{10,... | collective-permute-start | bytes 2359304 | tf_op jit(solution)/shard_map/ppermute | solution.py:59
  211.7 12.1 %slice-start = ((s8[6291456]{0:T(1024)(128)(4,1)}), s8[2097152]{0:T(1024)(128)(4,1)S(1)}, s32[]{:S(2)}) async-start(s8[6291456]{0:T(1024)(128)(4,1)} %bitcast.96), calls=%async_computation.9 | async-start | bytes 4194304
  218.2 5.6 %slice-start.1 = ((s8[6291456]{0:T(1024)(128)(4,1)}), s8[4194304]{0:T(1024)(128)(4,1)S(1)}, s32[]{:S(2)}) async-start(s8[6291456]{0:T(1024)(128)(4,1)} %bitcast.96), calls=%async_computation.10 | async-start | bytes 8388608
  227.7 3.9 %copy-start.3 = (bf16[2,2048,128]{2,1,0:T(8,128)(2,1)S(1)}, bf16[2,2048,128]{2,1,0:T(8,128)(2,1)}, u32[]{:S(2)}) copy-start(bf16[2,2048,128]{2,1,0:T(8,128)(2,1)} %param.11) | copy-start | bytes 3145732
  227.7 5.7 %slice-start.2 = ((s8[6291456]{0:T(1024)(128)(4,1)}), s8[2097152]{0:T(1024)(128)(4,1)S(1)}, s32[]{:S(2)}) async-start(s8[6291456]{0:T(1024)(128)(4,1)} %bitcast.100), calls=%async_computation.11 | async-start | bytes 4194304
  231.6 2.2 slice-start.3
  231.6 2.3 copy-start.9
  242.9 59.8 %copy-start.11 = (bf16[128,256]{1,0:T(8,128)(2,1)S(1)}, bf16[128,256]{1,0:T(8,128)(2,1)}, u32[]{:S(2)}) copy-start(bf16[128,256]{1,0:T(8,128)(2,1)} %param.8) | copy-start | bytes 196612
  242.9 59.8 %copy-start.13 = (s32[128,8]{0,1:T(8,128)S(1)}, s32[128,8]{0,1:T(8,128)}, u32[]{:S(2)}) copy-start(s32[128,8]{0,1:T(8,128)} %param.9) | copy-start | bytes 12292
  245.8 47.1 %all-to-all-start.1 = ((bf16[2,768,256]{2,0,1:T(2,128)(2,1)}), bf16[2,768,256]{2,0,1:T(2,128)(2,1)S(1)}, u32[]{:S(2)}, u32[]{:S(2)}) async-start(bf16[2,768,256]{2,0,1:T(2,128)(2,1)} %copy.68), calls=%async_computation.2 | async-start | bytes 1572864 | tf_op jit(solution)/shard_map/all_to_all | solution.py:108
  292.8 31.6 %all-to-all-start.3 = ((bf16[2,768,256]{2,0,1:T(2,128)(2,1)}), bf16[2,768,256]{2,0,1:T(2,128)(2,1)S(1)}, u32[]{:S(2)}, u32[]{:S(2)}) async-start(bf16[2,768,256]{2,0,1:T(2,128)(2,1)} %copy.78), calls=%async_computation.5 | async-start | bytes 1572864 | tf_op jit(solution)/shard_map/all_to_all | solution.py:109
  307.2 3.0 collective-permute-start.7
  310.2 14.3 %collective-permute-start.8 = (f32[128,8]{1,0:T(8,128)S(1)}, f32[128,8]{1,0:T(8,128)S(1)}, u32[]{:S(2)}, u32[]{:S(2)}) collective-permute-start(f32[128,8]{1,0:T(8,128)S(1)} %add.99), channel_id=1, source_target_pairs={{0,2},{1,3},{2,0},{3,1},{4,6},{5,7},{6,4},{7,5},{8,10},{9,11},{10,... | collective-permute-start | bytes 12296 | tf_op jit(solution)/shard_map/ppermute | solution.py:126
  324.6 5.9 %collective-permute-start.9 = (f32[128,8]{1,0:T(8,128)S(1)}, f32[128,8]{1,0:T(8,128)S(1)}, u32[]{:S(2)}, u32[]{:S(2)}) collective-permute-start(f32[128,8]{1,0:T(8,128)S(1)} %add.100), channel_id=1, source_target_pairs={{0,4},{1,5},{2,6},{3,7},{4,0},{5,1},{6,2},{7,3},{8,12},{9,13},{10,... | collective-permute-start | bytes 12296 | tf_op jit(solution)/shard_map/ppermute | solution.py:126
Sparse Core Ops, SparseCore 0:
  45.4 40.3 all-gather.1
  98.5 56.0 reduce-scatter.2
  243.0 46.9 reduce-scatter.4

commit v8 on v6

--- a/solution.py
+++ b/solution.py
@@ -97,9 +97,10 @@
     in_part, grad_gate_w, grad_up_w, grad_down = lax.optimization_barrier(
         (in_part.astype(jnp.bfloat16), grad_gate_w, grad_up_w, grad_down)
     )
-    in_sum = lax.psum_scatter(in_part, "et", scatter_dimension=2, tiled=True)
+    in_part = in_part.reshape(local_experts, groups, capacity, features).transpose(1, 0, 2, 3)
+    in_sum = lax.psum_scatter(in_part, "et", scatter_dimension=3, tiled=True)
     back_out = lax.all_to_all(out_sum, "dp", split_axis=1, concat_axis=0, tiled=True)
-    back_grad = lax.all_to_all(in_sum, "dp", split_axis=1, concat_axis=0, tiled=True)
+    back_grad = lax.all_to_all(in_sum, "dp", split_axis=0, concat_axis=0, tiled=True)
     back_out = back_out.reshape(slots, width)
     back_grad = back_grad.reshape(slots, width)
     mixed = jnp.einsum(

time: 275 us -> 268 us (0.975)
  waiting for transfers between devices: 113 us -> 108 us
    all_to_all x1, waiting for transfers between devices: 9.25 us -> 5.8 us  [layer(): lax.all_to_all(in_sum, 'dp', split_axis=0, concat_axis=0, tiled=True)]
    reshape x0 -> x1, local copies, waits for them, and re-layouts: none -> 3.23 us  [layer(): in_part.reshape(local_experts, groups, capacity, features)]
    reduce_scatter x1 -> x0, local copies, waits for them, and re-layouts: 2.83 us -> none  [layer(): in_sum = lax.psum_scatter(in_part, 'et', scatter_dimension=2, tiled=True)]
where the time goes in v8:
time: 268 us; the launch traced here: 267 us
  waiting for transfers between devices  108 us (40%)
  blocking collectives  60.5 us (23%)
  matrix products  42.6 us (16%)
  starting transfers between devices  21.5 us (8%)
  local copies, waits for them, and re-layouts  17 us (6%)
  between operations  14.1 us (5%)
  other arithmetic  3.33 us (1%)
    reduce_scatter x1, waiting for transfers between devices, layer(): in_sum = lax.psum_scatter(in_part, 'et', scatter_dimension=3, tiled=True)  34.5 us
    all_gather x1, waiting for transfers between devices, layer(): expert_cot = lax.all_gather(expert_cot_part, 'et', axis=0)  33.9 us
    all_to_all x1, blocking collectives, layer(): lax.all_to_all(picked.reshape(experts, capacity, width), 'dp', split_axis...  33.9 us
    all_to_all x1, blocking collectives, layer(): lax.all_to_all(scaled.reshape(experts, capacity, width), 'dp', split_axis...  26.7 us
    reduce_scatter x1, waiting for transfers between devices, layer(): out_sum = lax.psum_scatter(out_part, 'et', scatter_dimension=2, tiled=True)  20.3 us
    all_gather x1, waiting for transfers between devices, layer(): expert_in = lax.all_gather(expert_in_part, 'et', axis=0)  10.9 us
    all_to_all x1, starting transfers between devices, layer(): lax.all_to_all(out_sum, 'dp', split_axis=1, concat_axis=0, tiled=True)  10.1 us
    all_to_all x1, starting transfers between devices, layer(): lax.all_to_all(in_sum, 'dp', split_axis=0, concat_axis=0, tiled=True)  10 us
  transfers between devices with their start and end apart: 9, of which 6 were waited for; matrix products, arithmetic and copies ran while one was open for 22% of the time, Pallas kernels for 0%

profile of v8, /device:TPU:2, one launch (start us, length us, event | category | flops | bytes accessed | tf_op | source)
XLA Modules:
  0.0 266.9 jit_solution(15299917504939589605)
XLA Ops:
  7.2 0.0 copy-start
  7.2 0.0 copy-start.10
  7.2 0.0 all-gather.3.cloned.1.call-start
  7.3 0.9 copy.33
  8.1 0.1 reshape.105
  8.2 0.0 copy-start.12
  8.2 0.6 fusion.15
  8.8 1.3 fusion.11
  10.1 0.0 copy-start.8
  10.1 0.3 convolution_convert_fusion.2
  10.5 33.9 %all_to_all.50 = bf16[64,24,256]{2,1,0:T(8,128)(2,1)S(1)} all-to-all(bf16[64,24,256]{2,1,0:T(8,128)(2,1)S(1)} %bitcast.96), channel_id=1, replica_groups=mesh['dp'=32,'et'=8] {'dp'}, dimensions={0} | all-to-all | bytes 1572864 | tf_op jit(solution)/shard_map/all_to_all | solution.py:49
  44.4 0.9 copy.35
  45.3 0.0 all-gather.3.cloned.1.call-update
  45.3 0.0 all-gather.5.cloned.1.call-start
  45.4 0.1 copy.34
  45.5 0.1 broadcast_in_dim.18
  45.6 1.2 fusion.8
  46.9 0.3 convolution_convert_fusion.1
  47.2 26.7 %all_to_all.51 = bf16[64,24,256]{2,1,0:T(8,128)(2,1)S(1)} all-to-all(bf16[64,24,256]{2,1,0:T(8,128)(2,1)S(1)} %bitcast.97), channel_id=1, replica_groups=mesh['dp'=32,'et'=8] {'dp'}, dimensions={0} | all-to-all | bytes 1572864 | tf_op jit(solution)/shard_map/all_to_all | solution.py:52
  73.9 0.9 copy.38
  74.8 0.0 all-gather.5.cloned.1.call-update
  74.9 0.0 reduce-scatter.3.cloned.1.call-start
  74.9 10.9 %all-gather.3.cloned.1.call-done = bf16[8,2,768,256]{3,2,0,1:T(8,128)(2,1)} async-done(((bf16[1,2,768,256]{3,2,0,1:T(8,128)(2,1)}), bf16[8,2,768,256]{3,2,0,1:T(8,128)(2,1)}) %all-gather.3.cloned.1.call-update) | async-done | bytes 6291472 | tf_op jit(solution)/shard_map/all_gather | solution.py:56
  85.8 0.0 copy-done.2
  85.8 4.7 %convolution_bitcast_fusion.2 = f32[2,768,128]{2,1,0:T(8,128)S(1)} fusion(bf16[8,2,768,256]{3,2,0,1:T(8,128)(2,1)} %all-gather.3.cloned.1.call-done, bf16[2,8,256,128]{3,2,1,0:T(8,128)(2,1)S(1)} %bitcast.89), kind=kOutput, calls=%fused_computation.18 | convolution fusion | flops 805306368 | bytes 8126464 | tf_op jit(solution)/shard_map/jesd,ejdf->esf/dot_general | solution.py:61
  90.5 0.0 copy-start.7
  90.5 0.0 copy-start.6
  90.6 2.7 multiply_convert_fusion.2
  93.2 4.4 %convolution_convert_fusion = bf16[2,768,2048]{2,1,0:T(8,128)(2,1)} fusion(bf16[2,768,128]{2,1,0:T(8,128)(2,1)S(1)} %get-tuple-element.15, bf16[2,128,2048]{2,1,0:T(8,128)(2,1)S(1)} %copy-done.6), kind=kOutput, calls=%fused_computation.5 | convolution fusion | flops 808452096 | bytes 7733248 | tf_op jit(solution)/shard_map/esf,efd->esd/dot_general | solution.py:66
  97.6 0.0 reduce-scatter.3.cloned.1.call-update
  97.6 0.2 reduce-scatter.5.cloned.1.call-start
  97.9 33.9 %all-gather.5.cloned.1.call-done = bf16[8,2,768,256]{3,2,0,1:T(8,128)(2,1)} async-done(((bf16[1,2,768,256]{3,2,0,1:T(8,128)(2,1)}), bf16[8,2,768,256]{3,2,0,1:T(8,128)(2,1)}) %all-gather.5.cloned.1.call-update) | async-done | bytes 6291472 | tf_op jit(solution)/shard_map/all_gather | solution.py:57
  131.7 6.8 %fusion.20 = f32[2,128,8,256]{1,3,2,0:T(8,128)} fusion(bf16[8,2,768,256]{3,2,0,1:T(8,128)(2,1)} %all-gather.5.cloned.1.call-done, bf16[2,768,128]{2,1,0:T(8,128)(2,1)S(1)} %get-tuple-element.15), kind=kOutput, calls=%fused_computation.33 | convolution fusion | flops 805306368 | bytes 8781824 | tf_op jit(solution)/shard_map/esf,jesd->efjd/dot_general | solution.py:79
  138.5 5.5 %multiply_convert_fusion = (bf16[2,768,128]{2,1,0:T(8,128)(2,1)S(1)}, bf16[2,768,128]{2,1,0:T(8,128)(2,1)S(1)}) fusion(f32[2,768,128]{2,1,0:T(8,128)} %copy-done.7, f32[2,768,128]{2,1,0:T(8,128)} %get-tuple-element.13, bf16[8,2,768,256]{3,2,0,1:T(8,128)(2,1)} %all-gather.5.cloned.1.call-done, bf16[2,16,8,8,256]{4,3,2,1,0:T(8,128)(2,1)} %bitcast.100), kind=kOutput, calls=%fused_computation.27 | convolution fusion | flops 807862272 | bytes 9699328 | tf_op jit(solution)/shard_map/jesd,efjd->esf/dot_general | solution.py:72
  144.1 4.0 %fusion.22 = f32[2,8,256,128]{3,2,1,0:T(8,128)} fusion(bf16[8,2,768,256]{3,2,0,1:T(8,128)(2,1)S(1)} %bitcast.83, bf16[2,768,128]{2,1,0:T(8,128)(2,1)S(1)} %get-tuple-element.32), kind=kOutput, calls=%fused_computation.35 | convolution fusion | flops 805306368 | bytes 8781824 | tf_op jit(solution)/shard_map/jesd,esf->ejdf/dot_general | solution.py:85
  148.1 4.0 %fusion.24 = f32[2,8,256,128]{3,2,1,0:T(8,128)} fusion(bf16[8,2,768,256]{3,2,0,1:T(8,128)(2,1)S(1)} %bitcast.83, bf16[2,768,128]{2,1,0:T(8,128)(2,1)S(1)} %get-tuple-element.33), kind=kOutput, calls=%fused_computation.37 | convolution fusion | flops 805306368 | bytes 8781824 | tf_op jit(solution)/shard_map/jesd,esf->ejdf/dot_general | solution.py:82
  152.0 1.8 fusion.41
  153.8 2.1 add_convert_fusion
  155.9 3.2 %copy.67 = bf16[2,32,24,2048]{3,2,0,1:T(8,128)(2,1)} copy(bf16[2,32,24,2048]{3,2,1,0:T(8,128)(2,1)S(1)} %bitcast.87) | data formatting | bytes 12582912 | tf_op jit(solution)/shard_map/reshape | solution.py:100
  159.1 0.0 reduce-scatter.5.cloned.1.call-update
  159.2 20.3 %reduce-scatter.3.cloned.1.call-done = bf16[2,768,256]{2,1,0:T(8,128)(2,1)} async-done(((bf16[2,768,2048]{2,1,0:T(8,128)(2,1)}), bf16[2,768,256]{2,1,0:T(8,128)(2,1)}) %reduce-scatter.3.cloned.1.call-update) | async-done | bytes 786448 | tf_op jit(solution)/shard_map/reduce_scatter | solution.py:94
  179.5 2.8 %copy.36 = bf16[2,768,256]{2,0,1:T(2,128)(2,1)} copy(bf16[2,768,256]{2,1,0:T(8,128)(2,1)} %reduce-scatter.3.cloned.1.call-done) | data formatting | bytes 1572864 | tf_op jit(solution)/shard_map/reduce_scatter | solution.py:94
  182.3 10.1 %all-to-all-start.1 = ((bf16[2,768,256]{2,0,1:T(2,128)(2,1)}), bf16[2,768,256]{2,0,1:T(2,128)(2,1)S(1)}, u32[]{:S(2)}, u32[]{:S(2)}) async-start(bf16[2,768,256]{2,0,1:T(2,128)(2,1)} %copy.36), calls=%async_computation.2 | async-start | bytes 1572864 | tf_op jit(solution)/shard_map/all_to_all | solution.py:102
  192.4 34.5 %reduce-scatter.5.cloned.1.call-done = bf16[32,2,24,256]{3,2,1,0:T(8,128)(2,1)} async-done(((bf16[32,2,24,2048]{3,2,1,0:T(8,128)(2,1)}), bf16[32,2,24,256]{3,2,1,0:T(8,128)(2,1)}) %reduce-scatter.5.cloned.1.call-update) | async-done | bytes 786448 | tf_op jit(solution)/shard_map/reduce_scatter | solution.py:101
  227.0 0.0 all-to-all-done.1
  227.0 10.0 %all-to-all-start.3 = ((bf16[32,2,24,256]{3,2,1,0:T(8,128)(2,1)}), bf16[32,2,24,256]{3,2,1,0:T(8,128)(2,1)S(1)}, u32[]{:S(2)}, u32[]{:S(2)}) async-start(bf16[32,2,24,256]{3,2,1,0:T(8,128)(2,1)} %reduce-scatter.5.cloned.1.call-done), calls=%async_computation.5 | async-start | bytes 1572864 | tf_op jit(solution)/shard_map/all_to_all | solution.py:103
  237.0 0.7 convert_element_type.85
  237.7 0.1 copy.45
  237.8 0.1 mul.76
  237.9 0.1 copy.37
  238.0 3.9 %gather_fusion = bf16[1024,256]{1,0:T(8,128)(2,1)S(1)} fusion(bf16[1536,256]{1,0:T(8,128)(2,1)S(1)} %bitcast.84, s32[1024]{0:T(1024)S(1)} %broadcast_clamp_fusion), kind=kCustom, calls=%fused_computation | custom fusion | bytes 1052672 | tf_op jit(solution)/shard_map/gather | solution.py:112
  242.0 1.8 fusion.18
  243.7 0.0 collective-permute-start
  243.7 2.9 %copy.47 = f32[2,128,2048]{2,1,0:T(8,128)} copy(f32[2,128,2048]{1,2,0:T(8,128)} %bitcast.88) | data formatting | bytes 4194304
  246.6 0.0 collective-permute-done
  246.6 0.8 add.63
  247.4 0.1 collective-permute-start.1
  247.5 2.0 convolution_convert_fusion.4
  249.5 2.5 collective-permute-done.1
  252.1 0.9 collective-permute-start.2
  253.0 5.8 %all-to-all-done.3 = bf16[32,2,24,256]{3,2,1,0:T(8,128)(2,1)S(1)} async-done(((bf16[32,2,24,256]{3,2,1,0:T(8,128)(2,1)}), bf16[32,2,24,256]{3,2,1,0:T(8,128)(2,1)S(1)}, u32[]{:S(2)}, u32[]{:S(2)}) %all-to-all-start.3) | async-done | bytes 786464 | tf_op jit(solution)/shard_map/all_to_all | solution.py:103
  258.8 1.0 convolution_convert_fusion.3
  259.7 0.0 collective-permute-done.2
  259.7 0.7 copy.46
  (33 shorter events, 0.1 us)
Async XLA Ops:
  7.2 83.4 %copy-start = (bf16[2,2048,128]{2,1,0:T(8,128)(2,1)S(1)}, bf16[2,2048,128]{2,1,0:T(8,128)(2,1)}, u32[]{:S(2)}) copy-start(bf16[2,2048,128]{2,1,0:T(8,128)(2,1)} %param.12) | copy-start | bytes 3145732
  7.2 2.9 %copy-start.10 = (bf16[128,256]{1,0:T(8,128)(2,1)S(1)}, bf16[128,256]{1,0:T(8,128)(2,1)}, u32[]{:S(2)}) copy-start(bf16[128,256]{1,0:T(8,128)(2,1)} %param.7) | copy-start | bytes 196612
  7.2 78.6 %all-gather.3.cloned.1.call-start = ((), (), s32[]{:S(2)}) async-start(), calls=%async_computation.6 | async-start | bytes 7077888 | tf_op jit(solution)/shard_map/all_gather | solution.py:56
  8.2 37.2 %copy-start.12 = (bf16[128,8]{0,1:T(8,128)(2,1)S(1)}, bf16[128,8]{0,1:T(8,128)(2,1)}, u32[]{:S(2)}) copy-start(bf16[128,8]{0,1:T(8,128)(2,1)} %param.10) | copy-start | bytes 6148
  10.1 35.2 %copy-start.3 = (bf16[1536,128]{1,0:T(8,128)(2,1)}, bf16[1536,128]{1,0:T(8,128)(2,1)S(1)}, u32[]{:S(2)}) copy-start(bf16[1536,128]{1,0:T(8,128)(2,1)S(1)} %fusion.11) | copy-start | bytes 1179652
  10.1 36.7 %copy-start.8 = (bf16[128,256]{1,0:T(8,128)(2,1)S(1)}, bf16[128,256]{1,0:T(8,128)(2,1)}, u32[]{:S(2)}) copy-start(bf16[128,256]{1,0:T(8,128)(2,1)} %param.8) | copy-start | bytes 196612
  45.3 40.5 %copy-start.2 = (bf16[2,2048,128]{2,1,0:T(8,128)(2,1)S(1)}, bf16[2,2048,128]{2,1,0:T(8,128)(2,1)}, u32[]{:S(2)}) copy-start(bf16[2,2048,128]{2,1,0:T(8,128)(2,1)} %param.11) | copy-start | bytes 3145732
  45.3 86.4 %all-gather.5.cloned.1.call-start = ((), (), s32[]{:S(2)}) async-start(), calls=%async_computation.8 | async-start | bytes 7077888 | tf_op jit(solution)/shard_map/all_gather | solution.py:57
  46.9 28.0 %copy-start.5 = (bf16[1536,128]{1,0:T(8,128)(2,1)}, bf16[1536,128]{1,0:T(8,128)(2,1)S(1)}, u32[]{:S(2)}) copy-start(bf16[1536,128]{1,0:T(8,128)(2,1)S(1)} %fusion.8) | copy-start | bytes 1179652
  74.9 104.6 %reduce-scatter.3.cloned.1.call-start = ((), (), s32[]{:S(2)}) async-start(), calls=%async_computation.7 | async-start | bytes 7077888 | tf_op jit(solution)/shard_map/reduce_scatter | solution.py:94
  85.8 4.8 %copy-start.1 = (bf16[8,2,768,256]{3,2,0,1:T(8,128)(2,1)S(1)}, bf16[8,2,768,256]{3,2,0,1:T(8,128)(2,1)}, u32[]{:S(2)}) copy-start(bf16[8,2,768,256]{3,2,0,1:T(8,128)(2,1)} %all-gather.3.cloned.1.call-done) | copy-start | bytes 18874372
  90.5 2.7 %copy-start.7 = (f32[2,768,128]{2,1,0:T(8,128)}, f32[2,768,128]{2,1,0:T(8,128)S(1)}, u32[]{:S(2)}) copy-start(f32[2,768,128]{2,1,0:T(8,128)S(1)} %convolution_bitcast_fusion.2) | copy-start | bytes 2359300
  90.5 2.7 %copy-start.6 = (bf16[2,128,2048]{2,1,0:T(8,128)(2,1)S(1)}, bf16[2,128,2048]{2,1,0:T(8,128)(2,1)}, u32[]{:S(2)}) copy-start(bf16[2,128,2048]{2,1,0:T(8,128)(2,1)} %param.13) | copy-start | bytes 3145732
  97.6 129.3 %reduce-scatter.5.cloned.1.call-start = ((), (), s32[]{:S(2)}) async-start(), calls=%async_computation.9 | async-start | bytes 7077888 | tf_op jit(solution)/shard_map/reduce_scatter | solution.py:101
  131.7 12.3 %slice-start = ((s8[6291456]{0:T(1024)(128)(4,1)}), s8[4194304]{0:T(1024)(128)(4,1)S(1)}, s32[]{:S(2)}) async-start(s8[6291456]{0:T(1024)(128)(4,1)} %bitcast.82), calls=%async_computation.10 | async-start | bytes 8388608
  138.5 5.5 %slice-start.1 = ((s8[6291456]{0:T(1024)(128)(4,1)}), s8[2097152]{0:T(1024)(128)(4,1)S(1)}, s32[]{:S(2)}) async-start(s8[6291456]{0:T(1024)(128)(4,1)} %bitcast.82), calls=%async_computation.11 | async-start | bytes 4194304
  159.1 77.8 %copy-start.9 = (bf16[128,256]{1,0:T(8,128)(2,1)S(1)}, bf16[128,256]{1,0:T(8,128)(2,1)}, u32[]{:S(2)}) copy-start(bf16[128,256]{1,0:T(8,128)(2,1)} %param.8) | copy-start | bytes 196612
  159.1 78.5 %copy-start.11 = (s32[128,8]{0,1:T(8,128)S(1)}, s32[128,8]{0,1:T(8,128)}, u32[]{:S(2)}) copy-start(s32[128,8]{0,1:T(8,128)} %param.9) | copy-start | bytes 12292
  182.3 44.7 %all-to-all-start.1 = ((bf16[2,768,256]{2,0,1:T(2,128)(2,1)}), bf16[2,768,256]{2,0,1:T(2,128)(2,1)S(1)}, u32[]{:S(2)}, u32[]{:S(2)}) async-start(bf16[2,768,256]{2,0,1:T(2,128)(2,1)} %copy.36), calls=%async_computation.2 | async-start | bytes 1572864 | tf_op jit(solution)/shard_map/all_to_all | solution.py:102
  227.0 31.8 %all-to-all-start.3 = ((bf16[32,2,24,256]{3,2,1,0:T(8,128)(2,1)}), bf16[32,2,24,256]{3,2,1,0:T(8,128)(2,1)S(1)}, u32[]{:S(2)}, u32[]{:S(2)}) async-start(bf16[32,2,24,256]{3,2,1,0:T(8,128)(2,1)} %reduce-scatter.5.cloned.1.call-done), calls=%async_computation.5 | async-start | bytes 1572864 | tf_op jit(solution)/shard_map/all_to_all | solution.py:103
  238.0 20.8 %copy-start.4 = (bf16[1536,128]{1,0:T(8,128)(2,1)S(1)}, bf16[1536,128]{1,0:T(8,128)(2,1)}, u32[]{:S(2)}) copy-start(bf16[1536,128]{1,0:T(8,128)(2,1)} %copy-done.3) | copy-start | bytes 1179652
  243.7 2.9 %collective-permute-start = (f32[128,8]{1,0:T(8,128)}, f32[128,8]{1,0:T(8,128)S(1)}, u32[]{:S(2)}, u32[]{:S(2)}) collective-permute-start(f32[128,8]{1,0:T(8,128)} %fusion.18), channel_id=1, source_target_pairs={{0,1},{1,0},{2,3},{3,2},{4,5},{5,4},{6,7},{7,6},{8,9},{9,8},{10,11... | collective-permute-start | bytes 12296 | tf_op jit(solution)/shard_map/ppermute | solution.py:120
  247.4 4.6 %collective-permute-start.1 = (f32[128,8]{1,0:T(8,128)S(1)}, f32[128,8]{1,0:T(8,128)S(1)}, u32[]{:S(2)}, u32[]{:S(2)}) collective-permute-start(f32[128,8]{1,0:T(8,128)S(1)} %add.63), channel_id=1, source_target_pairs={{0,2},{1,3},{2,0},{3,1},{4,6},{5,7},{6,4},{7,5},{8,10},{9,11},{10,... | collective-permute-start | bytes 12296 | tf_op jit(solution)/shard_map/ppermute | solution.py:120
  252.1 7.7 %collective-permute-start.2 = (f32[128,8]{1,0:T(8,128)S(1)}, f32[128,8]{1,0:T(8,128)S(1)}, u32[]{:S(2)}, u32[]{:S(2)}) collective-permute-start(f32[128,8]{1,0:T(8,128)S(1)} %add.64), channel_id=1, source_target_pairs={{0,4},{1,5},{2,6},{3,7},{4,0},{5,1},{6,2},{7,3},{8,12},{9,13},{10,... | collective-permute-start | bytes 12296 | tf_op jit(solution)/shard_map/ppermute | solution.py:120
Sparse Core Ops, SparseCore 0:
  45.4 40.3 all-gather.2
  88.2 43.4 all-gather.4
  134.3 45.1 reduce-scatter.2
  181.9 45.0 reduce-scatter.4
